TPU v7x, 256 devices: a whole 4x4x8 slice. The times are simulated.
256 devices in a mesh: dp: 4 (over y), expert: 64 (over x, z, core).
Axes of the slice: x: 4, y: 4, z: 8, core: 2. Of those that a mesh axis runs over, the one named last changes fastest.
Arguments:
- tokens: bfloat16 [2, 512, 7168], P(None, ('dp', 'expert')), parts along dimension 1, may hold values from -6 to 6
- expert_ids: int32 [2, 512, 8], P(None, ('dp', 'expert')), parts along dimension 1, may hold values from 0 to 15, all different within a row; in each aligned block of 2 rows (0 to 1, 2 to 3, ..., all dimensions but the last counted through in order) at most 2 rows name the same one
- gate_codes: int32 [2, 512, 8], P(None, ('dp', 'expert')), parts along dimension 1, may hold values from 1 to 1024
- w_gate: bfloat16 [256, 7168, 256], P(('dp', 'expert')), parts along dimension 0, may hold values from -0.0625 to 0.0625
- w_up: bfloat16 [256, 7168, 256], P(('dp', 'expert')), parts along dimension 0, may hold values from -0.0625 to 0.0625
- w_down: bfloat16 [256, 256, 7168], P(('dp', 'expert')), parts along dimension 0, may hold values from -0.1875 to 0.1875
Outputs:
- mixed: bfloat16 [2, 512, 7168], P(None, ('dp', 'expert')), parts along dimension 1
There are 4 independent parts, one for each index of `dp`. A program takes and returns all parts, laid end to end along the dimension named above; each array names one. Nothing has to cross between parts.
Inputs may be any that keep to these rules, and one draw needn't show every extreme that they name: `expert_ids`: each row names 8 different experts. In each step, the 2 rows of one device name no expert more than 2 times, and in every draw some such block names some expert exactly 2 times.
All inputs are finite; a program needn't handle non-finite values.
Results may differ from a plain program's by a relative error of at most 0.0058.
Values may be sent and summed in bfloat16 or wider, within the bound.
No kernel may reach another device: no remote copies, remote signals or barrier semaphores. Data moves between devices by JAX's collectives and lax.ppermute only.
A program may use at most 64 MiB of HBM per device.

v0:
```python
import jax
import jax.numpy as jnp
from jax import lax
from jax.sharding import PartitionSpec as P

EH = 1024
HS = 256


def route_tables(step_ids, step_codes, experts_all, capacity):
    row_count, top_count = step_ids.shape
    flat_ids = step_ids.reshape(-1)
    onehot = (flat_ids[:, None] == jnp.arange(experts_all, dtype=jnp.int32)[None, :]).astype(
        jnp.int32
    )
    slot_rank = jnp.sum(jnp.cumsum(onehot, 0) * onehot, 1) - 1
    slot_index = flat_ids * capacity + slot_rank
    placement = slot_index[:, None] == jnp.arange(experts_all * capacity, dtype=jnp.int32)[None, :]
    codes = step_codes.astype(jnp.float32)
    gate_weight = codes / jnp.sum(codes, 1, keepdims=True)
    mix_table = jnp.sum(
        (placement.astype(jnp.float32) * gate_weight.reshape(-1)[:, None]).reshape(
            row_count, top_count, -1
        ),
        1,
    )
    return (placement, mix_table)


def body(tokens, expert_ids, gate_codes, w_gate, w_up, w_down):
    step_count, row_count, width = tokens.shape
    top_count = expert_ids.shape[2]
    peer_count = lax.axis_size("expert")
    group_size = EH // HS
    experts_all = peer_count // group_size
    capacity = min(row_count, max(2, 2 * row_count * top_count // experts_all))
    my_gate = w_gate[0]
    my_up = w_up[0]
    my_down = w_down[0]
    results = []
    send_rows = []
    mix_tables = []
    for step in range(step_count):
        placement, mix_table = route_tables(
            expert_ids[step], gate_codes[step], experts_all, capacity
        )
        repeated = jnp.repeat(tokens[step], top_count, 0)
        slots = jnp.einsum(
            "as,ad->sd",
            placement.astype(jnp.bfloat16),
            repeated,
            preferred_element_type=jnp.float32,
        ).astype(jnp.bfloat16)
        slots = slots.reshape(experts_all, capacity, width)
        send_rows.append(jnp.repeat(slots, group_size, 0))
        mix_tables.append(mix_table)
    returned = []
    for step in range(step_count):
        received = lax.all_to_all(
            send_rows[step], "expert", split_axis=0, concat_axis=0, tiled=True
        )
        gate_act = jnp.einsum(
            "...cd,dh->...ch", received, my_gate, preferred_element_type=jnp.float32
        )
        up_act = jnp.einsum("...cd,dh->...ch", received, my_up, preferred_element_type=jnp.float32)
        hidden = (jax.nn.silu(gate_act) * up_act).astype(jnp.bfloat16)
        outputs_sent = jnp.einsum(
            "...ch,hd->...cd", hidden, my_down, preferred_element_type=jnp.float32
        ).astype(jnp.bfloat16)
        returned.append(
            lax.all_to_all(outputs_sent, "expert", split_axis=0, concat_axis=0, tiled=True)
        )
    for step in range(step_count):
        grouped = (
            returned[step].reshape(experts_all, group_size, capacity, width).astype(jnp.float32)
        )
        expert_out = jnp.sum(grouped, 1).reshape(-1, width)
        combined = jnp.dot(
            mix_tables[step],
            expert_out,
            precision=lax.Precision.HIGHEST,
            preferred_element_type=jnp.float32,
        )
        results.append(combined.astype(jnp.bfloat16))
    return jnp.stack(results, 0)


def solution(mesh):
    placed = (
        P(None, ("dp", "expert"), None),
        P(None, ("dp", "expert"), None),
        P(None, ("dp", "expert"), None),
        P(("dp", "expert"), None, None),
        P(("dp", "expert"), None, None),
        P(("dp", "expert"), None, None),
    )
    return jax.shard_map(
        body, mesh=mesh, in_specs=placed, out_specs=P(None, ("dp", "expert"), None), check_vma=False
    )
```

profile of v0, /device:TPU:32, one launch (start us, length us, event | category | flops | bytes accessed | tf_op | source)
XLA Modules:
  0.0 223.5 jit_solution(17310171280247649143)
XLA Ops:
  0.0 0.7 fusion.66
  0.7 0.1 eq.70
  0.8 0.1 fusion.61
  0.9 0.2 select_reduce_fusion.3
  1.1 0.8 slice_bitcast_fusion.1
  1.9 0.4 convolution_convert_fusion.3
  2.3 0.2 reshape.117
  2.5 2.2 broadcast_in_dim.9
  4.7 11.6 %all-to-all-start = ((bf16[64,2,7168]{2,1,0:T(2,128)(2,1)}), bf16[64,2,7168]{2,1,0:T(2,128)(2,1)S(1)}, u32[]{:S(2)}, u32[]{:S(2)}) async-start(bf16[64,2,7168]{2,1,0:T(2,128)(2,1)} %bitcast.4), calls=%async_computation | async-start | bytes 3670016 | tf_op jit(solution)/shard_map/all_to_all | solution.py:59
  16.3 0.1 eq.80
  16.4 0.1 fusion.60
  16.5 0.2 select_reduce_fusion.1
  16.7 0.4 convolution_convert_fusion.2
  17.1 0.2 reshape.121
  17.3 43.5 %all-to-all-done = bf16[64,2,7168]{2,1,0:T(2,128)(2,1)S(1)} async-done(((bf16[64,2,7168]{2,1,0:T(2,128)(2,1)}), bf16[64,2,7168]{2,1,0:T(2,128)(2,1)S(1)}, u32[]{:S(2)}, u32[]{:S(2)}) %all-to-all-start) | async-done | bytes 1835040 | tf_op jit(solution)/shard_map/all_to_all | solution.py:59
  60.7 2.2 broadcast_in_dim.11
  62.9 7.1 %all-to-all-start.2 = ((bf16[64,2,7168]{2,1,0:T(2,128)(2,1)}), bf16[64,2,7168]{2,1,0:T(2,128)(2,1)}, u32[]{:S(2)}, u32[]{:S(2)}) async-start(bf16[64,2,7168]{2,1,0:T(2,128)(2,1)} %bitcast.17), calls=%async_computation.2 | async-start | bytes 3670016 | tf_op jit(solution)/shard_map/all_to_all | solution.py:59
  70.0 2.7 %fusion.10 = f32[64,2,256]{2,0,1:T(8,128)S(1)} fusion(bf16[1,7168,256]{2,1,0:T(8,128)(2,1)} %param.9, bf16[64,2,7168]{2,1,0:T(2,128)(2,1)S(1)} %all-to-all-done), kind=kOutput, calls=%fused_computation.18 | convolution fusion | flops 469762048 | bytes 5636096 | tf_op jit(solution)/shard_map/...cd,dh->...ch/dot_general | solution.py:62
  72.7 6.6 %convolution_convert_fusion.1 = bf16[64,2,7168]{2,0,1:T(8,128)(2,1)} fusion(bf16[1,256,7168]{2,1,0:T(8,128)(2,1)} %param.11, bf16[1,7168,256]{2,1,0:T(8,128)(2,1)} %param.10, bf16[64,2,7168]{2,1,0:T(2,128)(2,1)S(1)} %all-to-all-done, f32[64,2,256]{2,0,1:T(8,128)S(1)} %fusion.10), kind=kOutput, calls=%fused_computation.1 | convolution fusion | flops 940638208 | bytes 11141120 | tf_op jit(solution)/shard_map/...ch,hd->...cd/dot_general | solution.py:67
  79.3 4.6 %copy.27 = bf16[64,2,7168]{2,1,0:T(2,128)(2,1)} copy(bf16[64,2,7168]{2,0,1:T(8,128)(2,1)} %convolution_convert_fusion.1) | data formatting | bytes 3670016 | tf_op jit(solution)/shard_map/convert_element_type | solution.py:69
  84.0 30.5 %all-to-all-done.2 = bf16[64,2,7168]{2,1,0:T(2,128)(2,1)} async-done(((bf16[64,2,7168]{2,1,0:T(2,128)(2,1)}), bf16[64,2,7168]{2,1,0:T(2,128)(2,1)}, u32[]{:S(2)}, u32[]{:S(2)}) %all-to-all-start.2) | async-done | bytes 1835040 | tf_op jit(solution)/shard_map/all_to_all | solution.py:59
  114.4 6.9 %all-to-all-start.1 = ((bf16[64,2,7168]{2,1,0:T(2,128)(2,1)}), bf16[64,2,7168]{2,1,0:T(2,128)(2,1)S(1)}, u32[]{:S(2)}, u32[]{:S(2)}) async-start(bf16[64,2,7168]{2,1,0:T(2,128)(2,1)} %copy.27), calls=%async_computation.1 | async-start | bytes 3670016 | tf_op jit(solution)/shard_map/all_to_all | solution.py:71
  121.4 3.2 %fusion.8 = f32[64,2,256]{2,0,1:T(8,128)S(1)} fusion(bf16[1,7168,256]{2,1,0:T(8,128)(2,1)} %param.9, bf16[64,2,7168]{2,1,0:T(2,128)(2,1)} %all-to-all-done.2), kind=kOutput, calls=%fused_computation.16 | convolution fusion | flops 469762048 | bytes 5636096 | tf_op jit(solution)/shard_map/...cd,dh->...ch/dot_general | solution.py:62
  124.6 7.1 %convolution_convert_fusion = bf16[64,2,7168]{2,0,1:T(8,128)(2,1)} fusion(bf16[1,256,7168]{2,1,0:T(8,128)(2,1)} %param.11, bf16[1,7168,256]{2,1,0:T(8,128)(2,1)} %param.10, bf16[64,2,7168]{2,1,0:T(2,128)(2,1)} %all-to-all-done.2, f32[64,2,256]{2,0,1:T(8,128)S(1)} %fusion.8), kind=kOutput, calls=%fused_computation | convolution fusion | flops 940638208 | bytes 11141120 | tf_op jit(solution)/shard_map/...ch,hd->...cd/dot_general | solution.py:67
  131.7 4.6 %copy.32 = bf16[64,2,7168]{2,1,0:T(2,128)(2,1)} copy(bf16[64,2,7168]{2,0,1:T(8,128)(2,1)} %convolution_convert_fusion) | data formatting | bytes 3670016 | tf_op jit(solution)/shard_map/convert_element_type | solution.py:69
  136.3 0.0 copy-start.1
  136.3 0.0 copy-start
  136.3 29.5 %all-to-all-done.1 = bf16[64,2,7168]{2,1,0:T(2,128)(2,1)S(1)} async-done(((bf16[64,2,7168]{2,1,0:T(2,128)(2,1)}), bf16[64,2,7168]{2,1,0:T(2,128)(2,1)S(1)}, u32[]{:S(2)}, u32[]{:S(2)}) %all-to-all-start.1) | async-done | bytes 1835040 | tf_op jit(solution)/shard_map/all_to_all | solution.py:71
  165.8 7.1 %all-to-all-start.3 = ((bf16[64,2,7168]{2,1,0:T(2,128)(2,1)}), bf16[64,2,7168]{2,1,0:T(2,128)(2,1)}, u32[]{:S(2)}, u32[]{:S(2)}) async-start(bf16[64,2,7168]{2,1,0:T(2,128)(2,1)} %copy.32), calls=%async_computation.3 | async-start | bytes 3670016 | tf_op jit(solution)/shard_map/all_to_all | solution.py:71
  172.9 0.1 sub.13
  173.0 0.1 sub.11
  173.1 0.0 copy-done.1
  173.1 0.1 convert_reduce_fusion.3
  173.2 0.1 bitcast_divide_fusion.1
  173.3 0.0 copy-done
  173.3 0.1 select_reduce_fusion
  173.4 1.7 convert_reduce_fusion.1
  175.2 0.6 reshape.119
  175.8 41.5 %all-to-all-done.3 = bf16[64,2,7168]{2,1,0:T(2,128)(2,1)} async-done(((bf16[64,2,7168]{2,1,0:T(2,128)(2,1)}), bf16[64,2,7168]{2,1,0:T(2,128)(2,1)}, u32[]{:S(2)}, u32[]{:S(2)}) %all-to-all-start.3) | async-done | bytes 1835040 | tf_op jit(solution)/shard_map/all_to_all | solution.py:71
  217.3 3.7 %convert_reduce_fusion = f32[16,2,7168]{2,1,0:T(2,128)S(1)} fusion(bf16[64,2,7168]{2,1,0:T(2,128)(2,1)} %all-to-all-done.3), kind=kLoop, calls=%fused_computation.8 | loop fusion | flops 1605632 | bytes 2752512 | tf_op jit(solution)/shard_map/reduce_sum | solution.py:77
  221.0 0.6 reshape.123
  221.7 0.5 fusion
  222.2 0.5 fusion.1
  222.8 0.7 pad_maximum_fusion
  (5 shorter events, 0.1 us)
Async XLA Ops:
  4.7 56.1 %all-to-all-start = ((bf16[64,2,7168]{2,1,0:T(2,128)(2,1)}), bf16[64,2,7168]{2,1,0:T(2,128)(2,1)S(1)}, u32[]{:S(2)}, u32[]{:S(2)}) async-start(bf16[64,2,7168]{2,1,0:T(2,128)(2,1)} %bitcast.4), calls=%async_computation | async-start | bytes 3670016 | tf_op jit(solution)/shard_map/all_to_all | solution.py:59
  62.9 51.5 %all-to-all-start.2 = ((bf16[64,2,7168]{2,1,0:T(2,128)(2,1)}), bf16[64,2,7168]{2,1,0:T(2,128)(2,1)}, u32[]{:S(2)}, u32[]{:S(2)}) async-start(bf16[64,2,7168]{2,1,0:T(2,128)(2,1)} %bitcast.17), calls=%async_computation.2 | async-start | bytes 3670016 | tf_op jit(solution)/shard_map/all_to_all | solution.py:59
  114.4 51.4 %all-to-all-start.1 = ((bf16[64,2,7168]{2,1,0:T(2,128)(2,1)}), bf16[64,2,7168]{2,1,0:T(2,128)(2,1)S(1)}, u32[]{:S(2)}, u32[]{:S(2)}) async-start(bf16[64,2,7168]{2,1,0:T(2,128)(2,1)} %copy.27), calls=%async_computation.1 | async-start | bytes 3670016 | tf_op jit(solution)/shard_map/all_to_all | solution.py:71
  136.3 36.8 %copy-start.1 = (s32[2,2,8]{2,1,0:T(2,128)S(1)}, s32[2,2,8]{2,1,0:T(2,128)}, u32[]{:S(2)}) copy-start(s32[2,2,8]{2,1,0:T(2,128)} %param.8) | copy-start | bytes 388
  136.3 37.0 %copy-start = (s32[2,2,8]{2,1,0:T(2,128)S(1)}, s32[2,2,8]{2,1,0:T(2,128)}, u32[]{:S(2)}) copy-start(s32[2,2,8]{2,1,0:T(2,128)} %param.7) | copy-start | bytes 388
  165.8 51.5 %all-to-all-start.3 = ((bf16[64,2,7168]{2,1,0:T(2,128)(2,1)}), bf16[64,2,7168]{2,1,0:T(2,128)(2,1)}, u32[]{:S(2)}, u32[]{:S(2)}) async-start(bf16[64,2,7168]{2,1,0:T(2,128)(2,1)} %copy.32), calls=%async_computation.3 | async-start | bytes 3670016 | tf_op jit(solution)/shard_map/all_to_all | solution.py:71
where the time goes:
time: 226 us; the launch traced here: 223 us
  waiting for transfers between devices  145 us (64%)
  starting transfers between devices  32.8 us (15%)
  matrix products  21.5 us (10%)
  local copies, waits for them, and re-layouts  17.1 us (8%)
  other arithmetic  7.09 us (3%)
    all_to_all x2, waiting for transfers between devices, body(): lax.all_to_all(send_rows[step], 'expert', split_axis=0, concat_axis=0, ti...  73.9 us
    all_to_all x2, waiting for transfers between devices, body(): lax.all_to_all(outputs_sent, 'expert', split_axis=0, concat_axis=0, tiled...  71 us
    all_to_all x2, starting transfers between devices, body(): lax.all_to_all(send_rows[step], 'expert', split_axis=0, concat_axis=0, ti...  18.7 us
    all_to_all x2, starting transfers between devices, body(): lax.all_to_all(outputs_sent, 'expert', split_axis=0, concat_axis=0, tiled...  14.1 us
    dot_general x2, matrix products, body(): jnp.einsum('...ch,hd->...cd', hidden, my_down, preferred_element_type=jnp...  13.7 us
    convert_element_type x2, local copies, waits for them, and re-layouts, body(): outputs_sent = jnp.einsum('...ch,hd->...cd', hidden, my_down, preferred_e...  9.25 us
    dot_general x2, matrix products, body(): jnp.einsum('...cd,dh->...ch', received, my_gate, preferred_element_type=j...  5.95 us
    reduce_sum x2, other arithmetic, body(): expert_out = jnp.sum(grouped, 1).reshape(-1, width)  5.46 us
  transfers between devices with their start and end apart: 4, of which 4 were waited for; matrix products, arithmetic and copies ran while one was open for 15% of the time, Pallas kernels for 0%

commit v1 on v0

v1 whole, which is shorter than its diff:
```python
import jax
import jax.numpy as jnp
import numpy as np
from jax import lax
from jax.sharding import Mesh
from jax.sharding import PartitionSpec as P

EH = 1024
HS = 256


def body(tokens, expert_ids, gate_codes, w_gate, w_up, w_down):
    step_count, row_count, width = tokens.shape
    group_size = EH // HS
    peer_count = lax.axis_size(("x", "z", "c"))
    experts_all = peer_count // group_size
    my_expert = lax.axis_index(("x", "z", "c")) // group_size

    codes = gate_codes.astype(jnp.float32)
    gate_weight = codes / jnp.sum(codes, -1, keepdims=True)
    onehot = expert_ids[..., None] == jnp.arange(experts_all, dtype=jnp.int32)
    table = jnp.sum(jnp.where(onehot, gate_weight[..., None], 0.0), -2)

    all_tokens = lax.all_gather(jnp.swapaxes(tokens, 0, 1), ("x", "z", "c"), axis=0, tiled=True)
    all_table = lax.all_gather(jnp.swapaxes(table, 0, 1), ("x", "z", "c"), axis=0, tiled=True)
    mine = jnp.arange(experts_all, dtype=jnp.int32) == my_expert
    scale = jnp.sum(jnp.where(mine, all_table, 0.0), -1)

    rows = all_tokens.reshape(-1, width)
    gate_act = jnp.dot(rows, w_gate[0], preferred_element_type=jnp.float32)
    up_act = jnp.dot(rows, w_up[0], preferred_element_type=jnp.float32)
    hidden = (jax.nn.silu(gate_act) * up_act).astype(jnp.bfloat16)
    partial_out = jnp.dot(hidden, w_down[0], preferred_element_type=jnp.float32).astype(
        jnp.bfloat16
    )
    contrib = partial_out.astype(jnp.float32) * scale.reshape(-1, 1)
    contrib = contrib.reshape(lax.axis_size(("x", "z")), lax.axis_size("c"), -1, width)
    contrib = jnp.swapaxes(contrib, 0, 1).reshape(-1, width)
    mixed = lax.psum_scatter(contrib, "c", scatter_dimension=0, tiled=True)
    mixed = lax.psum_scatter(mixed, ("x", "z"), scatter_dimension=0, tiled=True)
    mixed = lax.optimization_barrier(mixed)
    return jnp.swapaxes(mixed.reshape(-1, step_count, width), 0, 1).astype(jnp.bfloat16)


def solution(mesh):
    devices = np.asarray(mesh.devices)
    dp, expert = devices.shape
    chip_mesh = Mesh(devices.reshape(dp, 4, expert // 8, 2), ("dp", "x", "z", "c"))
    rows_spec = P(None, ("dp", "x", "z", "c"), None)
    blocks_spec = P(("dp", "x", "z", "c"), None, None)
    placed = (rows_spec, rows_spec, rows_spec, blocks_spec, blocks_spec, blocks_spec)
    return jax.shard_map(
        body, mesh=chip_mesh, in_specs=placed, out_specs=rows_spec, check_vma=False
    )
```

time: 226 us -> 343 us (1.52)
  blocking collectives: 0 us -> 225 us
  waiting for transfers between devices: 145 us -> 46.3 us
  starting transfers between devices: 32.8 us -> 0.04 us
  local copies, waits for them, and re-layouts: 17.1 us -> 36.4 us
  between operations: 0.15 us -> 14.1 us
  matrix products: 21.5 us -> 15.4 us
  other arithmetic: 7.09 us -> 1.83 us
    unnamed x0 -> x1, blocking collectives: none -> 173 us
    all_to_all x4 -> x0, waiting for transfers between devices: 145 us -> none  [the longest x2 73.9 us: body(): lax.all_to_all(send_rows[step], 'expert', split_axis=0, concat_axis=0, ti...]
    all_gather x0 -> x1, blocking collectives: none -> 52 us  [body(): lax.all_gather(jnp.swapaxes(table, 0, 1), ('x', 'z', 'c'), axis=0, tiled=...]
    all_to_all x4 -> x0, starting transfers between devices: 32.8 us -> none  [the longest x2 18.7 us: body(): lax.all_to_all(send_rows[step], 'expert', split_axis=0, concat_axis=0, ti...]
    reshape x4, local copies, waits for them, and re-layouts: 1.61 us -> 32.8 us  [the longest x2 15.4 us: body(): contrib.reshape(lax.axis_size(('x', 'z')), lax.axis_size('c'), -1, width)]
    all_gather x0 -> x1, waiting for transfers between devices: none -> 28.3 us  [body(): lax.all_gather(jnp.swapaxes(tokens, 0, 1), ('x', 'z', 'c'), axis=0, tiled...]
    reduce_scatter x0 -> x1, waiting for transfers between devices: none -> 17.9 us  [body(): mixed = lax.psum_scatter(contrib, 'c', scatter_dimension=0, tiled=True)]
    convert_element_type x2, local copies, waits for them, and re-layouts: 9.25 us -> 0.69 us  [body(): jnp.swapaxes(mixed.reshape(-1, step_count, width), 0, 1)]
  transfers between devices with their start and end apart: 4 -> 2, of which waited for: 4 -> 2; matrix products, arithmetic and copies ran while one was open for 15% -> 1% of each run, Pallas kernels for 0% -> 0%
where the time goes in v1:
time: 343 us; the launch traced here: 339 us
  blocking collectives  225 us (66%)
  waiting for transfers between devices  46.3 us (13%)
  local copies, waits for them, and re-layouts  36.4 us (11%)
  matrix products  15.4 us (4%)
  between operations  14.1 us (4%)
    unnamed x1, blocking collectives  173 us
    all_gather x1, blocking collectives, body(): lax.all_gather(jnp.swapaxes(table, 0, 1), ('x', 'z', 'c'), axis=0, tiled=...  52 us
    all_gather x1, waiting for transfers between devices, body(): lax.all_gather(jnp.swapaxes(tokens, 0, 1), ('x', 'z', 'c'), axis=0, tiled...  28.3 us
    reduce_scatter x1, waiting for transfers between devices, body(): mixed = lax.psum_scatter(contrib, 'c', scatter_dimension=0, tiled=True)  17.9 us
    reshape x2, local copies, waits for them, and re-layouts, body(): contrib.reshape(lax.axis_size(('x', 'z')), lax.axis_size('c'), -1, width)  15.4 us
    dot_general x1, matrix products, body(): jnp.dot(hidden, w_down[0], preferred_element_type=jnp.float32)  11.2 us
    reshape x1, local copies, waits for them, and re-layouts, body(): contrib = jnp.swapaxes(contrib, 0, 1).reshape(-1, width)  8.98 us
    reshape x1, local copies, waits for them, and re-layouts, body(): rows = all_tokens.reshape(-1, width)  8.39 us
  transfers between devices with their start and end apart: 2, of which 2 were waited for; matrix products, arithmetic and copies ran while one was open for 1% of the time, Pallas kernels for 0%

profile of v1, /device:TPU:32, one launch (start us, length us, event | category | flops | bytes accessed | tf_op | source)
XLA Modules:
  0.0 338.7 jit_solution(16789418684903518490)
XLA Ops:
  6.5 0.0 all-gather.2.cloned.1.call-start
  6.5 1.5 copy.20
  8.0 0.0 all-gather.2.cloned.1.call-update
  8.0 0.0 reduce-scatter.2.cloned.1.call-start
  8.1 0.8 convert_divide_fusion
  9.0 0.8 select_reduce_fusion.1
  9.8 52.0 %all_gather.7 = f32[128,2,16]{2,1,0:T(2,128)S(1)} all-gather(f32[2,2,16]{2,1,0:T(2,128)S(1)} %copy.14), channel_id=1, replica_groups=mesh['dp'=4,'x'=4,'z'=8,'c'=2] {'x','z','c'}, dimensions={0}, use_global_device_ids=true | all-gather | bytes 16640 | tf_op jit(solution)/shard_map/all_gather | solution.py:25
  61.8 0.2 select_reduce_fusion
  62.0 0.1 mul.27
  62.2 28.3 %all-gather.2.cloned.1.call-done = bf16[128,2,7168]{2,1,0:T(2,128)(2,1)} async-done(((bf16[2,2,7168]{2,1,0:T(2,128)(2,1)}), bf16[128,2,7168]{2,1,0:T(2,128)(2,1)}) %all-gather.2.cloned.1.call-update) | async-done | bytes 3670032 | tf_op jit(solution)/shard_map/all_gather | solution.py:24
  90.5 8.4 %reshape.16 = bf16[256,7168]{1,0:T(8,128)(2,1)} reshape(bf16[128,2,7168]{2,1,0:T(2,128)(2,1)} %all-gather.2.cloned.1.call-done) | data formatting | bytes 7340032 | tf_op jit(solution)/shard_map/reshape | solution.py:29
  98.9 4.3 %fusion.5 = f32[256,256]{1,0:T(8,128)S(1)} fusion(bf16[256,7168]{1,0:T(8,128)(2,1)} %reshape.16, bf16[1,7168,256]{2,1,0:T(8,128)(2,1)} %param.9), kind=kOutput, calls=%fused_computation.7 | convolution fusion | flops 939524096 | bytes 7602176 | tf_op jit(solution)/shard_map/dot_general | solution.py:30
  103.1 11.2 %fusion.1 = f32[256,7168]{1,0:T(8,128)} fusion(bf16[1,256,7168]{2,1,0:T(8,128)(2,1)} %param.11, f32[256]{0:T(256)S(1)} %mul.27, bf16[256,7168]{1,0:T(8,128)(2,1)} %reshape.16, bf16[1,7168,256]{2,1,0:T(8,128)(2,1)} %param.10, f32[256,256]{1,0:T(8,128)S(1)} %fusion.5), kind=kOutput, calls=%fused_computation.2 | convolution fusion | flops 1884946432 | bytes 18613248 | tf_op jit(solution)/shard_map/dot_general | solution.py:33
  114.3 8.8 %reshape.17 = f32[32,2,4,7168]{3,2,1,0:T(4,128)} reshape(f32[256,7168]{1,0:T(8,128)} %fusion.1) | data formatting | bytes 14680064 | tf_op jit(solution)/shard_map/reshape | solution.py:37
  123.1 6.6 %copy.19 = f32[32,2,4,7168]{3,2,0,1:T(4,128)} copy(f32[32,2,4,7168]{3,2,1,0:T(4,128)} %reshape.17) | data formatting | bytes 14680064 | tf_op jit(solution)/shard_map/reshape | solution.py:37
  129.7 9.0 %reshape.18 = f32[256,7168]{1,0:T(8,128)} reshape(f32[2,32,4,7168]{3,2,1,0:T(4,128)} %bitcast.26) | data formatting | bytes 14680064 | tf_op jit(solution)/shard_map/reshape | solution.py:38
  138.7 0.0 copy-start
  138.7 0.0 reduce-scatter.2.cloned.1.call-update
  138.7 0.6 copy-done
  139.4 0.6 dynamic-slice
  140.6 17.9 %reduce-scatter.2.cloned.1.call-done = f32[128,7168]{1,0:T(8,128)} async-done(((f32[256,7168]{1,0:T(8,128)}), f32[128,7168]{1,0:T(8,128)}) %reduce-scatter.2.cloned.1.call-update) | async-done | bytes 3670032 | tf_op jit(solution)/shard_map/reduce_scatter | solution.py:39
  158.6 172.5 %all-reduce.2 = bf16[128,7168]{1,0:T(8,128)(2,1)S(1)} all-reduce(f32[128,7168]{1,0:T(8,128)} %reduce-scatter.2.cloned.1.call-done), channel_id=3, replica_groups=mesh['dp'=4,'x'=4,'z'=8,'c'=2] {'x','z'}, use_global_device_ids=true, to_apply=%region_4.5.clone | all-reduce | flops 917504 | bytes 5505024
  331.2 0.7 copy.16
  (4 shorter events, 0.1 us)
Async XLA Ops:
  6.5 83.9 %all-gather.2.cloned.1.call-start = ((), (), s32[]{:S(2)}) async-start(), calls=%async_computation.1 | async-start | bytes 3727360 | tf_op jit(solution)/shard_map/all_gather | solution.py:24
  8.0 150.5 %reduce-scatter.2.cloned.1.call-start = ((), (), s32[]{:S(2)}) async-start(), calls=%async_computation.2 | async-start | bytes 11010048 | tf_op jit(solution)/shard_map/reduce_scatter | solution.py:39
  138.7 0.7 copy-start
Sparse Core Ops, SparseCore 0:
  10.1 80.3 all-gather.1
  138.9 19.6 reduce-scatter.1

commit v2 on v0

--- a/solution.py
+++ b/solution.py
@@ -34,10 +34,6 @@
     group_size = EH // HS
     experts_all = peer_count // group_size
     capacity = min(row_count, max(2, 2 * row_count * top_count // experts_all))
-    my_gate = w_gate[0]
-    my_up = w_up[0]
-    my_down = w_down[0]
-    results = []
     send_rows = []
     mix_tables = []
     for step in range(step_count):
@@ -51,33 +47,28 @@
             repeated,
             preferred_element_type=jnp.float32,
         ).astype(jnp.bfloat16)
-        slots = slots.reshape(experts_all, capacity, width)
-        send_rows.append(jnp.repeat(slots, group_size, 0))
+        send_rows.append(slots.reshape(experts_all, 1, capacity, width))
         mix_tables.append(mix_table)
-    returned = []
+    slots = jnp.repeat(jnp.concatenate(send_rows, 1), group_size, 0)
+    received = lax.all_to_all(slots, "expert", split_axis=0, concat_axis=0, tiled=True)
+    gate_act = jnp.einsum(
+        "...cd,dh->...ch", received, w_gate[0], preferred_element_type=jnp.float32
+    )
+    up_act = jnp.einsum("...cd,dh->...ch", received, w_up[0], preferred_element_type=jnp.float32)
+    hidden = (jax.nn.silu(gate_act) * up_act).astype(jnp.bfloat16)
+    outputs_sent = jnp.einsum(
+        "...ch,hd->...cd", hidden, w_down[0], preferred_element_type=jnp.float32
+    ).astype(jnp.bfloat16)
+    returned = lax.all_to_all(outputs_sent, "expert", split_axis=0, concat_axis=0, tiled=True)
+    grouped = returned.reshape(experts_all, group_size, step_count, capacity, width).astype(
+        jnp.float32
+    )
+    expert_out = jnp.sum(grouped, 1)
+    results = []
     for step in range(step_count):
-        received = lax.all_to_all(
-            send_rows[step], "expert", split_axis=0, concat_axis=0, tiled=True
-        )
-        gate_act = jnp.einsum(
-            "...cd,dh->...ch", received, my_gate, preferred_element_type=jnp.float32
-        )
-        up_act = jnp.einsum("...cd,dh->...ch", received, my_up, preferred_element_type=jnp.float32)
-        hidden = (jax.nn.silu(gate_act) * up_act).astype(jnp.bfloat16)
-        outputs_sent = jnp.einsum(
-            "...ch,hd->...cd", hidden, my_down, preferred_element_type=jnp.float32
-        ).astype(jnp.bfloat16)
-        returned.append(
-            lax.all_to_all(outputs_sent, "expert", split_axis=0, concat_axis=0, tiled=True)
-        )
-    for step in range(step_count):
-        grouped = (
-            returned[step].reshape(experts_all, group_size, capacity, width).astype(jnp.float32)
-        )
-        expert_out = jnp.sum(grouped, 1).reshape(-1, width)
         combined = jnp.dot(
             mix_tables[step],
-            expert_out,
+            expert_out[:, step].reshape(-1, width),
             precision=lax.Precision.HIGHEST,
             preferred_element_type=jnp.float32,
         )

time: 226 us -> 227 us (level)
  blocking collectives: 0 us -> 95.7 us
  waiting for transfers between devices: 145 us -> 82 us
  starting transfers between devices: 32.8 us -> 7.04 us
  matrix products: 21.5 us -> 13.3 us
  other arithmetic: 7.09 us -> 9.41 us
    all_to_all x0 -> x1, blocking collectives: none -> 95.7 us  [body(): lax.all_to_all(slots, 'expert', split_axis=0, concat_axis=0, tiled=True)]
    all_to_all x2 -> x0, waiting for transfers between devices: 73.9 us -> none  [body(): lax.all_to_all(send_rows[step], 'expert', split_axis=0, concat_axis=0, ti...]
    all_to_all x2 -> x0, starting transfers between devices: 18.7 us -> none  [body(): lax.all_to_all(send_rows[step], 'expert', split_axis=0, concat_axis=0, ti...]
    all_to_all x2 -> x1, waiting for transfers between devices: 71 us -> 82 us  [body(): lax.all_to_all(outputs_sent, 'expert', split_axis=0, concat_axis=0, tiled...]
    dot_general x6 -> x4, matrix products: 20.7 us -> 12.5 us  [the longest x1 10 us: body(): jnp.einsum('...ch,hd->...cd', hidden, w_down[0], preferred_element_type=j...]
    all_to_all x2 -> x1, starting transfers between devices: 14.1 us -> 7.04 us  [body(): lax.all_to_all(outputs_sent, 'expert', split_axis=0, concat_axis=0, tiled...]
    convert_element_type x2 -> x1, local copies, waits for them, and re-layouts: 9.25 us -> 7.65 us  [body(): outputs_sent = jnp.einsum('...ch,hd->...cd', hidden, w_down[0], preferred...]
    reduce_sum x2 -> x1, other arithmetic: 5.46 us -> 6.49 us  [body(): expert_out = jnp.sum(grouped, 1)]
  transfers between devices with their start and end apart: 4 -> 1, of which waited for: 4 -> 1; matrix products, arithmetic and copies ran while one was open for 15% -> 0% of each run, Pallas kernels for 0% -> 0%
where the time goes in v2:
time: 227 us; the launch traced here: 224 us
  blocking collectives  95.7 us (42%)
  waiting for transfers between devices  82 us (36%)
  local copies, waits for them, and re-layouts  15.9 us (7%)
  matrix products  13.3 us (6%)
  other arithmetic  9.41 us (4%)
  starting transfers between devices  7.04 us (3%)
    all_to_all x1, blocking collectives, body(): lax.all_to_all(slots, 'expert', split_axis=0, concat_axis=0, tiled=True)  95.7 us
    all_to_all x1, waiting for transfers between devices, body(): lax.all_to_all(outputs_sent, 'expert', split_axis=0, concat_axis=0, tiled...  82 us
    dot_general x1, matrix products, body(): jnp.einsum('...ch,hd->...cd', hidden, w_down[0], preferred_element_type=j...  10 us
    convert_element_type x1, local copies, waits for them, and re-layouts, body(): outputs_sent = jnp.einsum('...ch,hd->...cd', hidden, w_down[0], preferred...  7.65 us
    all_to_all x1, starting transfers between devices, body(): lax.all_to_all(outputs_sent, 'expert', split_axis=0, concat_axis=0, tiled...  7.04 us
    reduce_sum x1, other arithmetic, body(): expert_out = jnp.sum(grouped, 1)  6.49 us
  transfers between devices with their start and end apart: 1, of which 1 were waited for; matrix products, arithmetic and copies ran while one was open for 0% of the time, Pallas kernels for 0%

profile of v2, /device:TPU:32, one launch (start us, length us, event | category | flops | bytes accessed | tf_op | source)
XLA Modules:
  0.0 223.6 jit_solution(11457969177138336295)
XLA Ops:
  0.0 0.7 fusion.39
  0.7 0.1 eq.68
  0.8 0.1 reshape_squeeze.10
  0.9 0.1 fusion.33
  1.0 0.2 select_reduce_fusion.1
  1.2 0.1 fusion.34
  1.3 0.2 select_reduce_fusion.3
  1.5 0.8 slice_bitcast_fusion.1
  2.3 0.4 convolution_convert_fusion.2
  2.7 0.2 reshape.105
  2.9 0.4 convolution_convert_fusion.1
  3.2 0.2 reshape.107
  3.4 1.3 pad_maximum_fusion
  4.7 0.6 copy.19
  5.4 2.2 %broadcast_in_dim.8 = bf16[16,4,2,2,7168]{4,3,2,1,0:T(2,128)(2,1)S(1)} broadcast(bf16[16,2,2,7168]{3,2,1,0:T(2,128)(2,1)S(1)} %copy.19), dimensions={0,2,3,4} | broadcast | bytes 4587520 | tf_op jit(solution)/shard_map/broadcast_in_dim | solution.py:52
  7.6 0.0 copy-start.3
  7.6 95.7 %all_to_all.10 = bf16[64,2,2,7168]{3,2,1,0:T(2,128)(2,1)S(1)} all-to-all(bf16[64,2,2,7168]{3,2,1,0:T(2,128)(2,1)S(1)} %bitcast.57), channel_id=1, replica_groups=mesh['dp'=4,'expert'=64] {'expert'}, dimensions={0} | all-to-all | bytes 7340032 | tf_op jit(solution)/shard_map/all_to_all | solution.py:53
  103.4 0.0 copy-start
  103.4 1.8 copy-done
  105.2 0.0 copy-done.3
  105.2 1.4 fusion.5
  106.6 10.0 %convolution_convert_fusion = bf16[64,2,2,7168]{3,0,2,1:T(8,128)(2,1)} fusion(bf16[1,256,7168]{2,1,0:T(8,128)(2,1)} %param.11, bf16[1,7168,256]{2,1,0:T(8,128)(2,1)} %param.10, bf16[64,2,2,7168]{3,2,1,0:T(2,128)(2,1)} %copy-done, f32[64,2,2,256]{3,0,2,1:T(8,128)S(1)} %fusion.5), kind=kOutput, calls=%fused_computation | convolution fusion | flops 1881276416 | bytes 14942208 | tf_op jit(solution)/shard_map/...ch,hd->...cd/dot_general | solution.py:59
  116.6 7.6 %copy.22 = bf16[64,2,2,7168]{3,2,1,0:T(2,128)(2,1)} copy(bf16[64,2,2,7168]{3,0,2,1:T(8,128)(2,1)} %convolution_convert_fusion) | data formatting | bytes 7340032 | tf_op jit(solution)/shard_map/convert_element_type | solution.py:61
  124.3 0.0 copy-start.2
  124.3 0.0 copy-start.1
  124.3 7.0 %all-to-all-start.1 = ((bf16[64,2,2,7168]{3,2,1,0:T(2,128)(2,1)}), bf16[64,2,2,7168]{3,2,1,0:T(2,128)(2,1)}, u32[]{:S(2)}, u32[]{:S(2)}) async-start(bf16[64,2,2,7168]{3,2,1,0:T(2,128)(2,1)} %copy.22), calls=%async_computation.1 | async-start | bytes 7340032 | tf_op jit(solution)/shard_map/all_to_all | solution.py:62
  131.3 0.1 sub.13
  131.4 0.1 sub.11
  131.5 0.0 copy-done.2
  131.5 0.1 convert_reduce_fusion.2
  131.6 0.1 bitcast_divide_fusion.1
  131.7 0.0 copy-done.1
  131.7 0.1 select_reduce_fusion
  131.8 82.0 %all-to-all-done.1 = bf16[64,2,2,7168]{3,2,1,0:T(2,128)(2,1)} async-done(((bf16[64,2,2,7168]{3,2,1,0:T(2,128)(2,1)}), bf16[64,2,2,7168]{3,2,1,0:T(2,128)(2,1)}, u32[]{:S(2)}, u32[]{:S(2)}) %all-to-all-start.1) | async-done | bytes 3670048 | tf_op jit(solution)/shard_map/all_to_all | solution.py:62
  213.9 6.5 %convert_reduce_fusion = f32[16,2,2,7168]{3,2,1,0:T(2,128)S(1)} fusion(bf16[64,2,2,7168]{3,2,1,0:T(2,128)(2,1)} %all-to-all-done.1), kind=kLoop, calls=%fused_computation.7 | loop fusion | flops 3211264 | bytes 5505024 | tf_op jit(solution)/shard_map/reduce_sum | solution.py:66
  220.4 0.1 fusion.38
  220.5 0.6 reshape_squeeze.11
  221.1 0.6 reshape_squeeze.12
  221.8 0.5 fusion
  222.3 0.5 fusion.1
  222.9 0.7 pad_maximum_fusion.1
  (5 shorter events, 0.1 us)
Async XLA Ops:
  7.6 97.6 %copy-start.3 = (bf16[1,7168,256]{2,1,0:T(8,128)(2,1)S(1)}, bf16[1,7168,256]{2,1,0:T(8,128)(2,1)}, u32[]{:S(2)}) copy-start(bf16[1,7168,256]{2,1,0:T(8,128)(2,1)} %param.9) | copy-start | bytes 11010052
  103.4 1.8 copy-start
  124.3 7.2 %copy-start.2 = (s32[2,2,8]{2,1,0:T(2,128)S(1)}, s32[2,2,8]{2,1,0:T(2,128)}, u32[]{:S(2)}) copy-start(s32[2,2,8]{2,1,0:T(2,128)} %param.8) | copy-start | bytes 388
  124.3 7.4 %copy-start.1 = (s32[2,2,8]{2,1,0:T(2,128)S(1)}, s32[2,2,8]{2,1,0:T(2,128)}, u32[]{:S(2)}) copy-start(s32[2,2,8]{2,1,0:T(2,128)} %param.7) | copy-start | bytes 388
  124.3 89.6 %all-to-all-start.1 = ((bf16[64,2,2,7168]{3,2,1,0:T(2,128)(2,1)}), bf16[64,2,2,7168]{3,2,1,0:T(2,128)(2,1)}, u32[]{:S(2)}, u32[]{:S(2)}) async-start(bf16[64,2,2,7168]{3,2,1,0:T(2,128)(2,1)} %copy.22), calls=%async_computation.1 | async-start | bytes 7340032 | tf_op jit(solution)/shard_map/all_to_all | solution.py:62

commit v3 on v2

v3 whole, which is shorter than its diff:
```python
import jax
import jax.numpy as jnp
import numpy as np
from jax import lax
from jax.sharding import Mesh
from jax.sharding import PartitionSpec as P

EH = 1024
HS = 256
CROSS = ("x", "zh")


def route_tables(step_ids, step_codes, experts_all, capacity):
    row_count, top_count = step_ids.shape
    flat_ids = step_ids.reshape(-1)
    onehot = (flat_ids[:, None] == jnp.arange(experts_all, dtype=jnp.int32)[None, :]).astype(
        jnp.int32
    )
    slot_rank = jnp.sum(jnp.cumsum(onehot, 0) * onehot, 1) - 1
    slot_index = flat_ids * capacity + slot_rank
    placement = slot_index[:, None] == jnp.arange(experts_all * capacity, dtype=jnp.int32)[None, :]
    codes = step_codes.astype(jnp.float32)
    gate_weight = codes / jnp.sum(codes, 1, keepdims=True)
    mix_table = jnp.sum(
        (placement.astype(jnp.float32) * gate_weight.reshape(-1)[:, None]).reshape(
            row_count, top_count, -1
        ),
        1,
    )
    return (placement, mix_table)


def swap(value, axis):
    return lax.ppermute(value, axis, [(0, 1), (1, 0)])


def body(tokens, expert_ids, gate_codes, w_gate, w_up, w_down):
    step_count, row_count, width = tokens.shape
    top_count = expert_ids.shape[2]
    experts_all = lax.axis_size(CROSS)
    capacity = min(row_count, max(2, 2 * row_count * top_count // experts_all))
    send_rows = []
    mix_tables = []
    for step in range(step_count):
        placement, mix_table = route_tables(
            expert_ids[step], gate_codes[step], experts_all, capacity
        )
        repeated = jnp.repeat(tokens[step], top_count, 0)
        slots = jnp.einsum(
            "as,ad->sd",
            placement.astype(jnp.bfloat16),
            repeated,
            preferred_element_type=jnp.float32,
        ).astype(jnp.bfloat16)
        send_rows.append(slots.reshape(experts_all, 1, capacity, width))
        mix_tables.append(mix_table)
    slots = jnp.concatenate(send_rows, 1)
    received = lax.all_to_all(slots, CROSS, split_axis=0, concat_axis=0, tiled=True)
    received = jnp.stack([received, swap(received, "zl")], 0)
    received = jnp.stack([received, swap(received, "c")], 0)
    gate_act = jnp.einsum(
        "...cd,dh->...ch", received, w_gate[0], preferred_element_type=jnp.float32
    )
    up_act = jnp.einsum("...cd,dh->...ch", received, w_up[0], preferred_element_type=jnp.float32)
    hidden = (jax.nn.silu(gate_act) * up_act).astype(jnp.bfloat16)
    partial_out = jnp.einsum(
        "...ch,hd->...cd", hidden, w_down[0], preferred_element_type=jnp.float32
    ).astype(jnp.bfloat16)
    chip_sum = partial_out[0].astype(jnp.float32) + swap(partial_out[1], "c").astype(jnp.float32)
    chip_sum = chip_sum.astype(jnp.bfloat16)
    expert_out = chip_sum[0].astype(jnp.float32) + swap(chip_sum[1], "zl").astype(jnp.float32)
    returned = lax.all_to_all(
        expert_out.astype(jnp.bfloat16), CROSS, split_axis=0, concat_axis=0, tiled=True
    ).astype(jnp.float32)
    results = []
    for step in range(step_count):
        combined = jnp.dot(
            mix_tables[step],
            returned[:, step].reshape(-1, width),
            precision=lax.Precision.HIGHEST,
            preferred_element_type=jnp.float32,
        )
        results.append(combined.astype(jnp.bfloat16))
    return jnp.stack(results, 0)


def solution(mesh):
    devices = np.asarray(mesh.devices)
    dp, expert = devices.shape
    chip_mesh = Mesh(
        devices.reshape(dp, 4, expert // 16, 2, 2), ("dp", "x", "zh", "zl", "c")
    )
    rows_spec = P(None, ("dp", "x", "zh", "zl", "c"), None)
    blocks_spec = P(("dp", "x", "zh", "zl", "c"), None, None)
    placed = (rows_spec, rows_spec, rows_spec, blocks_spec, blocks_spec, blocks_spec)
    return jax.shard_map(
        body, mesh=chip_mesh, in_specs=placed, out_specs=rows_spec, check_vma=False
    )
```

time: 227 us -> 135 us (0.59); the launches traced: 224 us -> 135 us
  blocking collectives: 95.7 us -> 36.4 us
  local copies, waits for them, and re-layouts: 15.9 us -> 7.35 us
  matrix products: 13.3 us -> 4.78 us
  waiting for transfers between devices: 82 us -> 74.1 us
  other arithmetic: 9.41 us -> 3.69 us
    all_to_all x1, blocking collectives: 95.7 us -> 36.4 us  [body(): lax.all_to_all(slots, CROSS, split_axis=0, concat_axis=0, tiled=True)]
    all_to_all x1, waiting for transfers between devices: 82 us -> 26.3 us  [body(): lax.all_to_all(expert_out.astype(jnp.bfloat16), CROSS, split_axis=0, conc...]
    ppermute x0 -> x4, waiting for transfers between devices: none -> 47.9 us  [swap(): return lax.ppermute(value, axis, [(0, 1), (1, 0)])]
    dot_general x1, matrix products: 10 us -> 1.15 us  [body(): jnp.einsum('...ch,hd->...cd', hidden, w_down[0], preferred_element_type=j...]
    reduce_sum x1 -> x0, other arithmetic: 6.49 us -> none  [body(): expert_out = jnp.sum(grouped, 1)]
    convert_element_type x1, local copies, waits for them, and re-layouts: 7.65 us -> 1.87 us  [body(): expert_out.astype(jnp.bfloat16)]
    ppermute x0 -> x4, starting transfers between devices: none -> 3.11 us  [swap(): return lax.ppermute(value, axis, [(0, 1), (1, 0)])]
  transfers between devices with their start and end apart: 1 -> 5, of which waited for: 1 -> 5; matrix products, arithmetic and copies ran while one was open for 0% -> 0% of each run, Pallas kernels for 0% -> 0%
where the time goes in v3:
time: 135 us
  waiting for transfers between devices  74.1 us (55%)
  blocking collectives  36.4 us (27%)
  starting transfers between devices  8 us (6%)
  local copies, waits for them, and re-layouts  7.35 us (5%)
  matrix products  4.78 us (4%)
  other arithmetic  3.69 us (3%)
    ppermute x4, waiting for transfers between devices, swap(): return lax.ppermute(value, axis, [(0, 1), (1, 0)])  47.9 us
    all_to_all x1, blocking collectives, body(): lax.all_to_all(slots, CROSS, split_axis=0, concat_axis=0, tiled=True)  36.4 us
    all_to_all x1, waiting for transfers between devices, body(): lax.all_to_all(expert_out.astype(jnp.bfloat16), CROSS, split_axis=0, conc...  26.3 us
    all_to_all x1, starting transfers between devices, body(): lax.all_to_all(expert_out.astype(jnp.bfloat16), CROSS, split_axis=0, conc...  4.89 us
    ppermute x4, starting transfers between devices, swap(): return lax.ppermute(value, axis, [(0, 1), (1, 0)])  3.11 us
  transfers between devices with their start and end apart: 5, of which 5 were waited for; matrix products, arithmetic and copies ran while one was open for 0% of the time, Pallas kernels for 0%

profile of v3, /device:TPU:32, one launch (start us, length us, event | category | flops | bytes accessed | tf_op | source)
XLA Modules:
  0.0 134.6 jit_solution(542727391648591621)
XLA Ops:
  0.0 0.7 fusion.23
  0.7 0.1 reshape_squeeze.10
  0.8 0.1 fusion.14
  0.9 0.2 select_reduce_fusion.1
  1.1 0.8 slice_bitcast_fusion.5
  1.9 0.4 convolution_convert_fusion.1
  2.3 0.2 reshape.105
  2.5 0.1 eq.68
  2.6 0.1 fusion.15
  2.7 0.2 select_reduce_fusion.3
  2.9 0.4 convolution_convert_fusion.2
  3.3 0.2 reshape.103
  3.4 1.2 pad_maximum_fusion.4
  4.6 36.4 %all_to_all.10 = bf16[16,2,2,7168]{3,2,1,0:T(2,128)(2,1)S(1)} all-to-all(bf16[16,2,2,7168]{3,2,1,0:T(2,128)(2,1)S(1)} %pad_maximum_fusion.4), channel_id=1, replica_groups=mesh['dp'=4,'x'=4,'zh'=4,'zl'=2,'c'=2] {'x','zh'}, dimensions={0} | all-to-all | bytes 1835008 | tf_op jit(solution)/shard_map/all_to_all | solution.py:58
  41.1 0.0 copy-start.2
  41.1 0.3 copy.28
  41.4 2.1 %collective-permute-start = (bf16[16,2,2,7168]{3,0,2,1:T(8,128)(2,1)S(1)}, bf16[16,2,2,7168]{3,0,2,1:T(8,128)(2,1)S(1)}, u32[]{:S(2)}, u32[]{:S(2)}) collective-permute-start(bf16[16,2,2,7168]{3,0,2,1:T(8,128)(2,1)S(1)} %copy.28), channel_id=1, source_target_pairs={{0,2},{2,0},{1,3},{3,1},{4,6},{6,4},{5,7},{7,5},{8,10},{10,8},{9,1... | collective-permute-start | bytes 2752520 | tf_op jit(solution)/shard_map/ppermute | solution.py:34
  43.5 18.6 %collective-permute-done = bf16[16,2,2,7168]{3,0,2,1:T(8,128)(2,1)S(1)} collective-permute-done((bf16[16,2,2,7168]{3,0,2,1:T(8,128)(2,1)S(1)}, bf16[16,2,2,7168]{3,0,2,1:T(8,128)(2,1)S(1)}, u32[]{:S(2)}, u32[]{:S(2)}) %collective-permute-start) | collective-permute-done | bytes 917536 | tf_op jit(solution)/shard_map/ppermute | solution.py:34
  62.1 0.2 fusion.21
  62.4 0.1 collective-permute-start.1
  62.5 3.8 %collective-permute-done.1 = bf16[2,16,2,2,7168]{4,1,3,2,0:T(8,128)(2,1)S(1)} collective-permute-done((bf16[2,16,2,2,7168]{4,1,3,2,0:T(8,128)(2,1)S(1)}, bf16[2,16,2,2,7168]{4,1,3,2,0:T(8,128)(2,1)S(1)}, u32[]{:S(2)}, u32[]{:S(2)}) %collective-permute-start.1) | collective-permute-done | bytes 1835040 | tf_op jit(solution)/shard_map/ppermute | solution.py:34
  66.2 0.0 copy-done.2
  66.2 0.0 copy-start.3
  66.2 1.1 fusion.6
  67.4 0.9 copy-done.3
  68.3 0.0 copy-start.4
  68.3 1.1 fusion.4
  69.4 0.9 copy-done.4
  70.3 1.1 convolution_convert_fusion
  71.5 0.2 slice_bitcast_fusion
  71.6 0.2 collective-permute-start.2
  71.9 3.6 %collective-permute-done.2 = bf16[2,16,2,2,7168]{4,1,3,2,0:T(8,128)(2,1)S(1)} collective-permute-done((bf16[2,16,2,2,7168]{4,1,3,2,0:T(8,128)(2,1)S(1)}, bf16[2,16,2,2,7168]{4,1,3,2,0:T(8,128)(2,1)S(1)}, u32[]{:S(2)}, u32[]{:S(2)}) %collective-permute-start.2) | collective-permute-done | bytes 1835040 | tf_op jit(solution)/shard_map/ppermute | solution.py:34
  75.5 0.4 fusion.2
  75.9 0.1 slice_bitcast_fusion.2
  76.0 0.0 copy-start.1
  76.0 0.0 copy-start
  76.0 0.7 collective-permute-start.3
  76.7 21.8 %collective-permute-done.3 = bf16[16,2,2,7168]{3,0,2,1:T(8,128)(2,1)S(1)} collective-permute-done((bf16[16,2,2,7168]{3,0,2,1:T(8,128)(2,1)S(1)}, bf16[16,2,2,7168]{3,0,2,1:T(8,128)(2,1)S(1)}, u32[]{:S(2)}, u32[]{:S(2)}) %collective-permute-start.3) | collective-permute-done | bytes 917536 | tf_op jit(solution)/shard_map/ppermute | solution.py:34
  98.5 0.2 fusion.8
  98.7 1.9 %copy.22 = bf16[16,2,2,7168]{3,2,1,0:T(2,128)(2,1)} copy(bf16[16,2,2,7168]{3,0,2,1:T(8,128)(2,1)S(1)} %fusion.8) | data formatting | bytes 1835008 | tf_op jit(solution)/shard_map/convert_element_type | solution.py:73
  100.6 4.9 %all-to-all-start.1 = ((bf16[16,2,2,7168]{3,2,1,0:T(2,128)(2,1)}), bf16[16,2,2,7168]{3,2,1,0:T(2,128)(2,1)S(1)}, u32[]{:S(2)}, u32[]{:S(2)}) async-start(bf16[16,2,2,7168]{3,2,1,0:T(2,128)(2,1)} %copy.22), calls=%async_computation.1 | async-start | bytes 1835008 | tf_op jit(solution)/shard_map/all_to_all | solution.py:72
  105.5 0.1 sub.13
  105.6 0.1 sub.11
  105.7 0.0 copy-done.1
  105.7 0.1 convert_reduce_fusion.1
  105.8 0.1 bitcast_divide_fusion.1
  105.9 0.0 copy-done
  105.9 0.1 select_reduce_fusion
  106.0 26.3 %all-to-all-done.1 = bf16[16,2,2,7168]{3,2,1,0:T(2,128)(2,1)S(1)} async-done(((bf16[16,2,2,7168]{3,2,1,0:T(2,128)(2,1)}), bf16[16,2,2,7168]{3,2,1,0:T(2,128)(2,1)S(1)}, u32[]{:S(2)}, u32[]{:S(2)}) %all-to-all-start.1) | async-done | bytes 917536 | tf_op jit(solution)/shard_map/all_to_all | solution.py:72
  132.2 0.6 fusion.22
  132.9 0.2 reshape_squeeze.11
  133.1 0.2 reshape_squeeze.12
  133.2 0.3 fusion
  133.6 0.3 fusion.1
  133.9 0.7 pad_maximum_fusion.5
  (5 shorter events, 0.1 us)
Async XLA Ops:
  41.1 25.1 %copy-start.2 = (bf16[1,7168,256]{2,1,0:T(8,128)(2,1)S(1)}, bf16[1,7168,256]{2,1,0:T(8,128)(2,1)}, u32[]{:S(2)}) copy-start(bf16[1,7168,256]{2,1,0:T(8,128)(2,1)} %param.9) | copy-start | bytes 11010052
  41.4 20.7 %collective-permute-start = (bf16[16,2,2,7168]{3,0,2,1:T(8,128)(2,1)S(1)}, bf16[16,2,2,7168]{3,0,2,1:T(8,128)(2,1)S(1)}, u32[]{:S(2)}, u32[]{:S(2)}) collective-permute-start(bf16[16,2,2,7168]{3,0,2,1:T(8,128)(2,1)S(1)} %copy.28), channel_id=1, source_target_pairs={{0,2},{2,0},{1,3},{3,1},{4,6},{6,4},{5,7},{7,5},{8,10},{10,8},{9,1... | collective-permute-start | bytes 2752520 | tf_op jit(solution)/shard_map/ppermute | solution.py:34
  62.4 3.9 %collective-permute-start.1 = (bf16[2,16,2,2,7168]{4,1,3,2,0:T(8,128)(2,1)S(1)}, bf16[2,16,2,2,7168]{4,1,3,2,0:T(8,128)(2,1)S(1)}, u32[]{:S(2)}, u32[]{:S(2)}) collective-permute-start(bf16[2,16,2,2,7168]{4,1,3,2,0:T(8,128)(2,1)S(1)} %get-tuple-element.8), channel_id=1, source_target_pairs={{0,1},{1,0},{2,3},{3,2},{4,5},{5,4},{6,7},{7,6},{8,9},{9,8},{10,11... | collective-permute-start | bytes 5505032 | tf_op jit(solution)/shard_map/ppermute | solution.py:34
  66.2 2.0 %copy-start.3 = (bf16[1,7168,256]{2,1,0:T(8,128)(2,1)S(1)}, bf16[1,7168,256]{2,1,0:T(8,128)(2,1)}, u32[]{:S(2)}) copy-start(bf16[1,7168,256]{2,1,0:T(8,128)(2,1)} %param.10) | copy-start | bytes 11010052
  68.3 2.0 %copy-start.4 = (bf16[1,256,7168]{2,1,0:T(8,128)(2,1)S(1)}, bf16[1,256,7168]{2,1,0:T(8,128)(2,1)}, u32[]{:S(2)}) copy-start(bf16[1,256,7168]{2,1,0:T(8,128)(2,1)} %param.11) | copy-start | bytes 11010052
  71.6 3.9 %collective-permute-start.2 = (bf16[2,16,2,2,7168]{4,1,3,2,0:T(8,128)(2,1)S(1)}, bf16[2,16,2,2,7168]{4,1,3,2,0:T(8,128)(2,1)S(1)}, u32[]{:S(2)}, u32[]{:S(2)}) collective-permute-start(bf16[2,16,2,2,7168]{4,1,3,2,0:T(8,128)(2,1)S(1)} %slice_bitcast_fusion), channel_id=1, source_target_pairs={{0,1},{1,0},{2,3},{3,2},{4,5},{5,4},{6,7},{7,6},{8,9},{9,8},{10,11... | collective-permute-start | bytes 5505032 | tf_op jit(solution)/shard_map/ppermute | solution.py:34
  76.0 29.7 %copy-start.1 = (s32[2,2,8]{2,1,0:T(2,128)S(1)}, s32[2,2,8]{2,1,0:T(2,128)}, u32[]{:S(2)}) copy-start(s32[2,2,8]{2,1,0:T(2,128)} %param.8) | copy-start | bytes 388
  76.0 29.9 %copy-start = (s32[2,2,8]{2,1,0:T(2,128)S(1)}, s32[2,2,8]{2,1,0:T(2,128)}, u32[]{:S(2)}) copy-start(s32[2,2,8]{2,1,0:T(2,128)} %param.7) | copy-start | bytes 388
  76.0 22.5 %collective-permute-start.3 = (bf16[16,2,2,7168]{3,0,2,1:T(8,128)(2,1)S(1)}, bf16[16,2,2,7168]{3,0,2,1:T(8,128)(2,1)S(1)}, u32[]{:S(2)}, u32[]{:S(2)}) collective-permute-start(bf16[16,2,2,7168]{3,0,2,1:T(8,128)(2,1)S(1)} %slice_bitcast_fusion.2), channel_id=1, source_target_pairs={{0,2},{2,0},{1,3},{3,1},{4,6},{6,4},{5,7},{7,5},{8,10},{10,8},{9,1... | collective-permute-start | bytes 2752520 | tf_op jit(solution)/shard_map/ppermute | solution.py:34
  100.6 31.6 %all-to-all-start.1 = ((bf16[16,2,2,7168]{3,2,1,0:T(2,128)(2,1)}), bf16[16,2,2,7168]{3,2,1,0:T(2,128)(2,1)S(1)}, u32[]{:S(2)}, u32[]{:S(2)}) async-start(bf16[16,2,2,7168]{3,2,1,0:T(2,128)(2,1)} %copy.22), calls=%async_computation.1 | async-start | bytes 1835008 | tf_op jit(solution)/shard_map/all_to_all | solution.py:72

commit v4 on v1

v4 whole, which is shorter than its diff:
```python
import jax
import jax.numpy as jnp
import numpy as np
from jax import lax
from jax.sharding import Mesh
from jax.sharding import PartitionSpec as P

EH = 1024
HS = 256
CROSS = ("x", "zh")
SPREAD = ("x", "zh", "zl")


def swap(value, axis):
    return lax.ppermute(value, axis, [(0, 1), (1, 0)])


def body(tokens, expert_ids, gate_codes, w_gate, w_up, w_down):
    step_count, row_count, width = tokens.shape
    experts_all = lax.axis_size(CROSS)
    codes = gate_codes.astype(jnp.float32)
    gate_weight = codes / jnp.sum(codes, -1, keepdims=True)
    chosen = expert_ids[..., None] == jnp.arange(experts_all, dtype=jnp.int32)
    table = jnp.sum(jnp.where(chosen, gate_weight[..., None], 0.0), -2)

    gathered = lax.all_gather(tokens, SPREAD, axis=0, tiled=False)
    rows = jnp.stack([gathered, swap(gathered, "c")], 0)
    gate_act = jnp.einsum("...d,dh->...h", rows, w_gate[0], preferred_element_type=jnp.float32)
    up_act = jnp.einsum("...d,dh->...h", rows, w_up[0], preferred_element_type=jnp.float32)
    hidden = (jax.nn.silu(gate_act) * up_act).astype(jnp.bfloat16)
    partial_out = jnp.einsum(
        "...h,hd->...d", hidden, w_down[0], preferred_element_type=jnp.float32
    ).astype(jnp.bfloat16)
    chip_sum = partial_out[0].astype(jnp.float32) + swap(partial_out[1], "c").astype(jnp.float32)
    chip_sum = chip_sum.astype(jnp.bfloat16).reshape(experts_all, 2, step_count, row_count, width)
    my_zl = lax.axis_index("zl")
    own = lax.dynamic_index_in_dim(chip_sum, my_zl, 1, keepdims=False)
    other = lax.dynamic_index_in_dim(chip_sum, 1 - my_zl, 1, keepdims=False)
    expert_out = own.astype(jnp.float32) + swap(other, "zl").astype(jnp.float32)
    returned = lax.all_to_all(
        expert_out.astype(jnp.bfloat16), CROSS, split_axis=0, concat_axis=0, tiled=True
    ).astype(jnp.float32)
    weights = jnp.moveaxis(table, -1, 0)[..., None]
    mixed = jnp.sum(weights * returned, 0)
    return mixed.astype(jnp.bfloat16)


def solution(mesh):
    devices = np.asarray(mesh.devices)
    dp, expert = devices.shape
    chip_mesh = Mesh(
        devices.reshape(dp, 4, expert // 16, 2, 2), ("dp", "x", "zh", "zl", "c")
    )
    rows_spec = P(None, ("dp", "x", "zh", "zl", "c"), None)
    blocks_spec = P(("dp", "x", "zh", "zl", "c"), None, None)
    placed = (rows_spec, rows_spec, rows_spec, blocks_spec, blocks_spec, blocks_spec)
    return jax.shard_map(
        body, mesh=chip_mesh, in_specs=placed, out_specs=rows_spec, check_vma=False
    )
```

time: 343 us -> 184 us (0.54); the launches traced: 339 us -> 184 us
  blocking collectives: 225 us -> 0 us
  waiting for transfers between devices: 46.3 us -> 137 us
  local copies, waits for them, and re-layouts: 36.4 us -> 16.3 us
  matrix products: 15.4 us -> 3.4 us
  starting transfers between devices: 0.04 us -> 7.92 us
  other arithmetic: 1.83 us -> 5.99 us
    unnamed x1 -> x0, blocking collectives: 173 us -> none
    all_gather x1, waiting for transfers between devices: 28.3 us -> 82 us  [body(): gathered = lax.all_gather(tokens, SPREAD, axis=0, tiled=False)]
    all_gather x1 -> x0, blocking collectives: 52 us -> none  [body(): lax.all_gather(jnp.swapaxes(table, 0, 1), ('x', 'z', 'c'), axis=0, tiled=...]
    reshape x4 -> x1, local copies, waits for them, and re-layouts: 32.8 us -> 3.88 us  [body(): chip_sum.astype(jnp.bfloat16)]
    ppermute x0 -> x3, waiting for transfers between devices: none -> 28 us  [swap(): return lax.ppermute(value, axis, [(0, 1), (1, 0)])]
    all_to_all x0 -> x1, waiting for transfers between devices: none -> 26.4 us  [body(): lax.all_to_all(expert_out.astype(jnp.bfloat16), CROSS, split_axis=0, conc...]
    reduce_scatter x1 -> x0, waiting for transfers between devices: 17.9 us -> none  [body(): mixed = lax.psum_scatter(contrib, 'c', scatter_dimension=0, tiled=True)]
    dot_general x2 -> x3, matrix products: 15.4 us -> 3.4 us  [the longest x1 1.14 us: body(): jnp.einsum('...d,dh->...h', rows, w_gate[0], preferred_element_type=jnp.f...]
  transfers between devices with their start and end apart: 2 -> 5, of which waited for: 2 -> 5; matrix products, arithmetic and copies ran while one was open for 1% -> 0% of each run, Pallas kernels for 0% -> 0%
where the time goes in v4:
time: 184 us
  waiting for transfers between devices  137 us (74%)
  local copies, waits for them, and re-layouts  16.3 us (9%)
  between operations  13.5 us (7%)
  starting transfers between devices  7.92 us (4%)
  other arithmetic  5.99 us (3%)
  matrix products  3.4 us (2%)
    all_gather x1, waiting for transfers between devices, body(): gathered = lax.all_gather(tokens, SPREAD, axis=0, tiled=False)  82 us
    ppermute x3, waiting for transfers between devices, swap(): return lax.ppermute(value, axis, [(0, 1), (1, 0)])  28 us
    all_to_all x1, waiting for transfers between devices, body(): lax.all_to_all(expert_out.astype(jnp.bfloat16), CROSS, split_axis=0, conc...  26.4 us
    all_to_all x1, starting transfers between devices, body(): lax.all_to_all(expert_out.astype(jnp.bfloat16), CROSS, split_axis=0, conc...  6.04 us
    reshape x1, local copies, waits for them, and re-layouts, body(): chip_sum.astype(jnp.bfloat16)  3.88 us
    dynamic_slice x1, local copies, waits for them, and re-layouts, body(): own = lax.dynamic_index_in_dim(chip_sum, my_zl, 1, keepdims=False)  3.78 us
    unnamed x15, local copies, waits for them, and re-layouts  3.76 us
    convert_element_type x1, other arithmetic, body(): chip_sum.astype(jnp.bfloat16)  3.74 us
  transfers between devices with their start and end apart: 5, of which 5 were waited for; matrix products, arithmetic and copies ran while one was open for 0% of the time, Pallas kernels for 0%

profile of v4, /device:TPU:32, one launch (start us, length us, event | category | flops | bytes accessed | tf_op | source)
XLA Modules:
  0.0 184.2 jit_solution(17024617476488528169)
XLA Ops:
  6.5 0.0 all-gather.3.cloned.1.call-start
  6.5 0.7 all-gather.3.cloned.1.call-update
  7.3 82.0 %all-gather.3.cloned.1.call-done = bf16[64,2,7168]{2,1,0:T(2,128)(2,1)} async-done(((bf16[2,2,7168]{2,1,0:T(2,128)(2,1)}), bf16[64,2,7168]{2,1,0:T(2,128)(2,1)}) %all-gather.3.cloned.1.call-update) | async-done | bytes 1835024 | tf_op jit(solution)/shard_map/all_gather | solution.py:26
  89.2 0.0 copy-start.1
  89.2 2.2 %copy.17 = bf16[32,2,2,7168]{3,0,2,1:T(8,128)(2,1)S(1)} copy(bf16[32,2,2,7168]{3,2,1,0:T(2,128)(2,1)} %bitcast.44) | data formatting | bytes 3670016 | tf_op jit(solution)/shard_map/all_gather | solution.py:26
  91.4 0.1 collective-permute-start
  91.5 0.0 copy-done.1
  91.5 0.0 copy-start.4
  91.6 0.5 copy.18
  92.1 3.2 %collective-permute-done = bf16[32,2,2,7168]{3,0,2,1:T(8,128)(2,1)S(1)} collective-permute-done((bf16[32,2,2,7168]{3,0,2,1:T(8,128)(2,1)S(1)}, bf16[32,2,2,7168]{3,0,2,1:T(8,128)(2,1)S(1)}, u32[]{:S(2)}, u32[]{:S(2)}) %collective-permute-start) | collective-permute-done | bytes 1835040 | tf_op jit(solution)/shard_map/ppermute | solution.py:15
  95.3 0.0 copy-done.4
  95.3 0.0 copy-start.5
  95.3 1.1 fusion.4
  96.5 0.9 copy-done.5
  97.3 0.0 copy-start.2
  97.3 1.1 fusion.2
  98.5 0.9 copy-done.2
  99.4 1.1 convolution_convert_fusion
  100.5 0.0 copy-start
  100.5 0.1 slice_bitcast_fusion
  100.7 1.6 copy-done
  102.3 0.1 collective-permute-start.1
  102.5 3.8 %collective-permute-done.1 = bf16[32,2,2,7168]{3,0,2,1:T(8,128)(2,1)} collective-permute-done((bf16[32,2,2,7168]{3,0,2,1:T(8,128)(2,1)S(1)}, bf16[32,2,2,7168]{3,0,2,1:T(8,128)(2,1)}, u32[]{:S(2)}, u32[]{:S(2)}) %collective-permute-start.1) | collective-permute-done | bytes 1835040 | tf_op jit(solution)/shard_map/ppermute | solution.py:15
  106.2 3.7 %fusion = bf16[32,2,2,7168]{3,0,2,1:T(8,128)(2,1)} fusion(bf16[32,2,2,7168]{3,0,2,1:T(8,128)(2,1)} %collective-permute-done.1, bf16[2,32,2,2,7168]{4,1,3,2,0:T(8,128)(2,1)} %copy-done), kind=kLoop, calls=%fused_computation.3 | loop fusion | flops 3670016 | bytes 5505024 | tf_op jit(solution)/shard_map/convert_element_type | solution.py:35
  110.0 3.9 %reshape.11 = bf16[16,2,2,2,7168]{4,1,0,3,2:T(2,128)(2,1)S(1)} reshape(bf16[32,2,2,7168]{3,0,2,1:T(8,128)(2,1)} %fusion) | data formatting | bytes 3670016 | tf_op jit(solution)/shard_map/reshape | solution.py:35
  113.9 3.8 %constant_dynamic-slice_fusion.1 = (bf16[16,1,2,2,7168]{4,1,0,3,2:T(2,128)(2,1)S(1)}, bf16[16,1,2,2,7168]{4,1,0,3,2:T(2,128)(2,1)S(1)}) fusion(bf16[16,2,2,2,7168]{4,1,0,3,2:T(2,128)(2,1)S(1)} %reshape.11, s32[]{:T(128)S(6)} %select_n.12, s32[]{:T(128)S(6)} %select_n.13), kind=kLoop, calls=%fused_computation.23 | loop fusion | bytes 3670024 | tf_op jit(solution)/shard_map/jit(dynamic_index_in_dim)/dynamic_slice | solution.py:37
  117.6 0.3 copy.31
  117.9 1.6 collective-permute-start.2
  119.6 21.0 %collective-permute-done.2 = bf16[16,2,2,7168]{3,0,2,1:T(8,128)(2,1)S(1)} collective-permute-done((bf16[16,2,2,7168]{3,0,2,1:T(8,128)(2,1)S(1)}, bf16[16,2,2,7168]{3,0,2,1:T(8,128)(2,1)S(1)}, u32[]{:S(2)}, u32[]{:S(2)}) %collective-permute-start.2) | collective-permute-done | bytes 917536 | tf_op jit(solution)/shard_map/ppermute | solution.py:15
  140.6 0.4 fusion.6
  141.0 0.0 copy-start.6
  141.0 0.0 copy-start.3
  141.0 1.9 %copy.21 = bf16[16,2,2,7168]{3,2,1,0:T(2,128)(2,1)} copy(bf16[16,2,2,7168]{3,0,2,1:T(8,128)(2,1)S(1)} %fusion.6) | data formatting | bytes 1835008 | tf_op jit(solution)/shard_map/convert_element_type | solution.py:41
  142.9 6.0 %all-to-all-start = ((bf16[16,2,2,7168]{3,2,1,0:T(2,128)(2,1)}), bf16[16,2,2,7168]{3,2,1,0:T(2,128)(2,1)S(1)}, u32[]{:S(2)}, u32[]{:S(2)}) async-start(bf16[16,2,2,7168]{3,2,1,0:T(2,128)(2,1)} %copy.21), calls=%async_computation | async-start | bytes 1835008 | tf_op jit(solution)/shard_map/all_to_all | solution.py:40
  148.9 0.0 copy-done.6
  149.0 0.1 convert_divide_fusion
  149.0 0.0 copy-done.3
  149.0 0.1 select_reduce_fusion
  149.1 0.1 copy.16
  149.2 26.4 %all-to-all-done = bf16[16,2,2,7168]{3,2,1,0:T(2,128)(2,1)S(1)} async-done(((bf16[16,2,2,7168]{3,2,1,0:T(2,128)(2,1)}), bf16[16,2,2,7168]{3,2,1,0:T(2,128)(2,1)S(1)}, u32[]{:S(2)}, u32[]{:S(2)}) %all-to-all-start) | async-done | bytes 917536 | tf_op jit(solution)/shard_map/all_to_all | solution.py:40
  175.6 1.7 multiply_reduce_fusion
Async XLA Ops:
  6.5 82.7 %all-gather.3.cloned.1.call-start = ((), (), s32[]{:S(2)}) async-start(), calls=%async_computation.1 | async-start | bytes 1892352 | tf_op jit(solution)/shard_map/all_gather | solution.py:26
  89.2 2.3 %copy-start.1 = (bf16[64,2,7168]{2,1,0:T(2,128)(2,1)S(1)}, bf16[64,2,7168]{2,1,0:T(2,128)(2,1)}, u32[]{:S(2)}) copy-start(bf16[64,2,7168]{2,1,0:T(2,128)(2,1)} %all-gather.3.cloned.1.call-done) | copy-start | bytes 5505028
  91.4 3.9 %collective-permute-start = (bf16[32,2,2,7168]{3,0,2,1:T(8,128)(2,1)S(1)}, bf16[32,2,2,7168]{3,0,2,1:T(8,128)(2,1)S(1)}, u32[]{:S(2)}, u32[]{:S(2)}) collective-permute-start(bf16[32,2,2,7168]{3,0,2,1:T(8,128)(2,1)S(1)} %copy.17), channel_id=1, source_target_pairs={{0,1},{1,0},{2,3},{3,2},{4,5},{5,4},{6,7},{7,6},{8,9},{9,8},{10,11... | collective-permute-start | bytes 5505032 | tf_op jit(solution)/shard_map/ppermute | solution.py:15
  91.5 3.8 %copy-start.4 = (bf16[1,7168,256]{2,1,0:T(8,128)(2,1)S(1)}, bf16[1,7168,256]{2,1,0:T(8,128)(2,1)}, u32[]{:S(2)}) copy-start(bf16[1,7168,256]{2,1,0:T(8,128)(2,1)} %param.9) | copy-start | bytes 11010052
  95.3 2.0 %copy-start.5 = (bf16[1,7168,256]{2,1,0:T(8,128)(2,1)S(1)}, bf16[1,7168,256]{2,1,0:T(8,128)(2,1)}, u32[]{:S(2)}) copy-start(bf16[1,7168,256]{2,1,0:T(8,128)(2,1)} %param.10) | copy-start | bytes 11010052
  97.3 2.0 %copy-start.2 = (bf16[1,256,7168]{2,1,0:T(8,128)(2,1)S(1)}, bf16[1,256,7168]{2,1,0:T(8,128)(2,1)}, u32[]{:S(2)}) copy-start(bf16[1,256,7168]{2,1,0:T(8,128)(2,1)} %param.11) | copy-start | bytes 11010052
  100.5 1.8 copy-start
  102.3 3.9 %collective-permute-start.1 = (bf16[32,2,2,7168]{3,0,2,1:T(8,128)(2,1)S(1)}, bf16[32,2,2,7168]{3,0,2,1:T(8,128)(2,1)}, u32[]{:S(2)}, u32[]{:S(2)}) collective-permute-start(bf16[32,2,2,7168]{3,0,2,1:T(8,128)(2,1)S(1)} %slice_bitcast_fusion), channel_id=1, source_target_pairs={{0,1},{1,0},{2,3},{3,2},{4,5},{5,4},{6,7},{7,6},{8,9},{9,8},{10,11... | collective-permute-start | bytes 5505032 | tf_op jit(solution)/shard_map/ppermute | solution.py:15
  117.9 22.7 %collective-permute-start.2 = (bf16[16,2,2,7168]{3,0,2,1:T(8,128)(2,1)S(1)}, bf16[16,2,2,7168]{3,0,2,1:T(8,128)(2,1)S(1)}, u32[]{:S(2)}, u32[]{:S(2)}) collective-permute-start(bf16[16,2,2,7168]{3,0,2,1:T(8,128)(2,1)S(1)} %bitcast.46), channel_id=1, source_target_pairs={{0,2},{2,0},{1,3},{3,1},{4,6},{6,4},{5,7},{7,5},{8,10},{10,8},{9,1... | collective-permute-start | bytes 2752520 | tf_op jit(solution)/shard_map/ppermute | solution.py:15
  141.0 8.0 %copy-start.6 = (s32[2,2,8]{2,1,0:T(2,128)S(1)}, s32[2,2,8]{2,1,0:T(2,128)}, u32[]{:S(2)}) copy-start(s32[2,2,8]{2,1,0:T(2,128)} %param.8) | copy-start | bytes 388
  141.0 8.0 %copy-start.3 = (s32[2,2,8]{2,1,0:T(2,128)S(1)}, s32[2,2,8]{2,1,0:T(2,128)}, u32[]{:S(2)}) copy-start(s32[2,2,8]{2,1,0:T(2,128)} %param.7) | copy-start | bytes 388
  142.9 32.7 %all-to-all-start = ((bf16[16,2,2,7168]{3,2,1,0:T(2,128)(2,1)}), bf16[16,2,2,7168]{3,2,1,0:T(2,128)(2,1)S(1)}, u32[]{:S(2)}, u32[]{:S(2)}) async-start(bf16[16,2,2,7168]{3,2,1,0:T(2,128)(2,1)} %copy.21), calls=%async_computation | async-start | bytes 1835008 | tf_op jit(solution)/shard_map/all_to_all | solution.py:40
Sparse Core Ops, SparseCore 0:
  9.9 79.2 all-gather.2

commit v5 on v3

--- a/solution.py
+++ b/solution.py
@@ -8,6 +8,7 @@
 EH = 1024
 HS = 256
 CROSS = ("x", "zh")
+PAIRS = ("x", "zh", "zl")
 
 
 def route_tables(step_ids, step_codes, experts_all, capacity):
@@ -54,9 +55,8 @@
         ).astype(jnp.bfloat16)
         send_rows.append(slots.reshape(experts_all, 1, capacity, width))
         mix_tables.append(mix_table)
-    slots = jnp.concatenate(send_rows, 1)
-    received = lax.all_to_all(slots, CROSS, split_axis=0, concat_axis=0, tiled=True)
-    received = jnp.stack([received, swap(received, "zl")], 0)
+    slots = jnp.repeat(jnp.concatenate(send_rows, 1), lax.axis_size("zl"), 0)
+    received = lax.all_to_all(slots, PAIRS, split_axis=0, concat_axis=0, tiled=True)
     received = jnp.stack([received, swap(received, "c")], 0)
     gate_act = jnp.einsum(
         "...cd,dh->...ch", received, w_gate[0], preferred_element_type=jnp.float32
@@ -67,11 +67,10 @@
         "...ch,hd->...cd", hidden, w_down[0], preferred_element_type=jnp.float32
     ).astype(jnp.bfloat16)
     chip_sum = partial_out[0].astype(jnp.float32) + swap(partial_out[1], "c").astype(jnp.float32)
-    chip_sum = chip_sum.astype(jnp.bfloat16)
-    expert_out = chip_sum[0].astype(jnp.float32) + swap(chip_sum[1], "zl").astype(jnp.float32)
     returned = lax.all_to_all(
-        expert_out.astype(jnp.bfloat16), CROSS, split_axis=0, concat_axis=0, tiled=True
+        chip_sum.astype(jnp.bfloat16), PAIRS, split_axis=0, concat_axis=0, tiled=True
     ).astype(jnp.float32)
+    returned = jnp.sum(returned.reshape(experts_all, -1, *returned.shape[1:]), 1)
     results = []
     for step in range(step_count):
         combined = jnp.dot(

time: 135 us -> 136 us (level)
  waiting for transfers between devices: 74.1 us -> 51 us
  blocking collectives: 36.4 us -> 56.7 us
  local copies, waits for them, and re-layouts: 7.35 us -> 10.9 us
  starting transfers between devices: 8 us -> 5.4 us
  other arithmetic: 3.69 us -> 5.59 us
    ppermute x4 -> x2, waiting for transfers between devices: 47.9 us -> 7.42 us  [swap(): return lax.ppermute(value, axis, [(0, 1), (1, 0)])]
    all_to_all x1, blocking collectives: 36.4 us -> 56.7 us  [body(): lax.all_to_all(slots, PAIRS, split_axis=0, concat_axis=0, tiled=True)]
    all_to_all x1, waiting for transfers between devices: 26.3 us -> 43.6 us  [body(): lax.all_to_all(chip_sum.astype(jnp.bfloat16), PAIRS, split_axis=0, concat...]
    ppermute x4 -> x2, starting transfers between devices: 3.11 us -> 0.32 us  [swap(): return lax.ppermute(value, axis, [(0, 1), (1, 0)])]
    reduce_sum x0 -> x1, other arithmetic: none -> 2.23 us  [body(): jnp.sum(returned.reshape(experts_all, -1, *returned.shape[1:]), 1)]
  transfers between devices with their start and end apart: 5 -> 3, of which waited for: 5 -> 3; matrix products, arithmetic and copies ran while one was open for 0% -> 0% of each run, Pallas kernels for 0% -> 0%
where the time goes in v5:
time: 136 us; the launch traced here: 135 us
  blocking collectives  56.7 us (42%)
  waiting for transfers between devices  51 us (38%)
  local copies, waits for them, and re-layouts  10.9 us (8%)
  other arithmetic  5.59 us (4%)
  starting transfers between devices  5.4 us (4%)
  matrix products  5.28 us (4%)
    all_to_all x1, blocking collectives, body(): lax.all_to_all(slots, PAIRS, split_axis=0, concat_axis=0, tiled=True)  56.7 us
    all_to_all x1, waiting for transfers between devices, body(): lax.all_to_all(chip_sum.astype(jnp.bfloat16), PAIRS, split_axis=0, concat...  43.6 us
    ppermute x2, waiting for transfers between devices, swap(): return lax.ppermute(value, axis, [(0, 1), (1, 0)])  7.42 us
    all_to_all x1, starting transfers between devices, body(): lax.all_to_all(chip_sum.astype(jnp.bfloat16), PAIRS, split_axis=0, concat...  5.08 us
    convert_element_type x1, local copies, waits for them, and re-layouts, body(): chip_sum.astype(jnp.bfloat16)  3.14 us
  transfers between devices with their start and end apart: 3, of which 3 were waited for; matrix products, arithmetic and copies ran while one was open for 0% of the time, Pallas kernels for 0%

profile of v5, /device:TPU:32, one launch (start us, length us, event | category | flops | bytes accessed | tf_op | source)
XLA Modules:
  0.0 135.1 jit_solution(4538749633358497216)
XLA Ops:
  0.0 0.7 fusion.21
  0.7 0.1 reshape_squeeze.10
  0.8 0.1 fusion.13
  0.9 0.2 select_reduce_fusion.1
  1.1 0.8 slice_bitcast_fusion.3
  1.9 0.4 convolution_convert_fusion.1
  2.3 0.2 reshape.112
  2.5 0.1 eq.68
  2.5 0.1 fusion.14
  2.7 0.2 select_reduce_fusion.3
  2.9 0.4 convolution_convert_fusion.2
  3.3 0.2 reshape.110
  3.4 1.3 pad_maximum_fusion.3
  4.7 0.6 copy.20
  5.4 1.1 broadcast_in_dim.8
  6.5 0.0 copy-start.3
  6.5 56.7 %all_to_all.10 = bf16[32,2,2,7168]{3,2,1,0:T(2,128)(2,1)S(1)} all-to-all(bf16[32,2,2,7168]{3,2,1,0:T(2,128)(2,1)S(1)} %bitcast.62), channel_id=1, replica_groups=mesh['dp'=4,'x'=4,'zh'=4,'zl'=2,'c'=2] {'x','zh','zl'}, dimensions={0} | all-to-all | bytes 3670016 | tf_op jit(solution)/shard_map/all_to_all | solution.py:59
  63.2 0.5 copy.37
  63.8 0.1 collective-permute-start
  63.9 3.8 %collective-permute-done = bf16[32,2,2,7168]{3,0,2,1:T(8,128)(2,1)S(1)} collective-permute-done((bf16[32,2,2,7168]{3,0,2,1:T(8,128)(2,1)S(1)}, bf16[32,2,2,7168]{3,0,2,1:T(8,128)(2,1)S(1)}, u32[]{:S(2)}, u32[]{:S(2)}) %collective-permute-start) | collective-permute-done | bytes 1835040 | tf_op jit(solution)/shard_map/ppermute | solution.py:35
  67.6 0.0 copy-done.3
  67.6 0.0 copy-start.4
  67.6 1.1 fusion.6
  68.8 0.9 copy-done.4
  69.7 0.0 copy-start
  69.7 1.2 fusion.4
  70.9 0.9 copy-done
  71.7 1.1 convolution_convert_fusion
  72.9 0.1 slice_bitcast_fusion
  73.0 0.2 collective-permute-start.1
  73.2 3.6 %collective-permute-done.1 = bf16[32,2,2,7168]{3,0,2,1:T(8,128)(2,1)S(1)} collective-permute-done((bf16[32,2,2,7168]{3,0,2,1:T(8,128)(2,1)S(1)}, bf16[32,2,2,7168]{3,0,2,1:T(8,128)(2,1)S(1)}, u32[]{:S(2)}, u32[]{:S(2)}) %collective-permute-start.1) | collective-permute-done | bytes 1835040 | tf_op jit(solution)/shard_map/ppermute | solution.py:35
  76.9 0.4 fusion.2
  77.3 0.0 copy-start.2
  77.3 0.0 copy-start.1
  77.3 3.1 %copy.23 = bf16[32,2,2,7168]{3,2,1,0:T(2,128)(2,1)} copy(bf16[32,2,2,7168]{3,0,2,1:T(8,128)(2,1)S(1)} %fusion.2) | data formatting | bytes 3670016 | tf_op jit(solution)/shard_map/convert_element_type | solution.py:71
  80.5 5.1 %all-to-all-start.1 = ((bf16[32,2,2,7168]{3,2,1,0:T(2,128)(2,1)}), bf16[32,2,2,7168]{3,2,1,0:T(2,128)(2,1)S(1)}, u32[]{:S(2)}, u32[]{:S(2)}) async-start(bf16[32,2,2,7168]{3,2,1,0:T(2,128)(2,1)} %copy.23), calls=%async_computation.1 | async-start | bytes 3670016 | tf_op jit(solution)/shard_map/all_to_all | solution.py:70
  85.6 0.1 sub.13
  85.7 0.1 sub.11
  85.7 0.0 copy-done.2
  85.7 0.1 convert_reduce_fusion.2
  85.9 0.1 bitcast_divide_fusion.1
  86.0 0.0 copy-done.1
  86.0 0.1 select_reduce_fusion
  86.1 43.6 %all-to-all-done.1 = bf16[32,2,2,7168]{3,2,1,0:T(2,128)(2,1)S(1)} async-done(((bf16[32,2,2,7168]{3,2,1,0:T(2,128)(2,1)}), bf16[32,2,2,7168]{3,2,1,0:T(2,128)(2,1)S(1)}, u32[]{:S(2)}, u32[]{:S(2)}) %all-to-all-start.1) | async-done | bytes 1835040 | tf_op jit(solution)/shard_map/all_to_all | solution.py:70
  129.7 2.2 %convert_reduce_fusion = f32[16,2,2,7168]{3,2,1,0:T(2,128)S(1)} fusion(bf16[32,2,2,7168]{3,2,1,0:T(2,128)(2,1)S(1)} %all-to-all-done.1), kind=kLoop, calls=%fused_computation.8 | loop fusion | flops 1376256 | bytes 3670016 | tf_op jit(solution)/shard_map/reduce_sum | solution.py:73
  131.9 0.1 fusion.20
  132.0 0.6 reshape_squeeze.11
  132.7 0.6 reshape_squeeze.12
  133.3 0.5 fusion
  133.9 0.5 fusion.1
  134.4 0.7 pad_maximum_fusion.4
  (5 shorter events, 0.1 us)
Async XLA Ops:
  6.5 61.2 %copy-start.3 = (bf16[1,7168,256]{2,1,0:T(8,128)(2,1)S(1)}, bf16[1,7168,256]{2,1,0:T(8,128)(2,1)}, u32[]{:S(2)}) copy-start(bf16[1,7168,256]{2,1,0:T(8,128)(2,1)} %param.9) | copy-start | bytes 11010052
  63.8 3.9 %collective-permute-start = (bf16[32,2,2,7168]{3,0,2,1:T(8,128)(2,1)S(1)}, bf16[32,2,2,7168]{3,0,2,1:T(8,128)(2,1)S(1)}, u32[]{:S(2)}, u32[]{:S(2)}) collective-permute-start(bf16[32,2,2,7168]{3,0,2,1:T(8,128)(2,1)S(1)} %copy.37), channel_id=1, source_target_pairs={{0,1},{1,0},{2,3},{3,2},{4,5},{5,4},{6,7},{7,6},{8,9},{9,8},{10,11... | collective-permute-start | bytes 5505032 | tf_op jit(solution)/shard_map/ppermute | solution.py:35
  67.6 2.0 %copy-start.4 = (bf16[1,7168,256]{2,1,0:T(8,128)(2,1)S(1)}, bf16[1,7168,256]{2,1,0:T(8,128)(2,1)}, u32[]{:S(2)}) copy-start(bf16[1,7168,256]{2,1,0:T(8,128)(2,1)} %param.10) | copy-start | bytes 11010052
  69.7 2.0 %copy-start = (bf16[1,256,7168]{2,1,0:T(8,128)(2,1)S(1)}, bf16[1,256,7168]{2,1,0:T(8,128)(2,1)}, u32[]{:S(2)}) copy-start(bf16[1,256,7168]{2,1,0:T(8,128)(2,1)} %param.11) | copy-start | bytes 11010052
  73.0 3.9 %collective-permute-start.1 = (bf16[32,2,2,7168]{3,0,2,1:T(8,128)(2,1)S(1)}, bf16[32,2,2,7168]{3,0,2,1:T(8,128)(2,1)S(1)}, u32[]{:S(2)}, u32[]{:S(2)}) collective-permute-start(bf16[32,2,2,7168]{3,0,2,1:T(8,128)(2,1)S(1)} %slice_bitcast_fusion), channel_id=1, source_target_pairs={{0,1},{1,0},{2,3},{3,2},{4,5},{5,4},{6,7},{7,6},{8,9},{9,8},{10,11... | collective-permute-start | bytes 5505032 | tf_op jit(solution)/shard_map/ppermute | solution.py:35
  77.3 8.4 %copy-start.2 = (s32[2,2,8]{2,1,0:T(2,128)S(1)}, s32[2,2,8]{2,1,0:T(2,128)}, u32[]{:S(2)}) copy-start(s32[2,2,8]{2,1,0:T(2,128)} %param.8) | copy-start | bytes 388
  77.3 8.6 %copy-start.1 = (s32[2,2,8]{2,1,0:T(2,128)S(1)}, s32[2,2,8]{2,1,0:T(2,128)}, u32[]{:S(2)}) copy-start(s32[2,2,8]{2,1,0:T(2,128)} %param.7) | copy-start | bytes 388
  80.5 49.2 %all-to-all-start.1 = ((bf16[32,2,2,7168]{3,2,1,0:T(2,128)(2,1)}), bf16[32,2,2,7168]{3,2,1,0:T(2,128)(2,1)S(1)}, u32[]{:S(2)}, u32[]{:S(2)}) async-start(bf16[32,2,2,7168]{3,2,1,0:T(2,128)(2,1)} %copy.23), calls=%async_computation.1 | async-start | bytes 3670016 | tf_op jit(solution)/shard_map/all_to_all | solution.py:70

commit v6 on v5

--- a/solution.py
+++ b/solution.py
@@ -47,15 +47,18 @@
             expert_ids[step], gate_codes[step], experts_all, capacity
         )
         repeated = jnp.repeat(tokens[step], top_count, 0)
+        chips = lax.axis_size("zl")
+        placement = jnp.repeat(placement.reshape(-1, experts_all, 1, capacity), chips, 2)
         slots = jnp.einsum(
             "as,ad->sd",
-            placement.astype(jnp.bfloat16),
+            placement.reshape(placement.shape[0], -1).astype(jnp.bfloat16),
             repeated,
             preferred_element_type=jnp.float32,
         ).astype(jnp.bfloat16)
-        send_rows.append(slots.reshape(experts_all, 1, capacity, width))
-        mix_tables.append(mix_table)
-    slots = jnp.repeat(jnp.concatenate(send_rows, 1), lax.axis_size("zl"), 0)
+        send_rows.append(slots.reshape(experts_all * chips, 1, capacity, width))
+        mix_table = jnp.repeat(mix_table.reshape(row_count, experts_all, 1, capacity), chips, 2)
+        mix_tables.append(mix_table.reshape(row_count, -1))
+    slots = jnp.concatenate(send_rows, 1)
     received = lax.all_to_all(slots, PAIRS, split_axis=0, concat_axis=0, tiled=True)
     received = jnp.stack([received, swap(received, "c")], 0)
     gate_act = jnp.einsum(
@@ -70,7 +73,6 @@
     returned = lax.all_to_all(
         chip_sum.astype(jnp.bfloat16), PAIRS, split_axis=0, concat_axis=0, tiled=True
     ).astype(jnp.float32)
-    returned = jnp.sum(returned.reshape(experts_all, -1, *returned.shape[1:]), 1)
     results = []
     for step in range(step_count):
         combined = jnp.dot(

time: 136 us -> 138 us (1.015)
  local copies, waits for them, and re-layouts: 10.9 us -> 13.7 us
    reduce_sum x1 -> x0, other arithmetic: 2.23 us -> none  [body(): jnp.sum(returned.reshape(experts_all, -1, *returned.shape[1:]), 1)]
    slice x1, local copies, waits for them, and re-layouts: 0.12 us -> 2.19 us  [body(): returned[:, step].reshape(-1, width)]
    another operation x2, local copies, waits for them, and re-layouts: 1.26 us -> 2.82 us  [body(): returned[:, step].reshape(-1, width)]
  transfers between devices with their start and end apart: 3 -> 3, of which waited for: 3 -> 3; matrix products, arithmetic and copies ran while one was open for 0% -> 1% of each run, Pallas kernels for 0% -> 0%
where the time goes in v6:
time: 138 us; the launch traced here: 136 us
  blocking collectives  56.7 us (41%)
  waiting for transfers between devices  50.5 us (37%)
  local copies, waits for them, and re-layouts  13.7 us (10%)
  starting transfers between devices  5.41 us (4%)
  matrix products  5.08 us (4%)
  other arithmetic  4.6 us (3%)
    all_to_all x1, blocking collectives, body(): lax.all_to_all(slots, PAIRS, split_axis=0, concat_axis=0, tiled=True)  56.7 us
    all_to_all x1, waiting for transfers between devices, body(): lax.all_to_all(chip_sum.astype(jnp.bfloat16), PAIRS, split_axis=0, concat...  43.1 us
    ppermute x2, waiting for transfers between devices, swap(): return lax.ppermute(value, axis, [(0, 1), (1, 0)])  7.41 us
    all_to_all x1, starting transfers between devices, body(): lax.all_to_all(chip_sum.astype(jnp.bfloat16), PAIRS, split_axis=0, concat...  5.09 us
    convert_element_type x1, local copies, waits for them, and re-layouts, body(): chip_sum.astype(jnp.bfloat16)  3.14 us
    another operation x2, local copies, waits for them, and re-layouts, body(): returned[:, step].reshape(-1, width)  2.82 us
  transfers between devices with their start and end apart: 3, of which 3 were waited for; matrix products, arithmetic and copies ran while one was open for 1% of the time, Pallas kernels for 0%

profile of v6, /device:TPU:32, one launch (start us, length us, event | category | flops | bytes accessed | tf_op | source)
XLA Modules:
  0.0 136.2 jit_solution(4442820679837736552)
XLA Ops:
  0.0 0.7 fusion.19
  0.7 0.1 reshape_squeeze.10
  0.8 0.1 fusion.13
  0.9 0.2 select_reduce_fusion.1
  1.1 0.1 eq.82
  1.2 0.1 fusion.14
  1.3 0.2 select_reduce_fusion.3
  1.5 0.1 broadcast_compare_fusion.1
  1.6 0.8 slice_bitcast_fusion.3
  2.4 0.4 convolution_convert_fusion.2
  2.8 0.3 reshape.140
  3.2 0.4 convolution_convert_fusion.1
  3.6 0.3 reshape.142
  3.9 2.4 %pad_maximum_fusion.3 = bf16[32,2,2,7168]{3,2,1,0:T(2,128)(2,1)S(1)} fusion(bf16[32,1,2,7168]{3,2,1,0:T(2,128)(2,1)S(1)} %bitcast.71, bf16[32,1,2,7168]{3,2,1,0:T(2,128)(2,1)S(1)} %bitcast.70), kind=kLoop, calls=%fused_computation.17 | loop fusion | flops 917504 | bytes 3670016 | tf_op jit(solution)/shard_map/concatenate | solution.py:61
  6.3 0.0 copy-start.3
  6.3 56.7 %all_to_all.10 = bf16[32,2,2,7168]{3,2,1,0:T(2,128)(2,1)S(1)} all-to-all(bf16[32,2,2,7168]{3,2,1,0:T(2,128)(2,1)S(1)} %pad_maximum_fusion.3), channel_id=1, replica_groups=mesh['dp'=4,'x'=4,'zh'=4,'zl'=2,'c'=2] {'x','zh','zl'}, dimensions={0} | all-to-all | bytes 3670016 | tf_op jit(solution)/shard_map/all_to_all | solution.py:62
  63.1 0.5 copy.28
  63.6 0.1 collective-permute-start
  63.7 3.8 %collective-permute-done = bf16[32,2,2,7168]{3,0,2,1:T(8,128)(2,1)S(1)} collective-permute-done((bf16[32,2,2,7168]{3,0,2,1:T(8,128)(2,1)S(1)}, bf16[32,2,2,7168]{3,0,2,1:T(8,128)(2,1)S(1)}, u32[]{:S(2)}, u32[]{:S(2)}) %collective-permute-start) | collective-permute-done | bytes 1835040 | tf_op jit(solution)/shard_map/ppermute | solution.py:35
  67.5 0.0 copy-done.3
  67.5 0.0 copy-start.4
  67.5 1.1 fusion.6
  68.6 0.9 copy-done.4
  69.5 0.0 copy-start
  69.5 1.2 fusion.4
  70.7 0.9 copy-done
  71.6 1.1 convolution_convert_fusion
  72.7 0.1 slice_bitcast_fusion
  72.8 0.2 collective-permute-start.1
  73.1 3.6 %collective-permute-done.1 = bf16[32,2,2,7168]{3,0,2,1:T(8,128)(2,1)S(1)} collective-permute-done((bf16[32,2,2,7168]{3,0,2,1:T(8,128)(2,1)S(1)}, bf16[32,2,2,7168]{3,0,2,1:T(8,128)(2,1)S(1)}, u32[]{:S(2)}, u32[]{:S(2)}) %collective-permute-start.1) | collective-permute-done | bytes 1835040 | tf_op jit(solution)/shard_map/ppermute | solution.py:35
  76.7 0.4 fusion.2
  77.2 0.0 copy-start.2
  77.2 0.0 copy-start.1
  77.2 3.1 %copy.22 = bf16[32,2,2,7168]{3,2,1,0:T(2,128)(2,1)} copy(bf16[32,2,2,7168]{3,0,2,1:T(8,128)(2,1)S(1)} %fusion.2) | data formatting | bytes 3670016 | tf_op jit(solution)/shard_map/convert_element_type | solution.py:74
  80.3 5.1 %all-to-all-start.1 = ((bf16[32,2,2,7168]{3,2,1,0:T(2,128)(2,1)}), bf16[32,2,2,7168]{3,2,1,0:T(2,128)(2,1)S(1)}, u32[]{:S(2)}, u32[]{:S(2)}) async-start(bf16[32,2,2,7168]{3,2,1,0:T(2,128)(2,1)} %copy.22), calls=%async_computation.1 | async-start | bytes 3670016 | tf_op jit(solution)/shard_map/all_to_all | solution.py:73
  85.4 0.1 sub.11
  85.5 0.1 sub.13
  85.6 0.0 copy-done.2
  85.6 0.1 convert_reduce_fusion.1
  85.7 0.1 bitcast_divide_fusion.1
  85.8 0.0 copy-done.1
  85.8 0.1 select_reduce_fusion.2
  85.9 0.1 reshape.138
  86.0 0.1 reshape_reshape.12
  86.1 0.1 select_reduce_fusion
  86.2 0.1 reshape.143
  86.3 0.1 reshape_reshape.15
  86.5 43.1 %all-to-all-done.1 = bf16[32,2,2,7168]{3,2,1,0:T(2,128)(2,1)S(1)} async-done(((bf16[32,2,2,7168]{3,2,1,0:T(2,128)(2,1)}), bf16[32,2,2,7168]{3,2,1,0:T(2,128)(2,1)S(1)}, u32[]{:S(2)}, u32[]{:S(2)}) %all-to-all-start.1) | async-done | bytes 1835040 | tf_op jit(solution)/shard_map/all_to_all | solution.py:73
  129.5 2.2 %fusion.18 = (bf16[32,1,2,7168]{3,2,1,0:T(2,128)(2,1)}, bf16[32,1,2,7168]{3,2,1,0:T(2,128)(2,1)S(1)}) fusion(bf16[32,2,2,7168]{3,2,1,0:T(2,128)(2,1)S(1)} %all-to-all-done.1), kind=kLoop, calls=%fused_computation.54 | loop fusion | bytes 3670016 | tf_op jit(solution)/shard_map/slice | solution.py:80
  131.7 2.5 %reshape_squeeze.11 = bf16[64,7168]{1,0:T(8,128)(2,1)S(1)} reshape(bf16[32,1,2,7168]{3,2,1,0:T(2,128)(2,1)} %get-tuple-element.7) | data formatting | bytes 1835008 | tf_op jit(solution)/shard_map/reshape;squeeze | solution.py:80
  134.2 0.3 reshape_squeeze.12
  134.5 0.5 fusion
  135.0 0.5 fusion.1
  135.5 0.7 pad_maximum_fusion.4
  (11 shorter events, 0.2 us)
Async XLA Ops:
  6.3 61.2 %copy-start.3 = (bf16[1,7168,256]{2,1,0:T(8,128)(2,1)S(1)}, bf16[1,7168,256]{2,1,0:T(8,128)(2,1)}, u32[]{:S(2)}) copy-start(bf16[1,7168,256]{2,1,0:T(8,128)(2,1)} %param.9) | copy-start | bytes 11010052
  63.6 3.9 %collective-permute-start = (bf16[32,2,2,7168]{3,0,2,1:T(8,128)(2,1)S(1)}, bf16[32,2,2,7168]{3,0,2,1:T(8,128)(2,1)S(1)}, u32[]{:S(2)}, u32[]{:S(2)}) collective-permute-start(bf16[32,2,2,7168]{3,0,2,1:T(8,128)(2,1)S(1)} %copy.28), channel_id=1, source_target_pairs={{0,1},{1,0},{2,3},{3,2},{4,5},{5,4},{6,7},{7,6},{8,9},{9,8},{10,11... | collective-permute-start | bytes 5505032 | tf_op jit(solution)/shard_map/ppermute | solution.py:35
  67.5 2.0 %copy-start.4 = (bf16[1,7168,256]{2,1,0:T(8,128)(2,1)S(1)}, bf16[1,7168,256]{2,1,0:T(8,128)(2,1)}, u32[]{:S(2)}) copy-start(bf16[1,7168,256]{2,1,0:T(8,128)(2,1)} %param.10) | copy-start | bytes 11010052
  69.5 2.0 %copy-start = (bf16[1,256,7168]{2,1,0:T(8,128)(2,1)S(1)}, bf16[1,256,7168]{2,1,0:T(8,128)(2,1)}, u32[]{:S(2)}) copy-start(bf16[1,256,7168]{2,1,0:T(8,128)(2,1)} %param.11) | copy-start | bytes 11010052
  72.8 3.9 %collective-permute-start.1 = (bf16[32,2,2,7168]{3,0,2,1:T(8,128)(2,1)S(1)}, bf16[32,2,2,7168]{3,0,2,1:T(8,128)(2,1)S(1)}, u32[]{:S(2)}, u32[]{:S(2)}) collective-permute-start(bf16[32,2,2,7168]{3,0,2,1:T(8,128)(2,1)S(1)} %slice_bitcast_fusion), channel_id=1, source_target_pairs={{0,1},{1,0},{2,3},{3,2},{4,5},{5,4},{6,7},{7,6},{8,9},{9,8},{10,11... | collective-permute-start | bytes 5505032 | tf_op jit(solution)/shard_map/ppermute | solution.py:35
  77.2 8.4 %copy-start.2 = (s32[2,2,8]{2,1,0:T(2,128)S(1)}, s32[2,2,8]{2,1,0:T(2,128)}, u32[]{:S(2)}) copy-start(s32[2,2,8]{2,1,0:T(2,128)} %param.8) | copy-start | bytes 388
  77.2 8.6 %copy-start.1 = (s32[2,2,8]{2,1,0:T(2,128)S(1)}, s32[2,2,8]{2,1,0:T(2,128)}, u32[]{:S(2)}) copy-start(s32[2,2,8]{2,1,0:T(2,128)} %param.7) | copy-start | bytes 388
  80.3 49.2 %all-to-all-start.1 = ((bf16[32,2,2,7168]{3,2,1,0:T(2,128)(2,1)}), bf16[32,2,2,7168]{3,2,1,0:T(2,128)(2,1)S(1)}, u32[]{:S(2)}, u32[]{:S(2)}) async-start(bf16[32,2,2,7168]{3,2,1,0:T(2,128)(2,1)} %copy.22), calls=%async_computation.1 | async-start | bytes 3670016 | tf_op jit(solution)/shard_map/all_to_all | solution.py:73

commit v7 on v3

--- a/solution.py
+++ b/solution.py
@@ -67,8 +67,7 @@
         "...ch,hd->...cd", hidden, w_down[0], preferred_element_type=jnp.float32
     ).astype(jnp.bfloat16)
     chip_sum = partial_out[0].astype(jnp.float32) + swap(partial_out[1], "c").astype(jnp.float32)
-    chip_sum = chip_sum.astype(jnp.bfloat16)
-    expert_out = chip_sum[0].astype(jnp.float32) + swap(chip_sum[1], "zl").astype(jnp.float32)
+    expert_out = chip_sum[0] + swap(chip_sum[1].astype(jnp.bfloat16), "zl").astype(jnp.float32)
     returned = lax.all_to_all(
         expert_out.astype(jnp.bfloat16), CROSS, split_axis=0, concat_axis=0, tiled=True
     ).astype(jnp.float32)

time: 135 us -> 135 us (level)
  no operation moved by 1% of the time
where the time goes in v7:
time: 135 us
  waiting for transfers between devices  74.1 us (55%)
  blocking collectives  36.4 us (27%)
  starting transfers between devices  8 us (6%)
  local copies, waits for them, and re-layouts  7.38 us (5%)
  matrix products  4.78 us (4%)
  other arithmetic  3.69 us (3%)
    ppermute x4, waiting for transfers between devices, swap(): return lax.ppermute(value, axis, [(0, 1), (1, 0)])  47.9 us
    all_to_all x1, blocking collectives, body(): lax.all_to_all(slots, CROSS, split_axis=0, concat_axis=0, tiled=True)  36.4 us
    all_to_all x1, waiting for transfers between devices, body(): lax.all_to_all(expert_out.astype(jnp.bfloat16), CROSS, split_axis=0, conc...  26.3 us
    all_to_all x1, starting transfers between devices, body(): lax.all_to_all(expert_out.astype(jnp.bfloat16), CROSS, split_axis=0, conc...  4.89 us
    ppermute x4, starting transfers between devices, swap(): return lax.ppermute(value, axis, [(0, 1), (1, 0)])  3.11 us
  transfers between devices with their start and end apart: 5, of which 5 were waited for; matrix products, arithmetic and copies ran while one was open for 0% of the time, Pallas kernels for 0%

profile of v7, /device:TPU:32, one launch (start us, length us, event | category | flops | bytes accessed | tf_op | source)
XLA Modules:
  0.0 134.6 jit_solution(6995902376583086833)
XLA Ops:
  0.0 0.7 fusion.24
  0.7 0.1 reshape_squeeze.10
  0.8 0.1 fusion.15
  0.9 0.2 select_reduce_fusion.1
  1.1 0.8 slice_bitcast_fusion.4
  1.9 0.4 convolution_convert_fusion.1
  2.3 0.2 reshape.104
  2.5 0.1 eq.68
  2.6 0.1 fusion.16
  2.7 0.2 select_reduce_fusion.3
  2.9 0.4 convolution_convert_fusion.2
  3.3 0.2 reshape.102
  3.4 1.2 pad_maximum_fusion.4
  4.6 36.4 %all_to_all.10 = bf16[16,2,2,7168]{3,2,1,0:T(2,128)(2,1)S(1)} all-to-all(bf16[16,2,2,7168]{3,2,1,0:T(2,128)(2,1)S(1)} %pad_maximum_fusion.4), channel_id=1, replica_groups=mesh['dp'=4,'x'=4,'zh'=4,'zl'=2,'c'=2] {'x','zh'}, dimensions={0} | all-to-all | bytes 1835008 | tf_op jit(solution)/shard_map/all_to_all | solution.py:58
  41.1 0.0 copy-start.2
  41.1 0.3 copy.28
  41.4 2.1 %collective-permute-start = (bf16[16,2,2,7168]{3,0,2,1:T(8,128)(2,1)S(1)}, bf16[16,2,2,7168]{3,0,2,1:T(8,128)(2,1)S(1)}, u32[]{:S(2)}, u32[]{:S(2)}) collective-permute-start(bf16[16,2,2,7168]{3,0,2,1:T(8,128)(2,1)S(1)} %copy.28), channel_id=1, source_target_pairs={{0,2},{2,0},{1,3},{3,1},{4,6},{6,4},{5,7},{7,5},{8,10},{10,8},{9,1... | collective-permute-start | bytes 2752520 | tf_op jit(solution)/shard_map/ppermute | solution.py:34
  43.5 18.6 %collective-permute-done = bf16[16,2,2,7168]{3,0,2,1:T(8,128)(2,1)S(1)} collective-permute-done((bf16[16,2,2,7168]{3,0,2,1:T(8,128)(2,1)S(1)}, bf16[16,2,2,7168]{3,0,2,1:T(8,128)(2,1)S(1)}, u32[]{:S(2)}, u32[]{:S(2)}) %collective-permute-start) | collective-permute-done | bytes 917536 | tf_op jit(solution)/shard_map/ppermute | solution.py:34
  62.1 0.2 fusion.22
  62.4 0.1 collective-permute-start.1
  62.5 3.8 %collective-permute-done.1 = bf16[2,16,2,2,7168]{4,1,3,2,0:T(8,128)(2,1)S(1)} collective-permute-done((bf16[2,16,2,2,7168]{4,1,3,2,0:T(8,128)(2,1)S(1)}, bf16[2,16,2,2,7168]{4,1,3,2,0:T(8,128)(2,1)S(1)}, u32[]{:S(2)}, u32[]{:S(2)}) %collective-permute-start.1) | collective-permute-done | bytes 1835040 | tf_op jit(solution)/shard_map/ppermute | solution.py:34
  66.2 0.0 copy-done.2
  66.2 0.0 copy-start.3
  66.2 1.1 fusion.5
  67.4 0.9 copy-done.3
  68.3 0.0 copy-start.4
  68.3 1.1 fusion.3
  69.4 0.9 copy-done.4
  70.3 1.1 convolution_convert_fusion
  71.5 0.2 slice_bitcast_fusion.1
  71.6 0.2 collective-permute-start.2
  71.9 3.6 %collective-permute-done.2 = bf16[2,16,2,2,7168]{4,1,3,2,0:T(8,128)(2,1)S(1)} collective-permute-done((bf16[2,16,2,2,7168]{4,1,3,2,0:T(8,128)(2,1)S(1)}, bf16[2,16,2,2,7168]{4,1,3,2,0:T(8,128)(2,1)S(1)}, u32[]{:S(2)}, u32[]{:S(2)}) %collective-permute-start.2) | collective-permute-done | bytes 1835040 | tf_op jit(solution)/shard_map/ppermute | solution.py:34
  75.5 0.4 convert_add_fusion
  76.0 0.1 fusion.9
  76.1 0.0 copy-start.1
  76.1 0.0 copy-start
  76.1 0.7 collective-permute-start.3
  76.8 21.8 %collective-permute-done.3 = bf16[16,2,2,7168]{3,0,2,1:T(8,128)(2,1)S(1)} collective-permute-done((bf16[16,2,2,7168]{3,0,2,1:T(8,128)(2,1)S(1)}, bf16[16,2,2,7168]{3,0,2,1:T(8,128)(2,1)S(1)}, u32[]{:S(2)}, u32[]{:S(2)}) %collective-permute-start.3) | collective-permute-done | bytes 917536 | tf_op jit(solution)/shard_map/ppermute | solution.py:34
  98.6 0.2 fusion.8
  98.8 1.9 %copy.22 = bf16[16,2,2,7168]{3,2,1,0:T(2,128)(2,1)} copy(bf16[16,2,2,7168]{3,0,2,1:T(8,128)(2,1)S(1)} %fusion.8) | data formatting | bytes 1835008 | tf_op jit(solution)/shard_map/convert_element_type | solution.py:72
  100.6 4.9 %all-to-all-start.1 = ((bf16[16,2,2,7168]{3,2,1,0:T(2,128)(2,1)}), bf16[16,2,2,7168]{3,2,1,0:T(2,128)(2,1)S(1)}, u32[]{:S(2)}, u32[]{:S(2)}) async-start(bf16[16,2,2,7168]{3,2,1,0:T(2,128)(2,1)} %copy.22), calls=%async_computation.1 | async-start | bytes 1835008 | tf_op jit(solution)/shard_map/all_to_all | solution.py:71
  105.5 0.1 sub.13
  105.6 0.1 sub.11
  105.7 0.0 copy-done.1
  105.7 0.1 convert_reduce_fusion.1
  105.8 0.1 bitcast_divide_fusion.1
  105.9 0.0 copy-done
  105.9 0.1 select_reduce_fusion
  106.0 26.3 %all-to-all-done.1 = bf16[16,2,2,7168]{3,2,1,0:T(2,128)(2,1)S(1)} async-done(((bf16[16,2,2,7168]{3,2,1,0:T(2,128)(2,1)}), bf16[16,2,2,7168]{3,2,1,0:T(2,128)(2,1)S(1)}, u32[]{:S(2)}, u32[]{:S(2)}) %all-to-all-start.1) | async-done | bytes 917536 | tf_op jit(solution)/shard_map/all_to_all | solution.py:71
  132.3 0.6 fusion.23
  132.9 0.2 reshape_squeeze.11
  133.1 0.2 reshape_squeeze.12
  133.3 0.3 fusion
  133.6 0.3 fusion.1
  133.9 0.7 pad_maximum_fusion.5
  (5 shorter events, 0.1 us)
Async XLA Ops:
  41.1 25.1 %copy-start.2 = (bf16[1,7168,256]{2,1,0:T(8,128)(2,1)S(1)}, bf16[1,7168,256]{2,1,0:T(8,128)(2,1)}, u32[]{:S(2)}) copy-start(bf16[1,7168,256]{2,1,0:T(8,128)(2,1)} %param.9) | copy-start | bytes 11010052
  41.4 20.7 %collective-permute-start = (bf16[16,2,2,7168]{3,0,2,1:T(8,128)(2,1)S(1)}, bf16[16,2,2,7168]{3,0,2,1:T(8,128)(2,1)S(1)}, u32[]{:S(2)}, u32[]{:S(2)}) collective-permute-start(bf16[16,2,2,7168]{3,0,2,1:T(8,128)(2,1)S(1)} %copy.28), channel_id=1, source_target_pairs={{0,2},{2,0},{1,3},{3,1},{4,6},{6,4},{5,7},{7,5},{8,10},{10,8},{9,1... | collective-permute-start | bytes 2752520 | tf_op jit(solution)/shard_map/ppermute | solution.py:34
  62.4 3.9 %collective-permute-start.1 = (bf16[2,16,2,2,7168]{4,1,3,2,0:T(8,128)(2,1)S(1)}, bf16[2,16,2,2,7168]{4,1,3,2,0:T(8,128)(2,1)S(1)}, u32[]{:S(2)}, u32[]{:S(2)}) collective-permute-start(bf16[2,16,2,2,7168]{4,1,3,2,0:T(8,128)(2,1)S(1)} %get-tuple-element.8), channel_id=1, source_target_pairs={{0,1},{1,0},{2,3},{3,2},{4,5},{5,4},{6,7},{7,6},{8,9},{9,8},{10,11... | collective-permute-start | bytes 5505032 | tf_op jit(solution)/shard_map/ppermute | solution.py:34
  66.2 2.0 %copy-start.3 = (bf16[1,7168,256]{2,1,0:T(8,128)(2,1)S(1)}, bf16[1,7168,256]{2,1,0:T(8,128)(2,1)}, u32[]{:S(2)}) copy-start(bf16[1,7168,256]{2,1,0:T(8,128)(2,1)} %param.10) | copy-start | bytes 11010052
  68.3 2.0 %copy-start.4 = (bf16[1,256,7168]{2,1,0:T(8,128)(2,1)S(1)}, bf16[1,256,7168]{2,1,0:T(8,128)(2,1)}, u32[]{:S(2)}) copy-start(bf16[1,256,7168]{2,1,0:T(8,128)(2,1)} %param.11) | copy-start | bytes 11010052
  71.6 3.9 %collective-permute-start.2 = (bf16[2,16,2,2,7168]{4,1,3,2,0:T(8,128)(2,1)S(1)}, bf16[2,16,2,2,7168]{4,1,3,2,0:T(8,128)(2,1)S(1)}, u32[]{:S(2)}, u32[]{:S(2)}) collective-permute-start(bf16[2,16,2,2,7168]{4,1,3,2,0:T(8,128)(2,1)S(1)} %slice_bitcast_fusion.1), channel_id=1, source_target_pairs={{0,1},{1,0},{2,3},{3,2},{4,5},{5,4},{6,7},{7,6},{8,9},{9,8},{10,11... | collective-permute-start | bytes 5505032 | tf_op jit(solution)/shard_map/ppermute | solution.py:34
  76.1 29.6 %copy-start.1 = (s32[2,2,8]{2,1,0:T(2,128)S(1)}, s32[2,2,8]{2,1,0:T(2,128)}, u32[]{:S(2)}) copy-start(s32[2,2,8]{2,1,0:T(2,128)} %param.8) | copy-start | bytes 388
  76.1 29.9 %copy-start = (s32[2,2,8]{2,1,0:T(2,128)S(1)}, s32[2,2,8]{2,1,0:T(2,128)}, u32[]{:S(2)}) copy-start(s32[2,2,8]{2,1,0:T(2,128)} %param.7) | copy-start | bytes 388
  76.1 22.5 %collective-permute-start.3 = (bf16[16,2,2,7168]{3,0,2,1:T(8,128)(2,1)S(1)}, bf16[16,2,2,7168]{3,0,2,1:T(8,128)(2,1)S(1)}, u32[]{:S(2)}, u32[]{:S(2)}) collective-permute-start(bf16[16,2,2,7168]{3,0,2,1:T(8,128)(2,1)S(1)} %fusion.9), channel_id=1, source_target_pairs={{0,2},{2,0},{1,3},{3,1},{4,6},{6,4},{5,7},{7,5},{8,10},{10,8},{9,1... | collective-permute-start | bytes 2752520 | tf_op jit(solution)/shard_map/ppermute | solution.py:34
  100.6 31.6 %all-to-all-start.1 = ((bf16[16,2,2,7168]{3,2,1,0:T(2,128)(2,1)}), bf16[16,2,2,7168]{3,2,1,0:T(2,128)(2,1)S(1)}, u32[]{:S(2)}, u32[]{:S(2)}) async-start(bf16[16,2,2,7168]{3,2,1,0:T(2,128)(2,1)} %copy.22), calls=%async_computation.1 | async-start | bytes 1835008 | tf_op jit(solution)/shard_map/all_to_all | solution.py:71

commit v8 on v7

--- a/solution.py
+++ b/solution.py
@@ -10,23 +10,20 @@
 CROSS = ("x", "zh")
 
 
-def route_tables(step_ids, step_codes, experts_all, capacity):
-    row_count, top_count = step_ids.shape
-    flat_ids = step_ids.reshape(-1)
-    onehot = (flat_ids[:, None] == jnp.arange(experts_all, dtype=jnp.int32)[None, :]).astype(
-        jnp.int32
+def route_tables(expert_ids, gate_codes, experts_all, capacity):
+    step_count, row_count, top_count = expert_ids.shape
+    flat = expert_ids.reshape(step_count, -1)
+    order = jnp.arange(row_count * top_count, dtype=jnp.int32)
+    earlier = order[None, :] < order[:, None]
+    same = flat[:, :, None] == flat[:, None, :]
+    slot_rank = jnp.sum(same & earlier, -1).reshape(expert_ids.shape)
+    hit = (expert_ids[..., None, None] == jnp.arange(experts_all, dtype=jnp.int32)[:, None]) & (
+        slot_rank[..., None, None] == jnp.arange(capacity, dtype=jnp.int32)
     )
-    slot_rank = jnp.sum(jnp.cumsum(onehot, 0) * onehot, 1) - 1
-    slot_index = flat_ids * capacity + slot_rank
-    placement = slot_index[:, None] == jnp.arange(experts_all * capacity, dtype=jnp.int32)[None, :]
-    codes = step_codes.astype(jnp.float32)
-    gate_weight = codes / jnp.sum(codes, 1, keepdims=True)
-    mix_table = jnp.sum(
-        (placement.astype(jnp.float32) * gate_weight.reshape(-1)[:, None]).reshape(
-            row_count, top_count, -1
-        ),
-        1,
-    )
+    codes = gate_codes.astype(jnp.float32)
+    gate_weight = codes / jnp.sum(codes, -1, keepdims=True)
+    placement = jnp.sum(hit.astype(jnp.int32), 2)
+    mix_table = jnp.sum(jnp.where(hit, gate_weight[..., None, None], 0.0), 2)
     return (placement, mix_table)
 
 
@@ -39,22 +36,13 @@
     top_count = expert_ids.shape[2]
     experts_all = lax.axis_size(CROSS)
     capacity = min(row_count, max(2, 2 * row_count * top_count // experts_all))
-    send_rows = []
-    mix_tables = []
-    for step in range(step_count):
-        placement, mix_table = route_tables(
-            expert_ids[step], gate_codes[step], experts_all, capacity
-        )
-        repeated = jnp.repeat(tokens[step], top_count, 0)
-        slots = jnp.einsum(
-            "as,ad->sd",
-            placement.astype(jnp.bfloat16),
-            repeated,
-            preferred_element_type=jnp.float32,
-        ).astype(jnp.bfloat16)
-        send_rows.append(slots.reshape(experts_all, 1, capacity, width))
-        mix_tables.append(mix_table)
-    slots = jnp.concatenate(send_rows, 1)
+    placement, mix_table = route_tables(expert_ids, gate_codes, experts_all, capacity)
+    slots = jnp.einsum(
+        "srec,srd->escd",
+        placement.astype(jnp.bfloat16),
+        tokens,
+        preferred_element_type=jnp.float32,
+    ).astype(jnp.bfloat16)
     received = lax.all_to_all(slots, CROSS, split_axis=0, concat_axis=0, tiled=True)
     received = jnp.stack([received, swap(received, "zl")], 0)
     received = jnp.stack([received, swap(received, "c")], 0)
@@ -74,7 +62,7 @@
     results = []
     for step in range(step_count):
         combined = jnp.dot(
-            mix_tables[step],
+            mix_table[step].reshape(row_count, -1),
             returned[:, step].reshape(-1, width),
             precision=lax.Precision.HIGHEST,
             preferred_element_type=jnp.float32,

time: 135 us -> 134 us (level)
  no operation moved by 1% of the time
where the time goes in v8:
time: 134 us; the launch traced here: 133 us
  waiting for transfers between devices  75 us (56%)
  blocking collectives  36.4 us (27%)
  local copies, waits for them, and re-layouts  7.36 us (5%)
  starting transfers between devices  7.1 us (5%)
  matrix products  4.47 us (3%)
  other arithmetic  2.82 us (2%)
    ppermute x4, waiting for transfers between devices, swap(): return lax.ppermute(value, axis, [(0, 1), (1, 0)])  48.8 us
    all_to_all x1, blocking collectives, body(): lax.all_to_all(slots, CROSS, split_axis=0, concat_axis=0, tiled=True)  36.4 us
    all_to_all x1, waiting for transfers between devices, body(): lax.all_to_all(expert_out.astype(jnp.bfloat16), CROSS, split_axis=0, conc...  26.2 us
    all_to_all x1, starting transfers between devices, body(): lax.all_to_all(expert_out.astype(jnp.bfloat16), CROSS, split_axis=0, conc...  4.92 us
  transfers between devices with their start and end apart: 5, of which 5 were waited for; matrix products, arithmetic and copies ran while one was open for 0% of the time, Pallas kernels for 0%

profile of v8, /device:TPU:32, one launch (start us, length us, event | category | flops | bytes accessed | tf_op | source)
XLA Modules:
  0.0 133.3 jit_solution(11222748990491615962)
XLA Ops:
  0.0 0.0 copy-start
  0.0 0.8 eq.56
  0.8 0.8 iota_compare_fusion
  1.5 0.2 convert_reduce_fusion
  1.7 0.1 eq.60
  1.8 0.1 fusion.14
  1.9 0.0 copy-done
  1.9 0.5 fusion
  2.4 0.9 copy.15
  3.4 36.4 %all_to_all.10 = bf16[16,2,2,7168]{3,2,1,0:T(2,128)(2,1)S(1)} all-to-all(bf16[16,2,2,7168]{3,2,1,0:T(2,128)(2,1)S(1)} %copy.15), channel_id=1, replica_groups=mesh['dp'=4,'x'=4,'zh'=4,'zl'=2,'c'=2] {'x','zh'}, dimensions={0} | all-to-all | bytes 1835008 | tf_op jit(solution)/shard_map/all_to_all | solution.py:46
  39.8 0.0 copy-start.1
  39.8 0.3 copy.28
  40.1 1.1 collective-permute-start
  41.2 19.6 %collective-permute-done = bf16[16,2,2,7168]{3,0,2,1:T(8,128)(2,1)S(1)} collective-permute-done((bf16[16,2,2,7168]{3,0,2,1:T(8,128)(2,1)S(1)}, bf16[16,2,2,7168]{3,0,2,1:T(8,128)(2,1)S(1)}, u32[]{:S(2)}, u32[]{:S(2)}) %collective-permute-start) | collective-permute-done | bytes 917536 | tf_op jit(solution)/shard_map/ppermute | solution.py:31
  60.8 0.2 fusion.24
  61.1 0.1 collective-permute-start.1
  61.2 3.8 %collective-permute-done.1 = bf16[2,16,2,2,7168]{4,1,3,2,0:T(8,128)(2,1)S(1)} collective-permute-done((bf16[2,16,2,2,7168]{4,1,3,2,0:T(8,128)(2,1)S(1)}, bf16[2,16,2,2,7168]{4,1,3,2,0:T(8,128)(2,1)S(1)}, u32[]{:S(2)}, u32[]{:S(2)}) %collective-permute-start.1) | collective-permute-done | bytes 1835040 | tf_op jit(solution)/shard_map/ppermute | solution.py:31
  64.9 0.0 copy-done.1
  64.9 0.0 copy-start.2
  64.9 1.1 fusion.4
  66.1 0.9 copy-done.2
  67.0 0.0 copy-start.3
  67.0 1.1 fusion.6
  68.1 0.9 copy-done.3
  69.0 1.1 convolution_convert_fusion
  70.2 0.2 slice_bitcast_fusion.1
  70.3 0.2 collective-permute-start.2
  70.5 3.6 %collective-permute-done.2 = bf16[2,16,2,2,7168]{4,1,3,2,0:T(8,128)(2,1)S(1)} collective-permute-done((bf16[2,16,2,2,7168]{4,1,3,2,0:T(8,128)(2,1)S(1)}, bf16[2,16,2,2,7168]{4,1,3,2,0:T(8,128)(2,1)S(1)}, u32[]{:S(2)}, u32[]{:S(2)}) %collective-permute-start.2) | collective-permute-done | bytes 1835040 | tf_op jit(solution)/shard_map/ppermute | solution.py:31
  74.2 0.4 convert_add_fusion
  74.7 0.1 fusion.10
  74.8 0.0 copy-start.4
  74.8 0.8 collective-permute-start.3
  75.5 21.7 %collective-permute-done.3 = bf16[16,2,2,7168]{3,0,2,1:T(8,128)(2,1)S(1)} collective-permute-done((bf16[16,2,2,7168]{3,0,2,1:T(8,128)(2,1)S(1)}, bf16[16,2,2,7168]{3,0,2,1:T(8,128)(2,1)S(1)}, u32[]{:S(2)}, u32[]{:S(2)}) %collective-permute-start.3) | collective-permute-done | bytes 917536 | tf_op jit(solution)/shard_map/ppermute | solution.py:31
  97.2 0.2 fusion.9
  97.4 1.9 %copy.18 = bf16[16,2,2,7168]{3,2,1,0:T(2,128)(2,1)} copy(bf16[16,2,2,7168]{3,0,2,1:T(8,128)(2,1)S(1)} %fusion.9) | data formatting | bytes 1835008 | tf_op jit(solution)/shard_map/convert_element_type | solution.py:60
  99.3 4.9 %all-to-all-start.1 = ((bf16[16,2,2,7168]{3,2,1,0:T(2,128)(2,1)}), bf16[16,2,2,7168]{3,2,1,0:T(2,128)(2,1)S(1)}, u32[]{:S(2)}, u32[]{:S(2)}) async-start(bf16[16,2,2,7168]{3,2,1,0:T(2,128)(2,1)} %copy.18), calls=%async_computation.1 | async-start | bytes 1835008 | tf_op jit(solution)/shard_map/all_to_all | solution.py:59
  104.2 0.0 copy-done.4
  104.2 0.1 convert_divide_fusion
  104.3 0.1 fusion.13
  104.4 0.1 copy.13
  104.5 0.1 reshape_squeeze.12
  104.6 0.1 copy.19
  104.7 0.1 reshape_squeeze.14
  104.8 26.2 %all-to-all-done.1 = bf16[16,2,2,7168]{3,2,1,0:T(2,128)(2,1)S(1)} async-done(((bf16[16,2,2,7168]{3,2,1,0:T(2,128)(2,1)}), bf16[16,2,2,7168]{3,2,1,0:T(2,128)(2,1)S(1)}, u32[]{:S(2)}, u32[]{:S(2)}) %all-to-all-start.1) | async-done | bytes 917536 | tf_op jit(solution)/shard_map/all_to_all | solution.py:59
  131.0 0.6 fusion.25
  131.6 0.2 reshape_squeeze.13
  131.8 0.2 reshape_squeeze.15
  132.0 0.3 fusion.1
  132.3 0.3 fusion.2
  132.6 0.7 pad_maximum_fusion.4
  (4 shorter events, 0.0 us)
Async XLA Ops:
  0.0 1.9 %copy-start = (bf16[2,2,7168]{2,1,0:T(2,128)(2,1)S(1)}, bf16[2,2,7168]{2,1,0:T(2,128)(2,1)}, u32[]{:S(2)}) copy-start(bf16[2,2,7168]{2,1,0:T(2,128)(2,1)} %param.6) | copy-start | bytes 172036
  39.8 25.1 %copy-start.1 = (bf16[1,7168,256]{2,1,0:T(8,128)(2,1)S(1)}, bf16[1,7168,256]{2,1,0:T(8,128)(2,1)}, u32[]{:S(2)}) copy-start(bf16[1,7168,256]{2,1,0:T(8,128)(2,1)} %param.10) | copy-start | bytes 11010052
  40.1 20.7 %collective-permute-start = (bf16[16,2,2,7168]{3,0,2,1:T(8,128)(2,1)S(1)}, bf16[16,2,2,7168]{3,0,2,1:T(8,128)(2,1)S(1)}, u32[]{:S(2)}, u32[]{:S(2)}) collective-permute-start(bf16[16,2,2,7168]{3,0,2,1:T(8,128)(2,1)S(1)} %copy.28), channel_id=1, source_target_pairs={{0,2},{2,0},{1,3},{3,1},{4,6},{6,4},{5,7},{7,5},{8,10},{10,8},{9,1... | collective-permute-start | bytes 2752520 | tf_op jit(solution)/shard_map/ppermute | solution.py:31
  61.1 3.9 %collective-permute-start.1 = (bf16[2,16,2,2,7168]{4,1,3,2,0:T(8,128)(2,1)S(1)}, bf16[2,16,2,2,7168]{4,1,3,2,0:T(8,128)(2,1)S(1)}, u32[]{:S(2)}, u32[]{:S(2)}) collective-permute-start(bf16[2,16,2,2,7168]{4,1,3,2,0:T(8,128)(2,1)S(1)} %get-tuple-element.6), channel_id=1, source_target_pairs={{0,1},{1,0},{2,3},{3,2},{4,5},{5,4},{6,7},{7,6},{8,9},{9,8},{10,11... | collective-permute-start | bytes 5505032 | tf_op jit(solution)/shard_map/ppermute | solution.py:31
  64.9 2.0 %copy-start.2 = (bf16[1,7168,256]{2,1,0:T(8,128)(2,1)S(1)}, bf16[1,7168,256]{2,1,0:T(8,128)(2,1)}, u32[]{:S(2)}) copy-start(bf16[1,7168,256]{2,1,0:T(8,128)(2,1)} %param.9) | copy-start | bytes 11010052
  67.0 2.0 %copy-start.3 = (bf16[1,256,7168]{2,1,0:T(8,128)(2,1)S(1)}, bf16[1,256,7168]{2,1,0:T(8,128)(2,1)}, u32[]{:S(2)}) copy-start(bf16[1,256,7168]{2,1,0:T(8,128)(2,1)} %param.11) | copy-start | bytes 11010052
  70.3 3.9 %collective-permute-start.2 = (bf16[2,16,2,2,7168]{4,1,3,2,0:T(8,128)(2,1)S(1)}, bf16[2,16,2,2,7168]{4,1,3,2,0:T(8,128)(2,1)S(1)}, u32[]{:S(2)}, u32[]{:S(2)}) collective-permute-start(bf16[2,16,2,2,7168]{4,1,3,2,0:T(8,128)(2,1)S(1)} %slice_bitcast_fusion.1), channel_id=1, source_target_pairs={{0,1},{1,0},{2,3},{3,2},{4,5},{5,4},{6,7},{7,6},{8,9},{9,8},{10,11... | collective-permute-start | bytes 5505032 | tf_op jit(solution)/shard_map/ppermute | solution.py:31
  74.8 29.5 %copy-start.4 = (s32[2,2,8]{2,1,0:T(2,128)S(1)}, s32[2,2,8]{2,1,0:T(2,128)}, u32[]{:S(2)}) copy-start(s32[2,2,8]{2,1,0:T(2,128)} %param.8) | copy-start | bytes 388
  74.8 22.5 %collective-permute-start.3 = (bf16[16,2,2,7168]{3,0,2,1:T(8,128)(2,1)S(1)}, bf16[16,2,2,7168]{3,0,2,1:T(8,128)(2,1)S(1)}, u32[]{:S(2)}, u32[]{:S(2)}) collective-permute-start(bf16[16,2,2,7168]{3,0,2,1:T(8,128)(2,1)S(1)} %fusion.10), channel_id=1, source_target_pairs={{0,2},{2,0},{1,3},{3,1},{4,6},{6,4},{5,7},{7,5},{8,10},{10,8},{9,1... | collective-permute-start | bytes 2752520 | tf_op jit(solution)/shard_map/ppermute | solution.py:31
  99.3 31.7 %all-to-all-start.1 = ((bf16[16,2,2,7168]{3,2,1,0:T(2,128)(2,1)}), bf16[16,2,2,7168]{3,2,1,0:T(2,128)(2,1)S(1)}, u32[]{:S(2)}, u32[]{:S(2)}) async-start(bf16[16,2,2,7168]{3,2,1,0:T(2,128)(2,1)} %copy.18), calls=%async_computation.1 | async-start | bytes 1835008 | tf_op jit(solution)/shard_map/all_to_all | solution.py:59

commit v9 on v8

--- a/solution.py
+++ b/solution.py
@@ -59,16 +59,14 @@
     returned = lax.all_to_all(
         expert_out.astype(jnp.bfloat16), CROSS, split_axis=0, concat_axis=0, tiled=True
     ).astype(jnp.float32)
-    results = []
-    for step in range(step_count):
-        combined = jnp.dot(
-            mix_table[step].reshape(row_count, -1),
-            returned[:, step].reshape(-1, width),
-            precision=lax.Precision.HIGHEST,
-            preferred_element_type=jnp.float32,
-        )
-        results.append(combined.astype(jnp.bfloat16))
-    return jnp.stack(results, 0)
+    mixed = jnp.einsum(
+        "srec,escd->srd",
+        mix_table,
+        returned,
+        precision=lax.Precision.HIGHEST,
+        preferred_element_type=jnp.float32,
+    )
+    return mixed.astype(jnp.bfloat16)
 
 
 def solution(mesh):

time: 134 us -> 133 us (level)
  no operation moved by 1% of the time
where the time goes in v9:
time: 133 us; the launch traced here: 132 us
  waiting for transfers between devices  75.3 us (57%)
  blocking collectives  36.4 us (27%)
  starting transfers between devices  7.1 us (5%)
  local copies, waits for them, and re-layouts  6.04 us (5%)
  matrix products  5.17 us (4%)
  other arithmetic  2.2 us (2%)
    ppermute x4, waiting for transfers between devices, swap(): return lax.ppermute(value, axis, [(0, 1), (1, 0)])  48.8 us
    all_to_all x1, blocking collectives, body(): lax.all_to_all(slots, CROSS, split_axis=0, concat_axis=0, tiled=True)  36.4 us
    all_to_all x1, waiting for transfers between devices, body(): lax.all_to_all(expert_out.astype(jnp.bfloat16), CROSS, split_axis=0, conc...  26.5 us
    all_to_all x1, starting transfers between devices, body(): lax.all_to_all(expert_out.astype(jnp.bfloat16), CROSS, split_axis=0, conc...  4.92 us
  transfers between devices with their start and end apart: 5, of which 5 were waited for; matrix products, arithmetic and copies ran while one was open for 0% of the time, Pallas kernels for 0%

profile of v9, /device:TPU:32, one launch (start us, length us, event | category | flops | bytes accessed | tf_op | source)
XLA Modules:
  0.0 132.3 jit_solution(14633359861920129550)
XLA Ops:
  0.0 0.0 copy-start
  0.0 0.8 eq.56
  0.8 0.8 iota_compare_fusion
  1.5 0.2 convert_reduce_fusion
  1.7 0.1 eq.60
  1.8 0.1 fusion.14
  1.9 0.0 copy-done
  1.9 0.5 fusion
  2.4 0.9 copy.13
  3.4 36.4 %all_to_all.10 = bf16[16,2,2,7168]{3,2,1,0:T(2,128)(2,1)S(1)} all-to-all(bf16[16,2,2,7168]{3,2,1,0:T(2,128)(2,1)S(1)} %copy.13), channel_id=1, replica_groups=mesh['dp'=4,'x'=4,'zh'=4,'zl'=2,'c'=2] {'x','zh'}, dimensions={0} | all-to-all | bytes 1835008 | tf_op jit(solution)/shard_map/all_to_all | solution.py:46
  39.8 0.0 copy-start.2
  39.8 0.3 copy.32
  40.1 1.1 collective-permute-start
  41.2 19.6 %collective-permute-done = bf16[16,2,2,7168]{3,0,2,1:T(8,128)(2,1)S(1)} collective-permute-done((bf16[16,2,2,7168]{3,0,2,1:T(8,128)(2,1)S(1)}, bf16[16,2,2,7168]{3,0,2,1:T(8,128)(2,1)S(1)}, u32[]{:S(2)}, u32[]{:S(2)}) %collective-permute-start) | collective-permute-done | bytes 917536 | tf_op jit(solution)/shard_map/ppermute | solution.py:31
  60.8 0.2 fusion.20
  61.1 0.1 collective-permute-start.1
  61.2 3.8 %collective-permute-done.1 = bf16[2,16,2,2,7168]{4,1,3,2,0:T(8,128)(2,1)S(1)} collective-permute-done((bf16[2,16,2,2,7168]{4,1,3,2,0:T(8,128)(2,1)S(1)}, bf16[2,16,2,2,7168]{4,1,3,2,0:T(8,128)(2,1)S(1)}, u32[]{:S(2)}, u32[]{:S(2)}) %collective-permute-start.1) | collective-permute-done | bytes 1835040 | tf_op jit(solution)/shard_map/ppermute | solution.py:31
  64.9 0.0 copy-done.2
  64.9 0.0 copy-start.3
  64.9 1.1 fusion.3
  66.1 0.9 copy-done.3
  67.0 0.0 copy-start.4
  67.0 1.1 fusion.5
  68.1 0.9 copy-done.4
  69.0 1.1 convolution_convert_fusion
  70.2 0.2 slice_bitcast_fusion.1
  70.3 0.2 collective-permute-start.2
  70.5 3.6 %collective-permute-done.2 = bf16[2,16,2,2,7168]{4,1,3,2,0:T(8,128)(2,1)S(1)} collective-permute-done((bf16[2,16,2,2,7168]{4,1,3,2,0:T(8,128)(2,1)S(1)}, bf16[2,16,2,2,7168]{4,1,3,2,0:T(8,128)(2,1)S(1)}, u32[]{:S(2)}, u32[]{:S(2)}) %collective-permute-start.2) | collective-permute-done | bytes 1835040 | tf_op jit(solution)/shard_map/ppermute | solution.py:31
  74.2 0.4 convert_add_fusion
  74.7 0.1 fusion.9
  74.8 0.0 copy-start.1
  74.8 0.8 collective-permute-start.3
  75.5 21.7 %collective-permute-done.3 = bf16[16,2,2,7168]{3,0,2,1:T(8,128)(2,1)S(1)} collective-permute-done((bf16[16,2,2,7168]{3,0,2,1:T(8,128)(2,1)S(1)}, bf16[16,2,2,7168]{3,0,2,1:T(8,128)(2,1)S(1)}, u32[]{:S(2)}, u32[]{:S(2)}) %collective-permute-start.3) | collective-permute-done | bytes 917536 | tf_op jit(solution)/shard_map/ppermute | solution.py:31
  97.2 0.2 fusion.8
  97.4 1.9 %copy.16 = bf16[16,2,2,7168]{3,2,1,0:T(2,128)(2,1)} copy(bf16[16,2,2,7168]{3,0,2,1:T(8,128)(2,1)S(1)} %fusion.8) | data formatting | bytes 1835008 | tf_op jit(solution)/shard_map/convert_element_type | solution.py:60
  99.3 4.9 %all-to-all-start.1 = ((bf16[16,2,2,7168]{3,2,1,0:T(2,128)(2,1)}), bf16[16,2,2,7168]{3,2,1,0:T(2,128)(2,1)S(1)}, u32[]{:S(2)}, u32[]{:S(2)}) async-start(bf16[16,2,2,7168]{3,2,1,0:T(2,128)(2,1)} %copy.16), calls=%async_computation.1 | async-start | bytes 1835008 | tf_op jit(solution)/shard_map/all_to_all | solution.py:59
  104.2 0.0 copy-done.1
  104.3 0.1 convert_reduce_fusion.1
  104.3 0.1 convert_divide_fusion
  104.4 0.1 fusion.13
  104.5 26.5 %all-to-all-done.1 = bf16[16,2,2,7168]{3,2,1,0:T(2,128)(2,1)S(1)} async-done(((bf16[16,2,2,7168]{3,2,1,0:T(2,128)(2,1)}), bf16[16,2,2,7168]{3,2,1,0:T(2,128)(2,1)S(1)}, u32[]{:S(2)}, u32[]{:S(2)}) %all-to-all-start.1) | async-done | bytes 917536 | tf_op jit(solution)/shard_map/all_to_all | solution.py:59
  131.0 1.3 fusion.1
  (3 shorter events, 0.0 us)
Async XLA Ops:
  0.0 1.9 %copy-start = (bf16[2,2,7168]{2,1,0:T(2,128)(2,1)S(1)}, bf16[2,2,7168]{2,1,0:T(2,128)(2,1)}, u32[]{:S(2)}) copy-start(bf16[2,2,7168]{2,1,0:T(2,128)(2,1)} %param.6) | copy-start | bytes 172036
  39.8 25.1 %copy-start.2 = (bf16[1,7168,256]{2,1,0:T(8,128)(2,1)S(1)}, bf16[1,7168,256]{2,1,0:T(8,128)(2,1)}, u32[]{:S(2)}) copy-start(bf16[1,7168,256]{2,1,0:T(8,128)(2,1)} %param.10) | copy-start | bytes 11010052
  40.1 20.7 %collective-permute-start = (bf16[16,2,2,7168]{3,0,2,1:T(8,128)(2,1)S(1)}, bf16[16,2,2,7168]{3,0,2,1:T(8,128)(2,1)S(1)}, u32[]{:S(2)}, u32[]{:S(2)}) collective-permute-start(bf16[16,2,2,7168]{3,0,2,1:T(8,128)(2,1)S(1)} %copy.32), channel_id=1, source_target_pairs={{0,2},{2,0},{1,3},{3,1},{4,6},{6,4},{5,7},{7,5},{8,10},{10,8},{9,1... | collective-permute-start | bytes 2752520 | tf_op jit(solution)/shard_map/ppermute | solution.py:31
  61.1 3.9 %collective-permute-start.1 = (bf16[2,16,2,2,7168]{4,1,3,2,0:T(8,128)(2,1)S(1)}, bf16[2,16,2,2,7168]{4,1,3,2,0:T(8,128)(2,1)S(1)}, u32[]{:S(2)}, u32[]{:S(2)}) collective-permute-start(bf16[2,16,2,2,7168]{4,1,3,2,0:T(8,128)(2,1)S(1)} %get-tuple-element.6), channel_id=1, source_target_pairs={{0,1},{1,0},{2,3},{3,2},{4,5},{5,4},{6,7},{7,6},{8,9},{9,8},{10,11... | collective-permute-start | bytes 5505032 | tf_op jit(solution)/shard_map/ppermute | solution.py:31
  64.9 2.0 %copy-start.3 = (bf16[1,7168,256]{2,1,0:T(8,128)(2,1)S(1)}, bf16[1,7168,256]{2,1,0:T(8,128)(2,1)}, u32[]{:S(2)}) copy-start(bf16[1,7168,256]{2,1,0:T(8,128)(2,1)} %param.9) | copy-start | bytes 11010052
  67.0 2.0 %copy-start.4 = (bf16[1,256,7168]{2,1,0:T(8,128)(2,1)S(1)}, bf16[1,256,7168]{2,1,0:T(8,128)(2,1)}, u32[]{:S(2)}) copy-start(bf16[1,256,7168]{2,1,0:T(8,128)(2,1)} %param.11) | copy-start | bytes 11010052
  70.3 3.9 %collective-permute-start.2 = (bf16[2,16,2,2,7168]{4,1,3,2,0:T(8,128)(2,1)S(1)}, bf16[2,16,2,2,7168]{4,1,3,2,0:T(8,128)(2,1)S(1)}, u32[]{:S(2)}, u32[]{:S(2)}) collective-permute-start(bf16[2,16,2,2,7168]{4,1,3,2,0:T(8,128)(2,1)S(1)} %slice_bitcast_fusion.1), channel_id=1, source_target_pairs={{0,1},{1,0},{2,3},{3,2},{4,5},{5,4},{6,7},{7,6},{8,9},{9,8},{10,11... | collective-permute-start | bytes 5505032 | tf_op jit(solution)/shard_map/ppermute | solution.py:31
  74.8 29.5 %copy-start.1 = (s32[2,2,8]{2,1,0:T(2,128)S(1)}, s32[2,2,8]{2,1,0:T(2,128)}, u32[]{:S(2)}) copy-start(s32[2,2,8]{2,1,0:T(2,128)} %param.8) | copy-start | bytes 388
  74.8 22.5 %collective-permute-start.3 = (bf16[16,2,2,7168]{3,0,2,1:T(8,128)(2,1)S(1)}, bf16[16,2,2,7168]{3,0,2,1:T(8,128)(2,1)S(1)}, u32[]{:S(2)}, u32[]{:S(2)}) collective-permute-start(bf16[16,2,2,7168]{3,0,2,1:T(8,128)(2,1)S(1)} %fusion.9), channel_id=1, source_target_pairs={{0,2},{2,0},{1,3},{3,1},{4,6},{6,4},{5,7},{7,5},{8,10},{10,8},{9,1... | collective-permute-start | bytes 2752520 | tf_op jit(solution)/shard_map/ppermute | solution.py:31
  99.3 31.7 %all-to-all-start.1 = ((bf16[16,2,2,7168]{3,2,1,0:T(2,128)(2,1)}), bf16[16,2,2,7168]{3,2,1,0:T(2,128)(2,1)S(1)}, u32[]{:S(2)}, u32[]{:S(2)}) async-start(bf16[16,2,2,7168]{3,2,1,0:T(2,128)(2,1)} %copy.16), calls=%async_computation.1 | async-start | bytes 1835008 | tf_op jit(solution)/shard_map/all_to_all | solution.py:59

commit v10 on v9

--- a/solution.py
+++ b/solution.py
@@ -44,8 +44,11 @@
         preferred_element_type=jnp.float32,
     ).astype(jnp.bfloat16)
     received = lax.all_to_all(slots, CROSS, split_axis=0, concat_axis=0, tiled=True)
-    received = jnp.stack([received, swap(received, "zl")], 0)
-    received = jnp.stack([received, swap(received, "c")], 0)
+    from_chip = swap(received, "zl")
+    received = jnp.stack(
+        [jnp.stack([received, from_chip], 0), jnp.stack([swap(received, "c"), swap(from_chip, "c")], 0)],
+        0,
+    )
     gate_act = jnp.einsum(
         "...cd,dh->...ch", received, w_gate[0], preferred_element_type=jnp.float32
     )
@@ -54,8 +57,10 @@
     partial_out = jnp.einsum(
         "...ch,hd->...cd", hidden, w_down[0], preferred_element_type=jnp.float32
     ).astype(jnp.bfloat16)
-    chip_sum = partial_out[0].astype(jnp.float32) + swap(partial_out[1], "c").astype(jnp.float32)
-    expert_out = chip_sum[0] + swap(chip_sum[1].astype(jnp.bfloat16), "zl").astype(jnp.float32)
+    leaving = partial_out[0, 1].astype(jnp.float32) + swap(partial_out[1, 1], "c").astype(jnp.float32)
+    arriving = swap(leaving.astype(jnp.bfloat16), "zl").astype(jnp.float32)
+    staying = partial_out[0, 0].astype(jnp.float32) + swap(partial_out[1, 0], "c").astype(jnp.float32)
+    expert_out = staying + arriving
     returned = lax.all_to_all(
         expert_out.astype(jnp.bfloat16), CROSS, split_axis=0, concat_axis=0, tiled=True
     ).astype(jnp.float32)

time: 133 us -> 130 us (0.977)
  waiting for transfers between devices: 75.3 us -> 72.1 us
    ppermute x4 -> x6, waiting for transfers between devices: 48.8 us -> 45.6 us  [swap(): return lax.ppermute(value, axis, [(0, 1), (1, 0)])]
  transfers between devices with their start and end apart: 5 -> 7, of which waited for: 5 -> 6; matrix products, arithmetic and copies ran while one was open for 0% -> 1% of each run, Pallas kernels for 0% -> 0%
where the time goes in v10:
time: 130 us; the launch traced here: 129 us
  waiting for transfers between devices  72.1 us (55%)
  blocking collectives  36.4 us (28%)
  starting transfers between devices  7.4 us (6%)
  local copies, waits for them, and re-layouts  5.91 us (5%)
  matrix products  5.14 us (4%)
  other arithmetic  2.21 us (2%)
    ppermute x6, waiting for transfers between devices, swap(): return lax.ppermute(value, axis, [(0, 1), (1, 0)])  45.6 us
    all_to_all x1, blocking collectives, body(): lax.all_to_all(slots, CROSS, split_axis=0, concat_axis=0, tiled=True)  36.4 us
    all_to_all x1, waiting for transfers between devices, body(): lax.all_to_all(expert_out.astype(jnp.bfloat16), CROSS, split_axis=0, conc...  26.5 us
    all_to_all x1, starting transfers between devices, body(): lax.all_to_all(expert_out.astype(jnp.bfloat16), CROSS, split_axis=0, conc...  4.91 us
  transfers between devices with their start and end apart: 7, of which 6 were waited for; matrix products, arithmetic and copies ran while one was open for 1% of the time, Pallas kernels for 0%

profile of v10, /device:TPU:32, one launch (start us, length us, event | category | flops | bytes accessed | tf_op | source)
XLA Modules:
  0.0 129.3 jit_solution(4780857048297990651)
XLA Ops:
  0.0 0.0 copy-start
  0.0 0.8 eq.56
  0.8 0.8 iota_compare_fusion
  1.5 0.2 convert_reduce_fusion
  1.7 0.1 eq.60
  1.8 0.1 fusion.14
  1.9 0.0 copy-done
  1.9 0.5 fusion
  2.4 0.9 copy.14
  3.4 36.4 %all_to_all.10 = bf16[16,2,2,7168]{3,2,1,0:T(2,128)(2,1)S(1)} all-to-all(bf16[16,2,2,7168]{3,2,1,0:T(2,128)(2,1)S(1)} %copy.14), channel_id=1, replica_groups=mesh['dp'=4,'x'=4,'zh'=4,'zl'=2,'c'=2] {'x','zh'}, dimensions={0} | all-to-all | bytes 1835008 | tf_op jit(solution)/shard_map/all_to_all | solution.py:46
  39.8 0.3 copy.34
  40.1 1.1 collective-permute-start
  41.2 0.0 collective-permute-start.1
  41.2 19.6 %collective-permute-done = bf16[16,2,2,7168]{3,0,2,1:T(8,128)(2,1)S(1)} collective-permute-done((bf16[16,2,2,7168]{3,0,2,1:T(8,128)(2,1)S(1)}, bf16[16,2,2,7168]{3,0,2,1:T(8,128)(2,1)S(1)}, u32[]{:S(2)}, u32[]{:S(2)}) %collective-permute-start) | collective-permute-done | bytes 917536 | tf_op jit(solution)/shard_map/ppermute | solution.py:31
  60.8 0.0 collective-permute-start.2
  60.8 0.0 copy-start.2
  60.8 0.2 maximum_bitcast_fusion
  61.0 0.0 collective-permute-done.1
  61.0 2.3 %collective-permute-done.2 = bf16[16,2,2,7168]{3,0,2,1:T(8,128)(2,1)S(1)} collective-permute-done((bf16[16,2,2,7168]{3,0,2,1:T(8,128)(2,1)S(1)}, bf16[16,2,2,7168]{3,0,2,1:T(8,128)(2,1)S(1)}, u32[]{:S(2)}, u32[]{:S(2)}) %collective-permute-start.2) | collective-permute-done | bytes 917536 | tf_op jit(solution)/shard_map/ppermute | solution.py:31
  63.3 0.2 maximum_bitcast_fusion.1
  63.5 0.0 copy-done.2
  63.5 0.0 copy-start.3
  63.5 1.1 fusion.3
  64.6 0.9 copy-done.3
  65.5 0.0 copy-start.4
  65.5 1.1 fusion.5
  66.6 0.9 copy-done.4
  67.5 1.1 convolution_convert_fusion
  68.7 0.1 slice_bitcast_fusion.2
  68.8 0.2 collective-permute-start.4
  69.1 0.4 collective-permute-start.3
  69.4 2.0 %collective-permute-done.4 = bf16[16,2,2,7168]{3,0,2,1:T(8,128)(2,1)S(1)} collective-permute-done((bf16[16,2,2,7168]{3,0,2,1:T(8,128)(2,1)S(1)}, bf16[16,2,2,7168]{3,0,2,1:T(8,128)(2,1)S(1)}, u32[]{:S(2)}, u32[]{:S(2)}) %collective-permute-start.4) | collective-permute-done | bytes 917536 | tf_op jit(solution)/shard_map/ppermute | solution.py:31
  71.4 0.2 fusion.7
  71.6 0.0 copy-start.1
  71.6 0.8 collective-permute-start.5
  72.4 0.3 collective-permute-done.3
  72.7 21.4 %collective-permute-done.5 = bf16[16,2,2,7168]{3,0,2,1:T(8,128)(2,1)S(1)} collective-permute-done((bf16[16,2,2,7168]{3,0,2,1:T(8,128)(2,1)S(1)}, bf16[16,2,2,7168]{3,0,2,1:T(8,128)(2,1)S(1)}, u32[]{:S(2)}, u32[]{:S(2)}) %collective-permute-start.5) | collective-permute-done | bytes 917536 | tf_op jit(solution)/shard_map/ppermute | solution.py:31
  94.1 0.3 fusion.9
  94.4 1.9 %copy.18 = bf16[16,2,2,7168]{3,2,1,0:T(2,128)(2,1)} copy(bf16[16,2,2,7168]{3,0,2,1:T(8,128)(2,1)S(1)} %fusion.9) | data formatting | bytes 1835008 | tf_op jit(solution)/shard_map/convert_element_type | solution.py:65
  96.3 4.9 %all-to-all-start.1 = ((bf16[16,2,2,7168]{3,2,1,0:T(2,128)(2,1)}), bf16[16,2,2,7168]{3,2,1,0:T(2,128)(2,1)S(1)}, u32[]{:S(2)}, u32[]{:S(2)}) async-start(bf16[16,2,2,7168]{3,2,1,0:T(2,128)(2,1)} %copy.18), calls=%async_computation.1 | async-start | bytes 1835008 | tf_op jit(solution)/shard_map/all_to_all | solution.py:64
  101.2 0.0 copy-done.1
  101.2 0.1 convert_reduce_fusion.1
  101.3 0.1 convert_divide_fusion
  101.4 0.1 fusion.13
  101.5 26.5 %all-to-all-done.1 = bf16[16,2,2,7168]{3,2,1,0:T(2,128)(2,1)S(1)} async-done(((bf16[16,2,2,7168]{3,2,1,0:T(2,128)(2,1)}), bf16[16,2,2,7168]{3,2,1,0:T(2,128)(2,1)S(1)}, u32[]{:S(2)}, u32[]{:S(2)}) %all-to-all-start.1) | async-done | bytes 917536 | tf_op jit(solution)/shard_map/all_to_all | solution.py:64
  128.0 1.3 %fusion.1 = bf16[2,2,7168]{2,1,0:T(2,128)(2,1)} fusion(bf16[16,2,2,7168]{3,2,1,0:T(2,128)(2,1)S(1)} %all-to-all-done.1, f32[2,2,16,2]{2,3,1,0:T(2,128)S(1)} %fusion.13), kind=kOutput, calls=%fused_computation.4 | convolution fusion | flops 11038720 | bytes 975360 | tf_op jit(solution)/shard_map/srec,escd->srd/dot_general | solution.py:67
  (3 shorter events, 0.0 us)
Async XLA Ops:
  0.0 1.9 %copy-start = (bf16[2,2,7168]{2,1,0:T(2,128)(2,1)S(1)}, bf16[2,2,7168]{2,1,0:T(2,128)(2,1)}, u32[]{:S(2)}) copy-start(bf16[2,2,7168]{2,1,0:T(2,128)(2,1)} %param.6) | copy-start | bytes 172036
  40.1 20.7 %collective-permute-start = (bf16[16,2,2,7168]{3,0,2,1:T(8,128)(2,1)S(1)}, bf16[16,2,2,7168]{3,0,2,1:T(8,128)(2,1)S(1)}, u32[]{:S(2)}, u32[]{:S(2)}) collective-permute-start(bf16[16,2,2,7168]{3,0,2,1:T(8,128)(2,1)S(1)} %copy.34), channel_id=1, source_target_pairs={{0,2},{2,0},{1,3},{3,1},{4,6},{6,4},{5,7},{7,5},{8,10},{10,8},{9,1... | collective-permute-start | bytes 2752520 | tf_op jit(solution)/shard_map/ppermute | solution.py:31
  41.2 19.8 %collective-permute-start.1 = (bf16[16,2,2,7168]{3,0,2,1:T(8,128)(2,1)S(1)}, bf16[16,2,2,7168]{3,0,2,1:T(8,128)(2,1)S(1)}, u32[]{:S(2)}, u32[]{:S(2)}) collective-permute-start(bf16[16,2,2,7168]{3,0,2,1:T(8,128)(2,1)S(1)} %copy.34), channel_id=1, source_target_pairs={{0,1},{1,0},{2,3},{3,2},{4,5},{5,4},{6,7},{7,6},{8,9},{9,8},{10,11... | collective-permute-start | bytes 2752520 | tf_op jit(solution)/shard_map/ppermute | solution.py:31
  60.8 2.5 %collective-permute-start.2 = (bf16[16,2,2,7168]{3,0,2,1:T(8,128)(2,1)S(1)}, bf16[16,2,2,7168]{3,0,2,1:T(8,128)(2,1)S(1)}, u32[]{:S(2)}, u32[]{:S(2)}) collective-permute-start(bf16[16,2,2,7168]{3,0,2,1:T(8,128)(2,1)S(1)} %collective-permute-done), channel_id=1, source_target_pairs={{0,1},{1,0},{2,3},{3,2},{4,5},{5,4},{6,7},{7,6},{8,9},{9,8},{10,11... | collective-permute-start | bytes 2752520 | tf_op jit(solution)/shard_map/ppermute | solution.py:31
  60.8 2.6 %copy-start.2 = (bf16[1,7168,256]{2,1,0:T(8,128)(2,1)S(1)}, bf16[1,7168,256]{2,1,0:T(8,128)(2,1)}, u32[]{:S(2)}) copy-start(bf16[1,7168,256]{2,1,0:T(8,128)(2,1)} %param.10) | copy-start | bytes 11010052
  63.5 2.0 %copy-start.3 = (bf16[1,7168,256]{2,1,0:T(8,128)(2,1)S(1)}, bf16[1,7168,256]{2,1,0:T(8,128)(2,1)}, u32[]{:S(2)}) copy-start(bf16[1,7168,256]{2,1,0:T(8,128)(2,1)} %param.9) | copy-start | bytes 11010052
  65.5 2.0 %copy-start.4 = (bf16[1,256,7168]{2,1,0:T(8,128)(2,1)S(1)}, bf16[1,256,7168]{2,1,0:T(8,128)(2,1)}, u32[]{:S(2)}) copy-start(bf16[1,256,7168]{2,1,0:T(8,128)(2,1)} %param.11) | copy-start | bytes 11010052
  68.8 2.6 %collective-permute-start.4 = (bf16[16,2,2,7168]{3,0,2,1:T(8,128)(2,1)S(1)}, bf16[16,2,2,7168]{3,0,2,1:T(8,128)(2,1)S(1)}, u32[]{:S(2)}, u32[]{:S(2)}) collective-permute-start(bf16[16,2,2,7168]{3,0,2,1:T(8,128)(2,1)S(1)} %get-tuple-element.6), channel_id=1, source_target_pairs={{0,1},{1,0},{2,3},{3,2},{4,5},{5,4},{6,7},{7,6},{8,9},{9,8},{10,11... | collective-permute-start | bytes 2752520 | tf_op jit(solution)/shard_map/ppermute | solution.py:31
  69.1 3.6 %collective-permute-start.3 = (bf16[16,2,2,7168]{3,0,2,1:T(8,128)(2,1)S(1)}, bf16[16,2,2,7168]{3,0,2,1:T(8,128)(2,1)S(1)}, u32[]{:S(2)}, u32[]{:S(2)}) collective-permute-start(bf16[16,2,2,7168]{3,0,2,1:T(8,128)(2,1)S(1)} %get-tuple-element.5), channel_id=1, source_target_pairs={{0,1},{1,0},{2,3},{3,2},{4,5},{5,4},{6,7},{7,6},{8,9},{9,8},{10,11... | collective-permute-start | bytes 2752520 | tf_op jit(solution)/shard_map/ppermute | solution.py:31
  71.6 29.6 %copy-start.1 = (s32[2,2,8]{2,1,0:T(2,128)S(1)}, s32[2,2,8]{2,1,0:T(2,128)}, u32[]{:S(2)}) copy-start(s32[2,2,8]{2,1,0:T(2,128)} %param.8) | copy-start | bytes 388
  71.6 22.5 %collective-permute-start.5 = (bf16[16,2,2,7168]{3,0,2,1:T(8,128)(2,1)S(1)}, bf16[16,2,2,7168]{3,0,2,1:T(8,128)(2,1)S(1)}, u32[]{:S(2)}, u32[]{:S(2)}) collective-permute-start(bf16[16,2,2,7168]{3,0,2,1:T(8,128)(2,1)S(1)} %fusion.7), channel_id=1, source_target_pairs={{0,2},{2,0},{1,3},{3,1},{4,6},{6,4},{5,7},{7,5},{8,10},{10,8},{9,1... | collective-permute-start | bytes 2752520 | tf_op jit(solution)/shard_map/ppermute | solution.py:31
  96.3 31.7 %all-to-all-start.1 = ((bf16[16,2,2,7168]{3,2,1,0:T(2,128)(2,1)}), bf16[16,2,2,7168]{3,2,1,0:T(2,128)(2,1)S(1)}, u32[]{:S(2)}, u32[]{:S(2)}) async-start(bf16[16,2,2,7168]{3,2,1,0:T(2,128)(2,1)} %copy.18), calls=%async_computation.1 | async-start | bytes 1835008 | tf_op jit(solution)/shard_map/all_to_all | solution.py:64

commit v11 on v10

--- a/solution.py
+++ b/solution.py
@@ -5,8 +5,7 @@
 from jax.sharding import Mesh
 from jax.sharding import PartitionSpec as P
 
-EH = 1024
-HS = 256
+
 CROSS = ("x", "zh")
 
 
@@ -27,12 +26,21 @@
     return (placement, mix_table)
 
 
+def expert_mlp(rows, gate, up, down):
+    gate_act = jnp.einsum("...d,dh->...h", rows, gate, preferred_element_type=jnp.float32)
+    up_act = jnp.einsum("...d,dh->...h", rows, up, preferred_element_type=jnp.float32)
+    hidden = (jax.nn.silu(gate_act) * up_act).astype(jnp.bfloat16)
+    return jnp.einsum("...h,hd->...d", hidden, down, preferred_element_type=jnp.float32).astype(
+        jnp.bfloat16
+    )
+
+
 def swap(value, axis):
     return lax.ppermute(value, axis, [(0, 1), (1, 0)])
 
 
-def body(tokens, expert_ids, gate_codes, w_gate, w_up, w_down):
-    step_count, row_count, width = tokens.shape
+def layer(tokens, expert_ids, gate_codes, w_gate, w_up, w_down):
+    _, row_count, _ = tokens.shape
     top_count = expert_ids.shape[2]
     experts_all = lax.axis_size(CROSS)
     capacity = min(row_count, max(2, 2 * row_count * top_count // experts_all))
@@ -45,21 +53,11 @@
     ).astype(jnp.bfloat16)
     received = lax.all_to_all(slots, CROSS, split_axis=0, concat_axis=0, tiled=True)
     from_chip = swap(received, "zl")
-    received = jnp.stack(
-        [jnp.stack([received, from_chip], 0), jnp.stack([swap(received, "c"), swap(from_chip, "c")], 0)],
-        0,
-    )
-    gate_act = jnp.einsum(
-        "...cd,dh->...ch", received, w_gate[0], preferred_element_type=jnp.float32
-    )
-    up_act = jnp.einsum("...cd,dh->...ch", received, w_up[0], preferred_element_type=jnp.float32)
-    hidden = (jax.nn.silu(gate_act) * up_act).astype(jnp.bfloat16)
-    partial_out = jnp.einsum(
-        "...ch,hd->...cd", hidden, w_down[0], preferred_element_type=jnp.float32
-    ).astype(jnp.bfloat16)
-    leaving = partial_out[0, 1].astype(jnp.float32) + swap(partial_out[1, 1], "c").astype(jnp.float32)
+    here = expert_mlp(jnp.stack([received, swap(received, "c")], 0), w_gate[0], w_up[0], w_down[0])
+    staying = here[0].astype(jnp.float32) + swap(here[1], "c").astype(jnp.float32)
+    there = expert_mlp(jnp.stack([from_chip, swap(from_chip, "c")], 0), w_gate[0], w_up[0], w_down[0])
+    leaving = there[0].astype(jnp.float32) + swap(there[1], "c").astype(jnp.float32)
     arriving = swap(leaving.astype(jnp.bfloat16), "zl").astype(jnp.float32)
-    staying = partial_out[0, 0].astype(jnp.float32) + swap(partial_out[1, 0], "c").astype(jnp.float32)
     expert_out = staying + arriving
     returned = lax.all_to_all(
         expert_out.astype(jnp.bfloat16), CROSS, split_axis=0, concat_axis=0, tiled=True
@@ -84,5 +82,5 @@
     blocks_spec = P(("dp", "x", "zh", "zl", "c"), None, None)
     placed = (rows_spec, rows_spec, rows_spec, blocks_spec, blocks_spec, blocks_spec)
     return jax.shard_map(
-        body, mesh=chip_mesh, in_specs=placed, out_specs=rows_spec, check_vma=False
+        layer, mesh=chip_mesh, in_specs=placed, out_specs=rows_spec, check_vma=False
     )

time: 130 us -> 129 us (level); the launches traced: 129 us -> 126 us
  local copies, waits for them, and re-layouts: 5.91 us -> 4.09 us
  waiting for transfers between devices: 72.1 us -> 70.7 us
    unnamed x10, local copies, waits for them, and re-layouts: 1.85 us -> 0.03 us
    dot_general x5 -> x8, matrix products: 5.14 us -> 5.8 us  [the longest x2 1.35 us: expert_mlp(): jnp.einsum('...h,hd->...d', hidden, down, preferred_element_type=jnp.floa...]
  transfers between devices with their start and end apart: 7 -> 7, of which waited for: 6 -> 6; matrix products, arithmetic and copies ran while one was open for 1% -> 2% of each run, Pallas kernels for 0% -> 0%
where the time goes in v11:
time: 129 us; the launch traced here: 126 us
  waiting for transfers between devices  70.7 us (55%)
  blocking collectives  36.7 us (28%)
  starting transfers between devices  7.06 us (5%)
  matrix products  5.8 us (4%)
  local copies, waits for them, and re-layouts  4.09 us (3%)
  other arithmetic  1.9 us (1%)
    ppermute x6, waiting for transfers between devices, swap(): return lax.ppermute(value, axis, [(0, 1), (1, 0)])  45.2 us
    all_to_all x1, blocking collectives, layer(): lax.all_to_all(slots, CROSS, split_axis=0, concat_axis=0, tiled=True)  36.7 us
    all_to_all x1, waiting for transfers between devices, layer(): lax.all_to_all(expert_out.astype(jnp.bfloat16), CROSS, split_axis=0, conc...  25.5 us
    all_to_all x1, starting transfers between devices, layer(): lax.all_to_all(expert_out.astype(jnp.bfloat16), CROSS, split_axis=0, conc...  4.04 us
    ppermute x6, starting transfers between devices, swap(): return lax.ppermute(value, axis, [(0, 1), (1, 0)])  3.02 us
  transfers between devices with their start and end apart: 7, of which 6 were waited for; matrix products, arithmetic and copies ran while one was open for 2% of the time, Pallas kernels for 0%

profile of v11, /device:TPU:32, one launch (start us, length us, event | category | flops | bytes accessed | tf_op | source)
XLA Modules:
  0.0 126.4 jit_solution(5661812661985761115)
XLA Ops:
  0.0 0.0 copy-start
  0.0 0.8 eq.56
  0.8 0.8 iota_compare_fusion
  1.5 0.2 convert_reduce_fusion
  1.7 0.1 eq.60
  1.8 0.1 fusion.20
  1.9 0.0 copy-done
  1.9 0.5 fusion
  2.4 0.9 copy.14
  3.4 0.0 copy-start.3
  3.4 36.7 %all_to_all.10 = bf16[16,2,2,7168]{3,2,1,0:T(2,128)(2,1)S(1)} all-to-all(bf16[16,2,2,7168]{3,2,1,0:T(2,128)(2,1)S(1)} %copy.14), channel_id=1, replica_groups=mesh['dp'=4,'x'=4,'zh'=4,'zl'=2,'c'=2] {'x','zh'}, dimensions={0} | all-to-all | bytes 1835008 | tf_op jit(solution)/shard_map/all_to_all | solution.py:54
  40.1 0.3 copy.34
  40.3 0.1 collective-permute-start
  40.4 1.1 collective-permute-start.2
  41.6 1.3 %collective-permute-done = bf16[16,2,2,7168]{3,0,2,1:T(8,128)(2,1)S(1)} collective-permute-done((bf16[16,2,2,7168]{3,0,2,1:T(8,128)(2,1)S(1)}, bf16[16,2,2,7168]{3,0,2,1:T(8,128)(2,1)S(1)}, u32[]{:S(2)}, u32[]{:S(2)}) %collective-permute-start) | collective-permute-done | bytes 917536 | tf_op jit(solution)/shard_map/ppermute | solution.py:39
  42.9 0.0 copy-done.3
  42.9 0.0 copy-start.4
  42.9 0.7 fusion.10
  43.6 0.0 copy-start.1
  43.6 19.6 %collective-permute-done.2 = bf16[16,2,2,7168]{3,0,2,1:T(8,128)(2,1)S(1)} collective-permute-done((bf16[16,2,2,7168]{3,0,2,1:T(8,128)(2,1)S(1)}, bf16[16,2,2,7168]{3,0,2,1:T(8,128)(2,1)S(1)}, u32[]{:S(2)}, u32[]{:S(2)}) %collective-permute-start.2) | collective-permute-done | bytes 917536 | tf_op jit(solution)/shard_map/ppermute | solution.py:39
  63.2 0.0 collective-permute-start.3
  63.2 0.0 copy-done.4
  63.2 0.7 fusion.6
  63.9 0.0 copy-done.1
  63.9 0.7 convolution_convert_fusion.1
  64.6 1.1 collective-permute-done.3
  65.7 0.6 fusion.8
  66.3 0.6 fusion.4
  67.0 0.7 convolution_convert_fusion
  67.7 0.1 slice_bitcast_fusion
  67.7 0.2 collective-permute-start.4
  67.9 0.1 slice_bitcast_fusion.2
  68.0 0.5 collective-permute-start.1
  68.5 1.8 %collective-permute-done.4 = bf16[16,2,2,7168]{3,0,2,1:T(8,128)(2,1)S(1)} collective-permute-done((bf16[16,2,2,7168]{3,0,2,1:T(8,128)(2,1)S(1)}, bf16[16,2,2,7168]{3,0,2,1:T(8,128)(2,1)S(1)}, u32[]{:S(2)}, u32[]{:S(2)}) %collective-permute-start.4) | collective-permute-done | bytes 917536 | tf_op jit(solution)/shard_map/ppermute | solution.py:39
  70.3 0.2 fusion.12
  70.5 1.1 collective-permute-start.5
  71.6 0.0 collective-permute-done.1
  71.6 21.4 %collective-permute-done.5 = bf16[16,2,2,7168]{3,0,2,1:T(8,128)(2,1)S(1)} collective-permute-done((bf16[16,2,2,7168]{3,0,2,1:T(8,128)(2,1)S(1)}, bf16[16,2,2,7168]{3,0,2,1:T(8,128)(2,1)S(1)}, u32[]{:S(2)}, u32[]{:S(2)}) %collective-permute-start.5) | collective-permute-done | bytes 917536 | tf_op jit(solution)/shard_map/ppermute | solution.py:39
  93.0 0.3 fusion.14
  93.3 0.0 copy-start.2
  93.4 1.9 %copy.18 = bf16[16,2,2,7168]{3,2,1,0:T(2,128)(2,1)} copy(bf16[16,2,2,7168]{3,0,2,1:T(8,128)(2,1)S(1)} %fusion.14) | data formatting | bytes 1835008 | tf_op jit(solution)/shard_map/convert_element_type | solution.py:63
  95.2 4.0 %all-to-all-start.1 = ((bf16[16,2,2,7168]{3,2,1,0:T(2,128)(2,1)}), bf16[16,2,2,7168]{3,2,1,0:T(2,128)(2,1)S(1)}, u32[]{:S(2)}, u32[]{:S(2)}) async-start(bf16[16,2,2,7168]{3,2,1,0:T(2,128)(2,1)} %copy.18), calls=%async_computation.1 | async-start | bytes 1835008 | tf_op jit(solution)/shard_map/all_to_all | solution.py:62
  99.3 0.0 copy-done.2
  99.3 0.1 convert_reduce_fusion.1
  99.4 0.1 convert_divide_fusion
  99.4 0.1 fusion.19
  99.6 25.5 %all-to-all-done.1 = bf16[16,2,2,7168]{3,2,1,0:T(2,128)(2,1)S(1)} async-done(((bf16[16,2,2,7168]{3,2,1,0:T(2,128)(2,1)}), bf16[16,2,2,7168]{3,2,1,0:T(2,128)(2,1)S(1)}, u32[]{:S(2)}, u32[]{:S(2)}) %all-to-all-start.1) | async-done | bytes 917536 | tf_op jit(solution)/shard_map/all_to_all | solution.py:62
  125.1 1.3 %fusion.1 = bf16[2,2,7168]{2,1,0:T(2,128)(2,1)} fusion(bf16[16,2,2,7168]{3,2,1,0:T(2,128)(2,1)S(1)} %all-to-all-done.1, f32[2,2,16,2]{2,3,1,0:T(2,128)S(1)} %fusion.19), kind=kOutput, calls=%fused_computation.5 | convolution fusion | flops 11038720 | bytes 975360 | tf_op jit(solution)/shard_map/srec,escd->srd/dot_general | solution.py:65
  (3 shorter events, 0.0 us)
Async XLA Ops:
  0.0 1.9 %copy-start = (bf16[2,2,7168]{2,1,0:T(2,128)(2,1)S(1)}, bf16[2,2,7168]{2,1,0:T(2,128)(2,1)}, u32[]{:S(2)}) copy-start(bf16[2,2,7168]{2,1,0:T(2,128)(2,1)} %param.6) | copy-start | bytes 172036
  3.4 39.5 %copy-start.3 = (bf16[1,7168,256]{2,1,0:T(8,128)(2,1)S(1)}, bf16[1,7168,256]{2,1,0:T(8,128)(2,1)}, u32[]{:S(2)}) copy-start(bf16[1,7168,256]{2,1,0:T(8,128)(2,1)} %param.9) | copy-start | bytes 11010052
  40.3 2.6 %collective-permute-start = (bf16[16,2,2,7168]{3,0,2,1:T(8,128)(2,1)S(1)}, bf16[16,2,2,7168]{3,0,2,1:T(8,128)(2,1)S(1)}, u32[]{:S(2)}, u32[]{:S(2)}) collective-permute-start(bf16[16,2,2,7168]{3,0,2,1:T(8,128)(2,1)S(1)} %copy.34), channel_id=1, source_target_pairs={{0,1},{1,0},{2,3},{3,2},{4,5},{5,4},{6,7},{7,6},{8,9},{9,8},{10,11... | collective-permute-start | bytes 2752520 | tf_op jit(solution)/shard_map/ppermute | solution.py:39
  40.4 22.8 %collective-permute-start.2 = (bf16[16,2,2,7168]{3,0,2,1:T(8,128)(2,1)S(1)}, bf16[16,2,2,7168]{3,0,2,1:T(8,128)(2,1)S(1)}, u32[]{:S(2)}, u32[]{:S(2)}) collective-permute-start(bf16[16,2,2,7168]{3,0,2,1:T(8,128)(2,1)S(1)} %copy.34), channel_id=1, source_target_pairs={{0,2},{2,0},{1,3},{3,1},{4,6},{6,4},{5,7},{7,5},{8,10},{10,8},{9,1... | collective-permute-start | bytes 2752520 | tf_op jit(solution)/shard_map/ppermute | solution.py:39
  42.9 20.3 %copy-start.4 = (bf16[1,7168,256]{2,1,0:T(8,128)(2,1)S(1)}, bf16[1,7168,256]{2,1,0:T(8,128)(2,1)}, u32[]{:S(2)}) copy-start(bf16[1,7168,256]{2,1,0:T(8,128)(2,1)} %param.10) | copy-start | bytes 11010052
  43.6 20.3 %copy-start.1 = (bf16[1,256,7168]{2,1,0:T(8,128)(2,1)S(1)}, bf16[1,256,7168]{2,1,0:T(8,128)(2,1)}, u32[]{:S(2)}) copy-start(bf16[1,256,7168]{2,1,0:T(8,128)(2,1)} %param.11) | copy-start | bytes 11010052
  63.2 2.5 %collective-permute-start.3 = (bf16[16,2,2,7168]{3,0,2,1:T(8,128)(2,1)S(1)}, bf16[16,2,2,7168]{3,0,2,1:T(8,128)(2,1)S(1)}, u32[]{:S(2)}, u32[]{:S(2)}) collective-permute-start(bf16[16,2,2,7168]{3,0,2,1:T(8,128)(2,1)S(1)} %collective-permute-done.2), channel_id=1, source_target_pairs={{0,1},{1,0},{2,3},{3,2},{4,5},{5,4},{6,7},{7,6},{8,9},{9,8},{10,11... | collective-permute-start | bytes 2752520 | tf_op jit(solution)/shard_map/ppermute | solution.py:39
  67.7 2.6 %collective-permute-start.4 = (bf16[16,2,2,7168]{3,0,2,1:T(8,128)(2,1)S(1)}, bf16[16,2,2,7168]{3,0,2,1:T(8,128)(2,1)S(1)}, u32[]{:S(2)}, u32[]{:S(2)}) collective-permute-start(bf16[16,2,2,7168]{3,0,2,1:T(8,128)(2,1)S(1)} %slice_bitcast_fusion), channel_id=1, source_target_pairs={{0,1},{1,0},{2,3},{3,2},{4,5},{5,4},{6,7},{7,6},{8,9},{9,8},{10,11... | collective-permute-start | bytes 2752520 | tf_op jit(solution)/shard_map/ppermute | solution.py:39
  68.0 3.6 %collective-permute-start.1 = (bf16[16,2,2,7168]{3,0,2,1:T(8,128)(2,1)S(1)}, bf16[16,2,2,7168]{3,0,2,1:T(8,128)(2,1)S(1)}, u32[]{:S(2)}, u32[]{:S(2)}) collective-permute-start(bf16[16,2,2,7168]{3,0,2,1:T(8,128)(2,1)S(1)} %slice_bitcast_fusion.2), channel_id=1, source_target_pairs={{0,1},{1,0},{2,3},{3,2},{4,5},{5,4},{6,7},{7,6},{8,9},{9,8},{10,11... | collective-permute-start | bytes 2752520 | tf_op jit(solution)/shard_map/ppermute | solution.py:39
  70.5 22.5 %collective-permute-start.5 = (bf16[16,2,2,7168]{3,0,2,1:T(8,128)(2,1)S(1)}, bf16[16,2,2,7168]{3,0,2,1:T(8,128)(2,1)S(1)}, u32[]{:S(2)}, u32[]{:S(2)}) collective-permute-start(bf16[16,2,2,7168]{3,0,2,1:T(8,128)(2,1)S(1)} %fusion.12), channel_id=1, source_target_pairs={{0,2},{2,0},{1,3},{3,1},{4,6},{6,4},{5,7},{7,5},{8,10},{10,8},{9,1... | collective-permute-start | bytes 2752520 | tf_op jit(solution)/shard_map/ppermute | solution.py:39
  93.3 5.9 %copy-start.2 = (s32[2,2,8]{2,1,0:T(2,128)S(1)}, s32[2,2,8]{2,1,0:T(2,128)}, u32[]{:S(2)}) copy-start(s32[2,2,8]{2,1,0:T(2,128)} %param.8) | copy-start | bytes 388
  95.2 29.9 %all-to-all-start.1 = ((bf16[16,2,2,7168]{3,2,1,0:T(2,128)(2,1)}), bf16[16,2,2,7168]{3,2,1,0:T(2,128)(2,1)S(1)}, u32[]{:S(2)}, u32[]{:S(2)}) async-start(bf16[16,2,2,7168]{3,2,1,0:T(2,128)(2,1)} %copy.18), calls=%async_computation.1 | async-start | bytes 1835008 | tf_op jit(solution)/shard_map/all_to_all | solution.py:62

commit v12 on v11

--- a/solution.py
+++ b/solution.py
@@ -26,6 +26,10 @@
     return (placement, mix_table)
 
 
+def mix_of(expert_ids, gate_codes, experts_all, capacity):
+    return route_tables(lax.optimization_barrier(expert_ids), gate_codes, experts_all, capacity)[1]
+
+
 def expert_mlp(rows, gate, up, down):
     gate_act = jnp.einsum("...d,dh->...h", rows, gate, preferred_element_type=jnp.float32)
     up_act = jnp.einsum("...d,dh->...h", rows, up, preferred_element_type=jnp.float32)
@@ -44,7 +48,7 @@
     top_count = expert_ids.shape[2]
     experts_all = lax.axis_size(CROSS)
     capacity = min(row_count, max(2, 2 * row_count * top_count // experts_all))
-    placement, mix_table = route_tables(expert_ids, gate_codes, experts_all, capacity)
+    placement = route_tables(expert_ids, gate_codes, experts_all, capacity)[0]
     slots = jnp.einsum(
         "srec,srd->escd",
         placement.astype(jnp.bfloat16),
@@ -53,6 +57,7 @@
     ).astype(jnp.bfloat16)
     received = lax.all_to_all(slots, CROSS, split_axis=0, concat_axis=0, tiled=True)
     from_chip = swap(received, "zl")
+    mix_table = mix_of(expert_ids, gate_codes, experts_all, capacity)
     here = expert_mlp(jnp.stack([received, swap(received, "c")], 0), w_gate[0], w_up[0], w_down[0])
     staying = here[0].astype(jnp.float32) + swap(here[1], "c").astype(jnp.float32)
     there = expert_mlp(jnp.stack([from_chip, swap(from_chip, "c")], 0), w_gate[0], w_up[0], w_down[0])

time: 129 us -> 128 us (level)
  the two profiles are of different devices: /device:TPU:32 before, /device:TPU:0 now
where the time goes in v12:
time: 128 us
  waiting for transfers between devices  73 us (57%)
  blocking collectives  36.9 us (29%)
  matrix products  5.79 us (5%)
  local copies, waits for them, and re-layouts  4.95 us (4%)
  starting transfers between devices  4.87 us (4%)
  other arithmetic  2.01 us (2%)
    ppermute x6, waiting for transfers between devices, swap(): return lax.ppermute(value, axis, [(0, 1), (1, 0)])  47 us
    all_to_all x1, blocking collectives, layer(): lax.all_to_all(slots, CROSS, split_axis=0, concat_axis=0, tiled=True)  36.9 us
    all_to_all x1, waiting for transfers between devices, layer(): lax.all_to_all(expert_out.astype(jnp.bfloat16), CROSS, split_axis=0, conc...  26 us
    all_to_all x1, starting transfers between devices, layer(): lax.all_to_all(expert_out.astype(jnp.bfloat16), CROSS, split_axis=0, conc...  3.63 us
  transfers between devices with their start and end apart: 7, of which 7 were waited for; matrix products, arithmetic and copies ran while one was open for 2% of the time, Pallas kernels for 0%

profile of v12, /device:TPU:0, one launch (start us, length us, event | category | flops | bytes accessed | tf_op | source)
XLA Modules:
  0.0 127.7 jit_solution(18265722988154667910)
XLA Ops:
  0.0 0.0 copy-start
  0.0 0.8 eq.120
  0.8 0.8 iota_compare_fusion
  1.5 0.8 eq.109
  2.3 0.2 convert_reduce_fusion.2
  2.5 0.1 eq.124
  2.6 0.1 convert_reduce_fusion
  2.7 0.0 copy-done
  2.7 0.5 fusion
  3.2 0.9 copy.14
  4.2 0.0 copy-start.4
  4.2 36.9 %all_to_all.10 = bf16[16,2,2,7168]{3,2,1,0:T(2,128)(2,1)S(1)} all-to-all(bf16[16,2,2,7168]{3,2,1,0:T(2,128)(2,1)S(1)} %copy.14), channel_id=1, replica_groups=mesh['dp'=4,'x'=4,'zh'=4,'zl'=2,'c'=2] {'x','zh'}, dimensions={0} | all-to-all | bytes 1835008 | tf_op jit(solution)/shard_map/all_to_all | solution.py:58
  41.1 0.3 copy.34
  41.4 0.1 collective-permute-start
  41.5 0.1 collective-permute-start.2
  41.6 2.4 %collective-permute-done = bf16[16,2,2,7168]{3,0,2,1:T(8,128)(2,1)S(1)} collective-permute-done((bf16[16,2,2,7168]{3,0,2,1:T(8,128)(2,1)S(1)}, bf16[16,2,2,7168]{3,0,2,1:T(8,128)(2,1)S(1)}, u32[]{:S(2)}, u32[]{:S(2)}) %collective-permute-start) | collective-permute-done | bytes 917536 | tf_op jit(solution)/shard_map/ppermute | solution.py:43
  44.0 0.0 copy-done.4
  44.0 0.0 copy-start.5
  44.0 0.7 fusion.10
  44.7 0.0 copy-start.1
  44.7 19.6 %collective-permute-done.2 = bf16[16,2,2,7168]{3,0,2,1:T(8,128)(2,1)S(1)} collective-permute-done((bf16[16,2,2,7168]{3,0,2,1:T(8,128)(2,1)S(1)}, bf16[16,2,2,7168]{3,0,2,1:T(8,128)(2,1)S(1)}, u32[]{:S(2)}, u32[]{:S(2)}) %collective-permute-start.2) | collective-permute-done | bytes 917536 | tf_op jit(solution)/shard_map/ppermute | solution.py:43
  64.3 0.0 collective-permute-start.3
  64.3 0.0 copy-done.5
  64.3 0.7 fusion.6
  65.0 0.0 copy-done.1
  65.0 0.7 convolution_convert_fusion.1
  65.6 1.1 collective-permute-done.3
  66.7 0.6 fusion.8
  67.4 0.6 fusion.4
  68.0 0.7 convolution_convert_fusion
  68.7 0.1 slice_bitcast_fusion
  68.8 0.2 collective-permute-start.4
  69.0 0.1 slice_bitcast_fusion.2
  69.1 0.5 collective-permute-start.1
  69.5 1.8 %collective-permute-done.4 = bf16[16,2,2,7168]{3,0,2,1:T(8,128)(2,1)S(1)} collective-permute-done((bf16[16,2,2,7168]{3,0,2,1:T(8,128)(2,1)S(1)}, bf16[16,2,2,7168]{3,0,2,1:T(8,128)(2,1)S(1)}, u32[]{:S(2)}, u32[]{:S(2)}) %collective-permute-start.4) | collective-permute-done | bytes 917536 | tf_op jit(solution)/shard_map/ppermute | solution.py:43
  71.3 0.2 fusion.12
  71.6 0.4 collective-permute-start.5
  71.9 0.7 collective-permute-done.1
  72.7 21.4 %collective-permute-done.5 = bf16[16,2,2,7168]{3,0,2,1:T(8,128)(2,1)S(1)} collective-permute-done((bf16[16,2,2,7168]{3,0,2,1:T(8,128)(2,1)S(1)}, bf16[16,2,2,7168]{3,0,2,1:T(8,128)(2,1)S(1)}, u32[]{:S(2)}, u32[]{:S(2)}) %collective-permute-start.5) | collective-permute-done | bytes 917536 | tf_op jit(solution)/shard_map/ppermute | solution.py:43
  94.1 0.3 fusion.14
  94.4 0.0 copy-start.3
  94.4 0.0 copy-start.2
  94.4 1.9 %copy.18 = bf16[16,2,2,7168]{3,2,1,0:T(2,128)(2,1)} copy(bf16[16,2,2,7168]{3,0,2,1:T(8,128)(2,1)S(1)} %fusion.14) | data formatting | bytes 1835008 | tf_op jit(solution)/shard_map/convert_element_type | solution.py:68
  96.3 3.6 %all-to-all-start.1 = ((bf16[16,2,2,7168]{3,2,1,0:T(2,128)(2,1)}), bf16[16,2,2,7168]{3,2,1,0:T(2,128)(2,1)S(1)}, u32[]{:S(2)}, u32[]{:S(2)}) async-start(bf16[16,2,2,7168]{3,2,1,0:T(2,128)(2,1)} %copy.18), calls=%async_computation.1 | async-start | bytes 1835008 | tf_op jit(solution)/shard_map/all_to_all | solution.py:67
  99.9 0.1 eq.113
  100.0 0.0 copy-done.3
  100.0 0.1 convert_reduce_fusion.3
  100.1 0.1 convert_divide_fusion
  100.2 0.0 copy-done.2
  100.2 0.1 iota_compare_fusion.1
  100.3 0.1 select_reduce_fusion
  100.4 26.0 %all-to-all-done.1 = bf16[16,2,2,7168]{3,2,1,0:T(2,128)(2,1)S(1)} async-done(((bf16[16,2,2,7168]{3,2,1,0:T(2,128)(2,1)}), bf16[16,2,2,7168]{3,2,1,0:T(2,128)(2,1)S(1)}, u32[]{:S(2)}, u32[]{:S(2)}) %all-to-all-start.1) | async-done | bytes 917536 | tf_op jit(solution)/shard_map/all_to_all | solution.py:67
  126.4 1.3 %fusion.1 = bf16[2,2,7168]{2,1,0:T(2,128)(2,1)} fusion(bf16[16,2,2,7168]{3,2,1,0:T(2,128)(2,1)S(1)} %all-to-all-done.1, f32[2,2,16,2]{2,3,1,0:T(2,128)S(1)} %select_reduce_fusion), kind=kOutput, calls=%fused_computation.5 | convolution fusion | flops 11038720 | bytes 975360 | tf_op jit(solution)/shard_map/srec,escd->srd/dot_general | solution.py:70
  (4 shorter events, 0.0 us)
Async XLA Ops:
  0.0 2.7 %copy-start = (bf16[2,2,7168]{2,1,0:T(2,128)(2,1)S(1)}, bf16[2,2,7168]{2,1,0:T(2,128)(2,1)}, u32[]{:S(2)}) copy-start(bf16[2,2,7168]{2,1,0:T(2,128)(2,1)} %param.6) | copy-start | bytes 172036
  4.2 39.8 %copy-start.4 = (bf16[1,7168,256]{2,1,0:T(8,128)(2,1)S(1)}, bf16[1,7168,256]{2,1,0:T(8,128)(2,1)}, u32[]{:S(2)}) copy-start(bf16[1,7168,256]{2,1,0:T(8,128)(2,1)} %param.9) | copy-start | bytes 11010052
  41.4 2.6 %collective-permute-start = (bf16[16,2,2,7168]{3,0,2,1:T(8,128)(2,1)S(1)}, bf16[16,2,2,7168]{3,0,2,1:T(8,128)(2,1)S(1)}, u32[]{:S(2)}, u32[]{:S(2)}) collective-permute-start(bf16[16,2,2,7168]{3,0,2,1:T(8,128)(2,1)S(1)} %copy.34), channel_id=1, source_target_pairs={{0,1},{1,0},{2,3},{3,2},{4,5},{5,4},{6,7},{7,6},{8,9},{9,8},{10,11... | collective-permute-start | bytes 2752520 | tf_op jit(solution)/shard_map/ppermute | solution.py:43
  41.5 22.8 %collective-permute-start.2 = (bf16[16,2,2,7168]{3,0,2,1:T(8,128)(2,1)S(1)}, bf16[16,2,2,7168]{3,0,2,1:T(8,128)(2,1)S(1)}, u32[]{:S(2)}, u32[]{:S(2)}) collective-permute-start(bf16[16,2,2,7168]{3,0,2,1:T(8,128)(2,1)S(1)} %copy.34), channel_id=1, source_target_pairs={{0,2},{2,0},{1,3},{3,1},{4,6},{6,4},{5,7},{7,5},{8,10},{10,8},{9,1... | collective-permute-start | bytes 2752520 | tf_op jit(solution)/shard_map/ppermute | solution.py:43
  44.0 20.3 %copy-start.5 = (bf16[1,7168,256]{2,1,0:T(8,128)(2,1)S(1)}, bf16[1,7168,256]{2,1,0:T(8,128)(2,1)}, u32[]{:S(2)}) copy-start(bf16[1,7168,256]{2,1,0:T(8,128)(2,1)} %param.10) | copy-start | bytes 11010052
  44.7 20.3 %copy-start.1 = (bf16[1,256,7168]{2,1,0:T(8,128)(2,1)S(1)}, bf16[1,256,7168]{2,1,0:T(8,128)(2,1)}, u32[]{:S(2)}) copy-start(bf16[1,256,7168]{2,1,0:T(8,128)(2,1)} %param.11) | copy-start | bytes 11010052
  64.3 2.5 %collective-permute-start.3 = (bf16[16,2,2,7168]{3,0,2,1:T(8,128)(2,1)S(1)}, bf16[16,2,2,7168]{3,0,2,1:T(8,128)(2,1)S(1)}, u32[]{:S(2)}, u32[]{:S(2)}) collective-permute-start(bf16[16,2,2,7168]{3,0,2,1:T(8,128)(2,1)S(1)} %collective-permute-done.2), channel_id=1, source_target_pairs={{0,1},{1,0},{2,3},{3,2},{4,5},{5,4},{6,7},{7,6},{8,9},{9,8},{10,11... | collective-permute-start | bytes 2752520 | tf_op jit(solution)/shard_map/ppermute | solution.py:43
  68.8 2.6 %collective-permute-start.4 = (bf16[16,2,2,7168]{3,0,2,1:T(8,128)(2,1)S(1)}, bf16[16,2,2,7168]{3,0,2,1:T(8,128)(2,1)S(1)}, u32[]{:S(2)}, u32[]{:S(2)}) collective-permute-start(bf16[16,2,2,7168]{3,0,2,1:T(8,128)(2,1)S(1)} %slice_bitcast_fusion), channel_id=1, source_target_pairs={{0,1},{1,0},{2,3},{3,2},{4,5},{5,4},{6,7},{7,6},{8,9},{9,8},{10,11... | collective-permute-start | bytes 2752520 | tf_op jit(solution)/shard_map/ppermute | solution.py:43
  69.1 3.6 %collective-permute-start.1 = (bf16[16,2,2,7168]{3,0,2,1:T(8,128)(2,1)S(1)}, bf16[16,2,2,7168]{3,0,2,1:T(8,128)(2,1)S(1)}, u32[]{:S(2)}, u32[]{:S(2)}) collective-permute-start(bf16[16,2,2,7168]{3,0,2,1:T(8,128)(2,1)S(1)} %slice_bitcast_fusion.2), channel_id=1, source_target_pairs={{0,1},{1,0},{2,3},{3,2},{4,5},{5,4},{6,7},{7,6},{8,9},{9,8},{10,11... | collective-permute-start | bytes 2752520 | tf_op jit(solution)/shard_map/ppermute | solution.py:43
  71.6 22.5 %collective-permute-start.5 = (bf16[16,2,2,7168]{3,0,2,1:T(8,128)(2,1)S(1)}, bf16[16,2,2,7168]{3,0,2,1:T(8,128)(2,1)S(1)}, u32[]{:S(2)}, u32[]{:S(2)}) collective-permute-start(bf16[16,2,2,7168]{3,0,2,1:T(8,128)(2,1)S(1)} %fusion.12), channel_id=1, source_target_pairs={{0,2},{2,0},{1,3},{3,1},{4,6},{6,4},{5,7},{7,5},{8,10},{10,8},{9,1... | collective-permute-start | bytes 2752520 | tf_op jit(solution)/shard_map/ppermute | solution.py:43
  94.4 5.6 %copy-start.3 = (s32[2,2,8]{2,1,0:T(2,128)S(1)}, s32[2,2,8]{2,1,0:T(2,128)}, u32[]{:S(2)}) copy-start(s32[2,2,8]{2,1,0:T(2,128)} %param.8) | copy-start | bytes 388
  94.4 5.8 %copy-start.2 = (s32[2,2,8]{2,1,0:T(2,128)S(1)}, s32[2,2,8]{2,1,0:T(2,128)}, u32[]{:S(2)}) copy-start(s32[2,2,8]{2,1,0:T(2,128)} %param.7) | copy-start | bytes 388
  96.3 30.1 %all-to-all-start.1 = ((bf16[16,2,2,7168]{3,2,1,0:T(2,128)(2,1)}), bf16[16,2,2,7168]{3,2,1,0:T(2,128)(2,1)S(1)}, u32[]{:S(2)}, u32[]{:S(2)}) async-start(bf16[16,2,2,7168]{3,2,1,0:T(2,128)(2,1)} %copy.18), calls=%async_computation.1 | async-start | bytes 1835008 | tf_op jit(solution)/shard_map/all_to_all | solution.py:67

commit v13 on v12

--- a/solution.py
+++ b/solution.py
@@ -60,8 +60,10 @@
     mix_table = mix_of(expert_ids, gate_codes, experts_all, capacity)
     here = expert_mlp(jnp.stack([received, swap(received, "c")], 0), w_gate[0], w_up[0], w_down[0])
     staying = here[0].astype(jnp.float32) + swap(here[1], "c").astype(jnp.float32)
-    there = expert_mlp(jnp.stack([from_chip, swap(from_chip, "c")], 0), w_gate[0], w_up[0], w_down[0])
-    leaving = there[0].astype(jnp.float32) + swap(there[1], "c").astype(jnp.float32)
+    from_chip_other = swap(from_chip, "c")
+    there_own = expert_mlp(from_chip, w_gate[0], w_up[0], w_down[0])
+    there_other = expert_mlp(from_chip_other, w_gate[0], w_up[0], w_down[0])
+    leaving = there_own.astype(jnp.float32) + swap(there_other, "c").astype(jnp.float32)
     arriving = swap(leaving.astype(jnp.bfloat16), "zl").astype(jnp.float32)
     expert_out = staying + arriving
     returned = lax.all_to_all(

time: 128 us -> 128 us (level)
  matrix products: 5.79 us -> 8.18 us
  waiting for transfers between devices: 73 us -> 71.5 us
    ppermute x6, waiting for transfers between devices: 47 us -> 45.5 us  [swap(): return lax.ppermute(value, axis, [(0, 1), (1, 0)])]
  transfers between devices with their start and end apart: 7 -> 7, of which waited for: 7 -> 7; matrix products, arithmetic and copies ran while one was open for 2% -> 4% of each run, Pallas kernels for 0% -> 0%
where the time goes in v13:
time: 128 us
  waiting for transfers between devices  71.5 us (56%)
  blocking collectives  36.7 us (29%)
  matrix products  8.18 us (6%)
  local copies, waits for them, and re-layouts  4.89 us (4%)
  starting transfers between devices  4.87 us (4%)
  other arithmetic  1.78 us (1%)
    ppermute x6, waiting for transfers between devices, swap(): return lax.ppermute(value, axis, [(0, 1), (1, 0)])  45.5 us
    all_to_all x1, blocking collectives, layer(): lax.all_to_all(slots, CROSS, split_axis=0, concat_axis=0, tiled=True)  36.7 us
    all_to_all x1, waiting for transfers between devices, layer(): lax.all_to_all(expert_out.astype(jnp.bfloat16), CROSS, split_axis=0, conc...  26 us
    all_to_all x1, starting transfers between devices, layer(): lax.all_to_all(expert_out.astype(jnp.bfloat16), CROSS, split_axis=0, conc...  3.63 us
  transfers between devices with their start and end apart: 7, of which 7 were waited for; matrix products, arithmetic and copies ran while one was open for 4% of the time, Pallas kernels for 0%

profile of v13, /device:TPU:0, one launch (start us, length us, event | category | flops | bytes accessed | tf_op | source)
XLA Modules:
  0.0 128.1 jit_solution(10101947181756139295)
XLA Ops:
  0.0 0.0 copy-start
  0.0 0.8 eq.120
  0.8 0.8 iota_compare_fusion
  1.5 0.8 eq.109
  2.3 0.2 convert_reduce_fusion.2
  2.5 0.1 eq.124
  2.6 0.0 copy-start.2
  2.6 0.1 convert_reduce_fusion
  2.7 0.0 copy-done
  2.7 0.5 fusion.1
  3.2 0.9 copy.14
  4.2 36.7 %all_to_all.10 = bf16[16,2,2,7168]{3,2,1,0:T(2,128)(2,1)S(1)} all-to-all(bf16[16,2,2,7168]{3,2,1,0:T(2,128)(2,1)S(1)} %copy.14), channel_id=1, replica_groups=mesh['dp'=4,'x'=4,'zh'=4,'zl'=2,'c'=2] {'x','zh'}, dimensions={0} | all-to-all | bytes 1835008 | tf_op jit(solution)/shard_map/all_to_all | solution.py:58
  40.8 0.3 copy.37
  41.1 0.1 collective-permute-start
  41.2 0.1 collective-permute-start.2
  41.3 2.4 %collective-permute-done = bf16[16,2,2,7168]{3,0,2,1:T(8,128)(2,1)S(1)} collective-permute-done((bf16[16,2,2,7168]{3,0,2,1:T(8,128)(2,1)S(1)}, bf16[16,2,2,7168]{3,0,2,1:T(8,128)(2,1)S(1)}, u32[]{:S(2)}, u32[]{:S(2)}) %collective-permute-start) | collective-permute-done | bytes 917536 | tf_op jit(solution)/shard_map/ppermute | solution.py:43
  43.7 0.0 copy-done.2
  43.7 0.0 copy-start.3
  43.7 0.7 fusion.4
  44.4 0.0 copy-start.1
  44.4 19.6 %collective-permute-done.2 = bf16[16,2,2,7168]{3,0,2,1:T(8,128)(2,1)S(1)} collective-permute-done((bf16[16,2,2,7168]{3,0,2,1:T(8,128)(2,1)S(1)}, bf16[16,2,2,7168]{3,0,2,1:T(8,128)(2,1)S(1)}, u32[]{:S(2)}, u32[]{:S(2)}) %collective-permute-start.2) | collective-permute-done | bytes 917536 | tf_op jit(solution)/shard_map/ppermute | solution.py:43
  64.0 0.0 collective-permute-start.3
  64.0 0.0 copy-done.3
  64.0 0.7 fusion.6
  64.7 0.0 copy-done.1
  64.7 0.7 convolution_convert_fusion
  65.4 1.1 collective-permute-done.3
  66.5 0.7 fusion.10
  67.2 0.7 fusion.14
  67.9 0.8 convolution_convert_fusion.2
  68.7 0.2 collective-permute-start.4
  68.9 0.1 slice_bitcast_fusion
  68.9 0.5 collective-permute-start.1
  69.4 0.7 fusion.12
  70.1 0.7 fusion.16
  70.8 0.4 collective-permute-done.4
  71.2 0.8 add_convert_fusion
  72.0 0.0 copy-start.5
  72.0 0.0 copy-start.4
  72.0 0.4 collective-permute-start.5
  72.4 0.2 collective-permute-done.1
  72.5 21.9 %collective-permute-done.5 = bf16[16,2,2,7168]{3,0,2,1:T(8,128)(2,1)S(1)} collective-permute-done((bf16[16,2,2,7168]{3,0,2,1:T(8,128)(2,1)S(1)}, bf16[16,2,2,7168]{3,0,2,1:T(8,128)(2,1)S(1)}, u32[]{:S(2)}, u32[]{:S(2)}) %collective-permute-start.5) | collective-permute-done | bytes 917536 | tf_op jit(solution)/shard_map/ppermute | solution.py:43
  94.5 0.3 fusion.19
  94.8 1.9 %copy.18 = bf16[16,2,2,7168]{3,2,1,0:T(2,128)(2,1)} copy(bf16[16,2,2,7168]{3,0,2,1:T(8,128)(2,1)S(1)} %fusion.19) | data formatting | bytes 1835008 | tf_op jit(solution)/shard_map/convert_element_type | solution.py:70
  96.7 3.6 %all-to-all-start.1 = ((bf16[16,2,2,7168]{3,2,1,0:T(2,128)(2,1)}), bf16[16,2,2,7168]{3,2,1,0:T(2,128)(2,1)S(1)}, u32[]{:S(2)}, u32[]{:S(2)}) async-start(bf16[16,2,2,7168]{3,2,1,0:T(2,128)(2,1)} %copy.18), calls=%async_computation.1 | async-start | bytes 1835008 | tf_op jit(solution)/shard_map/all_to_all | solution.py:69
  100.3 0.1 eq.113
  100.4 0.0 copy-done.5
  100.4 0.1 convert_reduce_fusion.3
  100.5 0.1 convert_divide_fusion
  100.6 0.0 copy-done.4
  100.6 0.1 iota_compare_fusion.1
  100.7 0.1 select_reduce_fusion
  100.8 26.0 %all-to-all-done.1 = bf16[16,2,2,7168]{3,2,1,0:T(2,128)(2,1)S(1)} async-done(((bf16[16,2,2,7168]{3,2,1,0:T(2,128)(2,1)}), bf16[16,2,2,7168]{3,2,1,0:T(2,128)(2,1)S(1)}, u32[]{:S(2)}, u32[]{:S(2)}) %all-to-all-start.1) | async-done | bytes 917536 | tf_op jit(solution)/shard_map/all_to_all | solution.py:69
  126.8 1.3 %fusion.2 = bf16[2,2,7168]{2,1,0:T(2,128)(2,1)} fusion(bf16[16,2,2,7168]{3,2,1,0:T(2,128)(2,1)S(1)} %all-to-all-done.1, f32[2,2,16,2]{2,3,1,0:T(2,128)S(1)} %select_reduce_fusion), kind=kOutput, calls=%fused_computation.7 | convolution fusion | flops 11038720 | bytes 975360 | tf_op jit(solution)/shard_map/srec,escd->srd/dot_general | solution.py:72
  (4 shorter events, 0.0 us)
Async XLA Ops:
  0.0 2.7 %copy-start = (bf16[2,2,7168]{2,1,0:T(2,128)(2,1)S(1)}, bf16[2,2,7168]{2,1,0:T(2,128)(2,1)}, u32[]{:S(2)}) copy-start(bf16[2,2,7168]{2,1,0:T(2,128)(2,1)} %param.6) | copy-start | bytes 172036
  2.6 41.1 %copy-start.2 = (bf16[1,7168,256]{2,1,0:T(8,128)(2,1)S(1)}, bf16[1,7168,256]{2,1,0:T(8,128)(2,1)}, u32[]{:S(2)}) copy-start(bf16[1,7168,256]{2,1,0:T(8,128)(2,1)} %param.10) | copy-start | bytes 11010052
  41.1 2.6 %collective-permute-start = (bf16[16,2,2,7168]{3,0,2,1:T(8,128)(2,1)S(1)}, bf16[16,2,2,7168]{3,0,2,1:T(8,128)(2,1)S(1)}, u32[]{:S(2)}, u32[]{:S(2)}) collective-permute-start(bf16[16,2,2,7168]{3,0,2,1:T(8,128)(2,1)S(1)} %copy.37), channel_id=1, source_target_pairs={{0,1},{1,0},{2,3},{3,2},{4,5},{5,4},{6,7},{7,6},{8,9},{9,8},{10,11... | collective-permute-start | bytes 2752520 | tf_op jit(solution)/shard_map/ppermute | solution.py:43
  41.2 22.8 %collective-permute-start.2 = (bf16[16,2,2,7168]{3,0,2,1:T(8,128)(2,1)S(1)}, bf16[16,2,2,7168]{3,0,2,1:T(8,128)(2,1)S(1)}, u32[]{:S(2)}, u32[]{:S(2)}) collective-permute-start(bf16[16,2,2,7168]{3,0,2,1:T(8,128)(2,1)S(1)} %copy.37), channel_id=1, source_target_pairs={{0,2},{2,0},{1,3},{3,1},{4,6},{6,4},{5,7},{7,5},{8,10},{10,8},{9,1... | collective-permute-start | bytes 2752520 | tf_op jit(solution)/shard_map/ppermute | solution.py:43
  43.7 20.3 %copy-start.3 = (bf16[1,7168,256]{2,1,0:T(8,128)(2,1)S(1)}, bf16[1,7168,256]{2,1,0:T(8,128)(2,1)}, u32[]{:S(2)}) copy-start(bf16[1,7168,256]{2,1,0:T(8,128)(2,1)} %param.9) | copy-start | bytes 11010052
  44.4 20.3 %copy-start.1 = (bf16[1,256,7168]{2,1,0:T(8,128)(2,1)S(1)}, bf16[1,256,7168]{2,1,0:T(8,128)(2,1)}, u32[]{:S(2)}) copy-start(bf16[1,256,7168]{2,1,0:T(8,128)(2,1)} %param.11) | copy-start | bytes 11010052
  64.0 2.5 %collective-permute-start.3 = (bf16[16,2,2,7168]{3,0,2,1:T(8,128)(2,1)S(1)}, bf16[16,2,2,7168]{3,0,2,1:T(8,128)(2,1)S(1)}, u32[]{:S(2)}, u32[]{:S(2)}) collective-permute-start(bf16[16,2,2,7168]{3,0,2,1:T(8,128)(2,1)S(1)} %collective-permute-done.2), channel_id=1, source_target_pairs={{0,1},{1,0},{2,3},{3,2},{4,5},{5,4},{6,7},{7,6},{8,9},{9,8},{10,11... | collective-permute-start | bytes 2752520 | tf_op jit(solution)/shard_map/ppermute | solution.py:43
  68.7 2.6 %collective-permute-start.4 = (bf16[16,2,2,7168]{3,0,2,1:T(8,128)(2,1)S(1)}, bf16[16,2,2,7168]{3,0,2,1:T(8,128)(2,1)S(1)}, u32[]{:S(2)}, u32[]{:S(2)}) collective-permute-start(bf16[16,2,2,7168]{3,0,2,1:T(8,128)(2,1)S(1)} %convolution_convert_fusion.2), channel_id=1, source_target_pairs={{0,1},{1,0},{2,3},{3,2},{4,5},{5,4},{6,7},{7,6},{8,9},{9,8},{10,11... | collective-permute-start | bytes 2752520 | tf_op jit(solution)/shard_map/ppermute | solution.py:43
  68.9 3.6 %collective-permute-start.1 = (bf16[16,2,2,7168]{3,0,2,1:T(8,128)(2,1)S(1)}, bf16[16,2,2,7168]{3,0,2,1:T(8,128)(2,1)S(1)}, u32[]{:S(2)}, u32[]{:S(2)}) collective-permute-start(bf16[16,2,2,7168]{3,0,2,1:T(8,128)(2,1)S(1)} %slice_bitcast_fusion), channel_id=1, source_target_pairs={{0,1},{1,0},{2,3},{3,2},{4,5},{5,4},{6,7},{7,6},{8,9},{9,8},{10,11... | collective-permute-start | bytes 2752520 | tf_op jit(solution)/shard_map/ppermute | solution.py:43
  72.0 28.5 %copy-start.5 = (s32[2,2,8]{2,1,0:T(2,128)S(1)}, s32[2,2,8]{2,1,0:T(2,128)}, u32[]{:S(2)}) copy-start(s32[2,2,8]{2,1,0:T(2,128)} %param.8) | copy-start | bytes 388
  72.0 28.6 %copy-start.4 = (s32[2,2,8]{2,1,0:T(2,128)S(1)}, s32[2,2,8]{2,1,0:T(2,128)}, u32[]{:S(2)}) copy-start(s32[2,2,8]{2,1,0:T(2,128)} %param.7) | copy-start | bytes 388
  72.0 22.5 %collective-permute-start.5 = (bf16[16,2,2,7168]{3,0,2,1:T(8,128)(2,1)S(1)}, bf16[16,2,2,7168]{3,0,2,1:T(8,128)(2,1)S(1)}, u32[]{:S(2)}, u32[]{:S(2)}) collective-permute-start(bf16[16,2,2,7168]{3,0,2,1:T(8,128)(2,1)S(1)} %add_convert_fusion), channel_id=1, source_target_pairs={{0,2},{2,0},{1,3},{3,1},{4,6},{6,4},{5,7},{7,5},{8,10},{10,8},{9,1... | collective-permute-start | bytes 2752520 | tf_op jit(solution)/shard_map/ppermute | solution.py:43
  96.7 30.1 %all-to-all-start.1 = ((bf16[16,2,2,7168]{3,2,1,0:T(2,128)(2,1)}), bf16[16,2,2,7168]{3,2,1,0:T(2,128)(2,1)S(1)}, u32[]{:S(2)}, u32[]{:S(2)}) async-start(bf16[16,2,2,7168]{3,2,1,0:T(2,128)(2,1)} %copy.18), calls=%async_computation.1 | async-start | bytes 1835008 | tf_op jit(solution)/shard_map/all_to_all | solution.py:69
